TPU v7x, 128 devices: a whole 4x4x4 slice. The times are simulated.
128 devices in a mesh: req: 32 (over z, x, core), head: 4 (over y).
Axes of the slice: x: 4, y: 4, z: 4, core: 2. Of those that a mesh axis runs over, the one named last changes fastest.
Arguments:
- query_new: bfloat16 [2048, 5120], P('req', 'head'), may hold values from -6 to 6
- key_new: bfloat16 [2048, 5120], P('req', 'head'), may hold values from -6 to 6
- value_new: bfloat16 [2048, 5120], P('req', 'head'), may hold values from -6 to 6
- key_pool: bfloat16 [113152, 5120], P('req', 'head'), may hold values from -368 to 368
- value_pool: bfloat16 [113152, 5120], P('req', 'head'), may hold values from -6 to 6
- lengths: int32 [2048], replicated, may hold values from 8 to 1024, as said below
- slot_request: int32 [2048], replicated, may hold values from 0 to 2047, as said below
- residual: bfloat16 [2048, 5120], P(None, 'req'), may hold values from -6 to 6
- out_proj: bfloat16 [5120, 5120], P('head', 'req'), may hold values from -0.15625 to 0.15625
- norm_gain: bfloat16 [5120], replicated, may hold values from 0.5 to 1.5
- gate_proj: bfloat16 [5120, 13824], P(None, ('req', 'head')), may hold values from -0.078125 to 0.078125
- up_proj: bfloat16 [5120, 13824], P(None, ('req', 'head')), may hold values from -0.078125 to 0.078125
- down_proj: bfloat16 [13824, 5120], P('req', 'head'), may hold values from -0.21875 to 0.21875
Outputs:
- attended: bfloat16 [2048, 5120], P('head', 'req')
- ffn_out: bfloat16 [2048, 5120], P('req', 'head')
Inputs may be any that keep to these rules, and one draw needn't show every extreme that they name: `slot_request`: a permutation of the requests; the 8 requests with more than 24 cached tokens sit two to an owner, on 4 owners. `lengths`: exactly 8 requests have 1024 // 2 to 1024 cached tokens and one of them has 1024; every other request has 8 to 24.
All inputs are finite; a program needn't handle non-finite values.
Results may differ from a plain program's by a relative error of at most 0.017.
Values may be sent and summed in bfloat16 or wider, within the bound.
No kernel may reach another device: no remote copies, remote signals or barrier semaphores. Data moves between devices by JAX's collectives and lax.ppermute only.
A program may use at most 192 MiB of HBM per device.

v0:
```python
import math

import jax
import jax.numpy as jnp
from jax import lax
from jax.sharding import PartitionSpec as P

D = 5120
HD = 128


def rope_tables(positions):
    half_dim = HD // 2
    freq_steps = jnp.arange(half_dim, dtype=jnp.float32)
    inverse = jnp.exp(freq_steps * (-2.0 * math.log(10000.0) / HD))
    angles = positions.astype(jnp.float32)[:, None] * inverse[None, :]
    return (jnp.cos(angles), jnp.sin(angles))


def rotate_half(vectors, cosine, sine_table):
    half_dim = HD // 2
    first_half = vectors[..., :half_dim]
    second = vectors[..., half_dim:]
    cos_grid = cosine[:, None, :]
    sin_grid = sine_table[:, None, :]
    return jnp.concatenate(
        [first_half * cos_grid - second * sin_grid, second * cos_grid + first_half * sin_grid],
        axis=-1,
    )


def attend_local(query_rot, key_rot, value_new, pool_keys, pool_values, seg_lengths):
    score_scale = HD ** (-0.5)
    seg_ends = jnp.cumsum(seg_lengths)
    starts = seg_ends - seg_lengths
    places = jnp.arange(pool_keys.shape[0], dtype=jnp.int32)
    member = (places[None, :] >= starts[:, None]) & (places[None, :] < seg_ends[:, None])
    scores = (
        jnp.einsum("rgd,pgd->grp", query_rot, pool_keys, preferred_element_type=jnp.float32)
        * score_scale
    )
    own_score = (
        jnp.sum(query_rot.astype(jnp.float32) * key_rot.astype(jnp.float32), axis=-1).T
        * score_scale
    )
    masked = jnp.where(member[None], scores, -jnp.inf)
    row_top = jnp.maximum(jnp.max(masked, axis=-1), own_score)
    weights = jnp.where(member[None], jnp.exp(scores - row_top[:, :, None]), 0.0)
    own_weight = jnp.exp(own_score - row_top)
    row_total = jnp.sum(weights, axis=-1) + own_weight
    summed = jnp.einsum(
        "grp,pgd->rgd",
        weights.astype(jnp.bfloat16),
        pool_values,
        preferred_element_type=jnp.float32,
    )
    own_bf = lax.optimization_barrier(own_weight.astype(jnp.bfloat16)).astype(jnp.float32)
    summed = summed + own_bf.T[:, :, None] * value_new.astype(jnp.float32)
    return (summed / row_total.T[:, :, None]).astype(jnp.bfloat16)


def body(
    query_new,
    key_new,
    value_new,
    key_pool,
    value_pool,
    lengths,
    slot_request,
    residual,
    out_proj,
    norm_gain,
    gate_proj,
    up_proj,
    down_proj,
):
    owned = query_new.shape[0]
    groups = query_new.shape[1] // HD
    pool_rows = key_pool.shape[0]
    req_count = lax.axis_size("req")
    head_count = lax.axis_size("head")
    first_slot = lax.axis_index("req") * owned
    my_requests = lax.dynamic_slice_in_dim(slot_request, first_slot, owned, 0)
    my_lengths = jnp.take(lengths, my_requests, axis=0)
    cosine, sine_table = rope_tables(my_lengths)
    shaped = (owned, groups, HD)
    query_rot = rotate_half(
        query_new.astype(jnp.float32).reshape(shaped), cosine, sine_table
    ).astype(jnp.bfloat16)
    key_rot = rotate_half(key_new.astype(jnp.float32).reshape(shaped), cosine, sine_table).astype(
        jnp.bfloat16
    )
    attention = attend_local(
        query_rot,
        key_rot,
        value_new.reshape(shaped),
        key_pool.reshape(pool_rows, groups, HD),
        value_pool.reshape(pool_rows, groups, HD),
        my_lengths,
    ).reshape(owned, groups * HD)
    partial_sums = jnp.dot(
        lax.all_gather(attention, "req", axis=0, tiled=True),
        out_proj,
        preferred_element_type=jnp.float32,
    )
    summed = lax.psum_scatter(partial_sums, "head", scatter_dimension=0, tiled=True)
    quarter = summed.shape[0]
    quarter_slots = lax.dynamic_slice_in_dim(
        slot_request, lax.axis_index("head") * quarter, quarter, 0
    )
    attended = (jnp.take(residual, quarter_slots, axis=0).astype(jnp.float32) + summed).astype(
        jnp.bfloat16
    )
    column_width = attended.shape[1]
    gain_grid = norm_gain.astype(jnp.float32).reshape(req_count, 1, column_width)
    everywhere = lax.all_gather(attended[None], ("req", "head"), axis=0, tiled=True)
    hidden_grid = everywhere.reshape(req_count, head_count, quarter, column_width).astype(
        jnp.float32
    )
    squares = jnp.sum(hidden_grid * hidden_grid, axis=(0, 3))
    inverse = lax.rsqrt(squares / D + 1e-05)
    scaled = (hidden_grid * inverse[None, :, :, None] * gain_grid[:, None]).astype(jnp.bfloat16)
    col_block = gate_proj.shape[1]
    gate_pre = jnp.einsum(
        "rhbc,rcf->hbf",
        scaled,
        gate_proj.reshape(req_count, column_width, col_block),
        preferred_element_type=jnp.float32,
    )
    upward = jnp.einsum(
        "rhbc,rcf->hbf",
        scaled,
        up_proj.reshape(req_count, column_width, col_block),
        preferred_element_type=jnp.float32,
    )
    active = (jax.nn.silu(gate_pre) * upward).astype(jnp.bfloat16)
    gathered = lax.all_gather(active, "head", axis=2, tiled=True)
    active_all = gathered.reshape(head_count * quarter, head_count * col_block)
    ffn_out = lax.psum_scatter(
        jnp.dot(active_all, down_proj, preferred_element_type=jnp.float32).astype(jnp.bfloat16),
        "req",
        scatter_dimension=0,
        tiled=True,
    )
    return (attended, ffn_out)


def solution(mesh):
    placed = (
        P("req", "head"),
        P("req", "head"),
        P("req", "head"),
        P("req", "head"),
        P("req", "head"),
        P(),
        P(),
        P(None, "req"),
        P("head", "req"),
        P(),
        P(None, ("req", "head")),
        P(None, ("req", "head")),
        P("req", "head"),
    )
    return jax.shard_map(
        body,
        mesh=mesh,
        in_specs=placed,
        out_specs=(P("head", "req"), P("req", "head")),
        check_vma=False,
    )
```

profile of v0, /device:TPU:0, one launch (start us, length us, event | category | flops | bytes accessed | tf_op | source)
XLA Modules:
  0.0 505.4 jit_solution(11591781493167109815)
XLA Ops:
  7.2 0.0 copy-start
  7.2 0.0 all-gather.5.cloned.1.call-start
  7.2 0.8 compare_select_fusion.1
  8.1 1.5 gather_fusion.1
  9.6 0.8 fusion.50
  10.3 1.0 reshape.192
  11.3 1.0 reshape.194
  12.4 0.1 copy.76
  12.5 0.1 reduce-window.7
  12.5 0.1 reduce.3
  12.7 0.3 fusion.41
  12.9 12.8 %copy.79 = bf16[3536,1280]{0,1:T(8,128)(2,1)} copy(bf16[3536,1280]{1,0:T(8,128)(2,1)} %param.16) | data formatting | bytes 18104320 | tf_op args[3]
  25.7 0.2 multiply_cosine_fusion
  25.9 0.3 fusion.51
  26.3 0.4 subtract_convert_fusion
  26.7 0.3 multiply_reduce_fusion.1
  27.0 6.1 %select_reduce_fusion = (f32[10,64]{1,0:T(8,128)S(1)}, f32[10,64,3536]{2,1,0:T(8,128)S(1)}) fusion(pred[64,3536]{1,0:T(8,128)(4,1)S(1)} %fusion.41, bf16[3536,10,128]{0,2,1:T(8,128)(2,1)} %bitcast.70, bf16[64,10,64]{2,0,1:T(8,128)(2,1)S(1)} %get-tuple-element.14, bf16[64,10,64]{2,0,1:T(8,128)(2,1)S(1)} %get-tuple-element.15), kind=kOutput, calls=%fused_computation.7 | convolution fusion | flops 586454400 | bytes 18497024 | tf_op jit(solution)/shard_map/rgd,pgd->grp/dot_general | solution.py:39
  33.2 0.0 copy-start.1
  33.2 3.5 copy-done.1
  36.7 2.4 fusion.2
  39.1 0.0 copy-start.5
  39.1 12.9 %copy.83 = bf16[3536,1280]{0,1:T(8,128)(2,1)} copy(bf16[3536,1280]{1,0:T(8,128)(2,1)} %param.17) | data formatting | bytes 18104320 | tf_op args[4]
  52.0 0.0 copy-done.5
  52.0 0.0 copy-start.3
  52.0 9.6 %fusion.38 = bf16[10,8,8,128]{3,2,1,0:T(8,128)(2,1)S(1)} fusion(bf16[3536,10,128]{0,2,1:T(8,128)(2,1)} %bitcast.71, f32[10,64,3536]{2,1,0:T(8,128)} %copy-done.1, f32[10,64]{1,0:T(8,128)S(1)} %get-tuple-element.17, pred[64,3536]{1,0:T(8,128)(4,1)S(1)} %fusion.41, f32[64,10]{0,1:T(8,128)S(1)} %fusion.44, f32[64,10]{0,1:T(8,128)S(1)} %convert_bitcast_fusion.1, ...), kind=kOutput, calls=%fused_computation.26 | convolution fusion | flops 588800000 | bytes 18665984 | tf_op jit(solution)/shard_map/grp,pgd->rgd/dot_general | solution.py:51
  61.6 0.0 copy-start.4
  61.6 0.0 copy-start.2
  61.7 0.7 copy.129
  62.3 0.0 all-gather.5.cloned.1.call-update
  62.4 0.0 reduce-scatter.3.cloned.1.call-start
  62.4 49.9 %all-gather.5.cloned.1.call-done = bf16[2048,1280]{1,0:T(8,128)(2,1)} async-done(((bf16[64,1280]{1,0:T(8,128)(2,1)}), bf16[2048,1280]{1,0:T(8,128)(2,1)}) %all-gather.5.cloned.1.call-update) | async-done | bytes 5242896 | tf_op jit(solution)/shard_map/all_gather | solution.py:102
  112.3 0.0 copy-done.3
  112.3 5.4 %fusion.53 = f32[2048,160]{0,1:T(8,128)} fusion(bf16[2048,1280]{1,0:T(8,128)(2,1)} %all-gather.5.cloned.1.call-done, bf16[1280,160]{0,1:T(8,128)(2,1)S(1)} %copy-done.3), kind=kOutput, calls=%fused_computation.65 | convolution fusion | flops 838860800 | bytes 6963200 | tf_op jit(solution)/shard_map/dot_general | solution.py:101
  117.8 0.0 reduce-scatter.3.cloned.1.call-update
  117.8 0.0 all-gather.9.cloned.1.call-start
  117.9 1.4 copy.74
  119.3 0.8 compare_and_fusion
  120.1 2.6 gather_fusion
  122.6 1.1 copy.75
  123.7 18.0 %reduce-scatter.3.cloned.1.call-done = f32[512,160]{0,1:T(8,128)} async-done(((f32[2048,160]{0,1:T(8,128)}), f32[512,160]{0,1:T(8,128)}) %reduce-scatter.3.cloned.1.call-update) | async-done | bytes 327696 | tf_op jit(solution)/shard_map/reduce_scatter | solution.py:106
  141.7 1.7 add_convert_fusion
  143.4 0.0 all-gather.9.cloned.1.call-update
  143.4 14.5 %all-gather.7.cloned.1.call-start = ((), (), s32[]{:S(2)}) async-start(), calls=%async_computation.4 | async-start | bytes 2211840 | tf_op jit(solution)/shard_map/all_gather | solution.py:137
  157.9 0.0 copy-done.4
  157.9 0.1 reshape.197
  158.0 0.0 copy-done.2
  158.0 1.5 copy.89
  159.5 1.7 copy.90
  161.3 81.7 %all-gather.9.cloned.1.call-done = bf16[65536,160]{0,1:T(8,128)(2,1)} async-done(((bf16[512,160]{0,1:T(8,128)(2,1)}), bf16[65536,160]{0,1:T(8,128)(2,1)}) %all-gather.9.cloned.1.call-update) | async-done | bytes 20971536 | tf_op jit(solution)/shard_map/all_gather | solution.py:116
  243.0 14.1 %multiply_reduce_fusion = f32[65536]{0:T(1024)S(1)} fusion(bf16[65536,160]{0,1:T(8,128)(2,1)} %all-gather.9.cloned.1.call-done), kind=kLoop, calls=%fused_computation.5 | loop fusion | flops 31391744 | bytes 21233664 | tf_op jit(solution)/shard_map/reduce_sum | solution.py:120
  257.1 0.1 reduce_sum.40
  257.2 0.1 reduce_sum.41
  257.3 39.2 %reshape.196 = f32[32,4,512,160]{2,1,0,3:T(4,128)} reshape(bf16[65536,160]{0,1:T(8,128)(2,1)} %all-gather.9.cloned.1.call-done) | data formatting | bytes 62914560 | tf_op jit(solution)/shard_map/convert_element_type | solution.py:117
  296.4 42.3 %fusion.14 = f32[4,512,108]{1,2,0:T(8,128)} fusion(bf16[32,160,108,1]{2,1,0,3:T(8,128)(2,1)} %bitcast.75, f32[32,4,512,160]{2,1,0,3:T(4,128)} %reshape.196, f32[32,160]{1,0:T(8,128)S(1)} %reshape.197, f32[4,512]{1,0:T(4,128)S(1)} %add_rsqrt_fusion), kind=kOutput, calls=%fused_computation.18 | convolution fusion | flops 2296381440 | bytes 43962368 | tf_op jit(solution)/shard_map/rhbc,rcf->hbf/dot_general | solution.py:124
  338.7 38.8 %fusion.23 = bf16[4,512,108]{1,2,0:T(8,128)(2,1)S(1)} fusion(bf16[32,160,108,1]{2,1,0,3:T(8,128)(2,1)S(1)} %bitcast.74, f32[32,4,512,160]{2,1,0,3:T(4,128)} %reshape.196, f32[32,160]{1,0:T(8,128)S(1)} %reshape.197, f32[4,512]{1,0:T(4,128)S(1)} %add_rsqrt_fusion, f32[4,512,108]{1,2,0:T(8,128)} %fusion.14), kind=kOutput, calls=%fused_computation.21 | convolution fusion | flops 2297708544 | bytes 44404736 | tf_op jit(solution)/shard_map/rhbc,rcf->hbf/dot_general | solution.py:130
  377.5 1.1 copy.91
  378.6 0.0 all-gather.7.cloned.1.call-update
  378.7 0.0 reduce-scatter.5.cloned.1.call-start
  378.7 28.2 %all-gather.7.cloned.1.call-done = bf16[4,512,432]{1,0,2:T(4,128)(2,1)} async-done(((bf16[4,512,108]{1,0,2:T(4,128)(2,1)}), bf16[4,512,432]{1,0,2:T(4,128)(2,1)}) %all-gather.7.cloned.1.call-update) | async-done | bytes 1769488 | tf_op jit(solution)/shard_map/all_gather | solution.py:137
  406.9 2.0 copy.103
  408.9 0.0 copy-done
  408.9 4.7 convolution_convert_fusion
  413.6 0.0 reduce-scatter.5.cloned.1.call-update
  413.6 84.9 %reduce-scatter.5.cloned.1.call-done = bf16[64,1280]{1,0:T(8,128)(2,1)} async-done(((bf16[2048,1280]{1,0:T(8,128)(2,1)}), bf16[64,1280]{1,0:T(8,128)(2,1)}) %reduce-scatter.5.cloned.1.call-update) | async-done | bytes 163856 | tf_op jit(solution)/shard_map/reduce_scatter | solution.py:139
  (8 shorter events, 0.1 us)
Async XLA Ops:
  7.2 401.8 %copy-start = (bf16[432,1280]{1,0:T(8,128)(2,1)S(1)}, bf16[432,1280]{1,0:T(8,128)(2,1)}, u32[]{:S(2)}) copy-start(bf16[432,1280]{1,0:T(8,128)(2,1)} %param.25) | copy-start | bytes 3317764
  7.2 105.2 %all-gather.5.cloned.1.call-start = ((), (), s32[]{:S(2)}) async-start(), calls=%async_computation.2 | async-start | bytes 5406720 | tf_op jit(solution)/shard_map/all_gather | solution.py:102
  33.2 3.6 copy-start.1
  39.1 12.9 %copy-start.5 = (bf16[64,1280]{1,0:T(8,128)(2,1)S(1)}, bf16[64,1280]{1,0:T(8,128)(2,1)}, u32[]{:S(2)}) copy-start(bf16[64,1280]{1,0:T(8,128)(2,1)} %param.15) | copy-start | bytes 491524
  52.0 60.3 %copy-start.3 = (bf16[1280,160]{0,1:T(8,128)(2,1)S(1)}, bf16[1280,160]{0,1:T(8,128)(2,1)}, u32[]{:S(2)}) copy-start(bf16[1280,160]{0,1:T(8,128)(2,1)} %param.21) | copy-start | bytes 1228804
  61.6 96.3 %copy-start.4 = (bf16[5120]{0:T(1024)(128)(2,1)S(1)}, bf16[5120]{0:T(1024)(128)(2,1)}, u32[]{:S(2)}) copy-start(bf16[5120]{0:T(1024)(128)(2,1)} %param.22) | copy-start | bytes 30724
  61.6 96.4 %copy-start.2 = (bf16[5120,108]{0,1:T(8,128)(2,1)S(1)}, bf16[5120,108]{0,1:T(8,128)(2,1)}, u32[]{:S(2)}) copy-start(bf16[5120,108]{0,1:T(8,128)(2,1)} %param.23) | copy-start | bytes 3317764
  62.4 79.3 %reduce-scatter.3.cloned.1.call-start = ((), (), s32[]{:S(2)}) async-start(), calls=%async_computation.3 | async-start | bytes 1638400 | tf_op jit(solution)/shard_map/reduce_scatter | solution.py:106
  117.8 125.2 %all-gather.9.cloned.1.call-start = ((), (), s32[]{:S(2)}) async-start(), calls=%async_computation.6 | async-start | bytes 21135360 | tf_op jit(solution)/shard_map/all_gather | solution.py:116
  143.4 263.5 %all-gather.7.cloned.1.call-start = ((), (), s32[]{:S(2)}) async-start(), calls=%async_computation.4 | async-start | bytes 2211840 | tf_op jit(solution)/shard_map/all_gather | solution.py:137
  378.7 119.9 %reduce-scatter.5.cloned.1.call-start = ((), (), s32[]{:S(2)}) async-start(), calls=%async_computation.5 | async-start | bytes 5406720 | tf_op jit(solution)/shard_map/reduce_scatter | solution.py:139
Sparse Core Ops, SparseCore 0:
  62.5 49.7 all-gather.4
  117.9 23.7 reduce-scatter.2
  145.1 97.7 all-gather.8
  378.8 28.0 all-gather.6
  413.8 84.7 reduce-scatter.4
where the time goes:
time: 516 us; the launch traced here: 505 us
  waiting for transfers between devices  263 us (51%)
  matrix products  107 us (21%)
  local copies, waits for them, and re-layouts  84.6 us (16%)
  other arithmetic  22.1 us (4%)
  starting transfers between devices  14.6 us (3%)
  between operations  14.4 us (3%)
    reduce_scatter x1, waiting for transfers between devices, body(): lax.psum_scatter(jnp.dot(active_all, down_proj, preferred_element_type=jn...  84.9 us
    all_gather x1, waiting for transfers between devices, body(): lax.all_gather(attended[None], ('req', 'head'), axis=0, tiled=True)  81.7 us
    all_gather x1, waiting for transfers between devices, body(): lax.all_gather(attention, 'req', axis=0, tiled=True)  49.9 us
    dot_general x1, matrix products, body(): jnp.einsum('rhbc,rcf->hbf', scaled, gate_proj.reshape(req_count, column_w...  42.3 us
    convert_element_type x1, local copies, waits for them, and re-layouts, body(): everywhere.reshape(req_count, head_count, quarter, column_width)  39.2 us
    dot_general x1, matrix products, body(): jnp.einsum('rhbc,rcf->hbf', scaled, up_proj.reshape(req_count, column_wid...  38.8 us
    unnamed x18, local copies, waits for them, and re-layouts  35.9 us
    all_gather x1, waiting for transfers between devices, body(): gathered = lax.all_gather(active, 'head', axis=2, tiled=True)  28.2 us
  transfers between devices with their start and end apart: 5, of which 5 were waited for; matrix products, arithmetic and copies ran while one was open for 2% of the time, Pallas kernels for 0%

commit v1 on v0

v1 whole, which is shorter than its diff:
```python
import math

import jax
import jax.numpy as jnp
from jax import lax
from jax.experimental import pallas as pl
from jax.experimental.pallas import tpu as pltpu
from jax.sharding import PartitionSpec as P

D = 5120
HD = 128
HEADS_PER_STEP = 2
R_PER_STEP = 8


def rope_tables(positions):
    half_dim = HD // 2
    freq_steps = jnp.arange(half_dim, dtype=jnp.float32)
    inverse = jnp.exp(freq_steps * (-2.0 * math.log(10000.0) / HD))
    angles = positions.astype(jnp.float32)[:, None] * inverse[None, :]
    return (jnp.cos(angles), jnp.sin(angles))


def rotate_half(vectors, cosine, sine_table):
    half_dim = HD // 2
    first_half = vectors[..., :half_dim]
    second = vectors[..., half_dim:]
    cos_grid = cosine[:, None, :]
    sin_grid = sine_table[:, None, :]
    return jnp.concatenate(
        [first_half * cos_grid - second * sin_grid, second * cos_grid + first_half * sin_grid],
        axis=-1,
    )


def attention_kernel(start_ref, end_ref, q_ref, k_ref, vn_ref, kp_ref, vp_ref, o_ref):
    score_scale = HD ** (-0.5)
    slots = q_ref.shape[0]
    rows = kp_ref.shape[0]
    places = lax.broadcasted_iota(jnp.int32, (slots, rows), 1)
    member = (places >= start_ref[...]) & (places < end_ref[...])
    for j in range(HEADS_PER_STEP):
        cols = slice(j * HD, (j + 1) * HD)
        query = q_ref[:, cols]
        scores = (
            lax.dot_general(
                query,
                kp_ref[:, cols],
                (((1,), (1,)), ((), ())),
                preferred_element_type=jnp.float32,
            )
            * score_scale
        )
        own_score = (
            jnp.sum(
                query.astype(jnp.float32) * k_ref[:, cols].astype(jnp.float32),
                axis=-1,
                keepdims=True,
            )
            * score_scale
        )
        masked = jnp.where(member, scores, -jnp.inf)
        row_top = jnp.maximum(jnp.max(masked, axis=-1, keepdims=True), own_score)
        weights = jnp.where(member, jnp.exp(scores - row_top), 0.0)
        own_weight = jnp.exp(own_score - row_top)
        row_total = jnp.sum(weights, axis=-1, keepdims=True) + own_weight
        summed = jnp.dot(
            weights.astype(jnp.bfloat16), vp_ref[:, cols], preferred_element_type=jnp.float32
        )
        own_bf = own_weight.astype(jnp.bfloat16).astype(jnp.float32)
        summed = summed + own_bf * vn_ref[:, cols].astype(jnp.float32)
        o_ref[:, cols] = (summed / row_total).astype(o_ref.dtype)


def attend_local(query_rot, key_rot, value_new, key_pool, value_pool, starts, ends):
    slots, width = query_rot.shape
    rows = key_pool.shape[0]
    block = HEADS_PER_STEP * HD
    steps = width // block
    slot_spec = pl.BlockSpec((slots, block), lambda g: (0, g))
    pool_spec = pl.BlockSpec((rows, block), lambda g: (0, g))
    bound_spec = pl.BlockSpec((slots, 1), lambda g: (0, 0))
    flops = 4 * slots * rows * width
    return pl.pallas_call(
        attention_kernel,
        grid=(steps,),
        in_specs=[bound_spec, bound_spec, slot_spec, slot_spec, slot_spec, pool_spec, pool_spec],
        out_specs=slot_spec,
        out_shape=jax.ShapeDtypeStruct((slots, width), jnp.bfloat16),
        cost_estimate=pl.CostEstimate(
            flops=flops,
            transcendentals=slots * rows * (width // HD),
            bytes_accessed=2 * rows * width * 2 + 4 * slots * width * 2,
        ),
    )(starts, ends, query_rot, key_rot, value_new, key_pool, value_pool)


def gate_up_kernel(x_ref, wg_ref, wu_ref, o_ref, acc_gate, acc_up):
    step = pl.program_id(0)
    quarters = x_ref.shape[1]
    width = x_ref.shape[3]

    @pl.when(step == 0)
    def _():
        acc_gate[...] = jnp.zeros_like(acc_gate)
        acc_up[...] = jnp.zeros_like(acc_up)

    def body(i, carry):
        w_gate = wg_ref[i]
        w_up = wu_ref[i]
        for quarter in range(quarters):
            cols = slice(quarter * width, (quarter + 1) * width)
            block = x_ref[i, quarter]
            acc_gate[:, cols] += jnp.dot(w_gate, block, preferred_element_type=jnp.float32)
            acc_up[:, cols] += jnp.dot(w_up, block, preferred_element_type=jnp.float32)
        return carry

    lax.fori_loop(0, x_ref.shape[0], body, 0)

    @pl.when(step == pl.num_programs(0) - 1)
    def _():
        gate_pre = acc_gate[...]
        silu = gate_pre / (1.0 + jnp.exp(-gate_pre))
        o_ref[...] = (silu * acc_up[...]).astype(o_ref.dtype)


def gate_up(hidden_t, gate_t, up_t):
    chunks, quarters, columns, width = hidden_t.shape
    units = gate_t.shape[1]
    slots = quarters * width
    return pl.pallas_call(
        gate_up_kernel,
        grid=(chunks // R_PER_STEP,),
        in_specs=[
            pl.BlockSpec((R_PER_STEP, quarters, columns, width), lambda s: (s, 0, 0, 0)),
            pl.BlockSpec((R_PER_STEP, units, columns), lambda s: (s, 0, 0)),
            pl.BlockSpec((R_PER_STEP, units, columns), lambda s: (s, 0, 0)),
        ],
        out_specs=pl.BlockSpec((units, slots), lambda s: (0, 0)),
        out_shape=jax.ShapeDtypeStruct((units, slots), jnp.bfloat16),
        scratch_shapes=[
            pltpu.VMEM((units, slots), jnp.float32),
            pltpu.VMEM((units, slots), jnp.float32),
        ],
        compiler_params=pltpu.CompilerParams(dimension_semantics=("arbitrary",)),
        cost_estimate=pl.CostEstimate(
            flops=4 * units * slots * chunks * columns,
            transcendentals=units * slots,
            bytes_accessed=hidden_t.size * 2 + 2 * gate_t.size * 2 + units * slots * 2,
        ),
    )(hidden_t, gate_t, up_t)


def body(
    query_new,
    key_new,
    value_new,
    key_pool,
    value_pool,
    lengths,
    slot_request,
    residual,
    out_proj,
    norm_gain,
    gate_proj,
    up_proj,
    down_proj,
):
    owned = query_new.shape[0]
    groups = query_new.shape[1] // HD
    req_count = lax.axis_size("req")
    head_count = lax.axis_size("head")
    first_slot = lax.axis_index("req") * owned
    my_requests = lax.dynamic_slice_in_dim(slot_request, first_slot, owned, 0)
    my_lengths = jnp.take(lengths, my_requests, axis=0)
    cosine, sine_table = rope_tables(my_lengths)
    shaped = (owned, groups, HD)
    query_rot = rotate_half(
        query_new.astype(jnp.float32).reshape(shaped), cosine, sine_table
    ).astype(jnp.bfloat16)
    key_rot = rotate_half(key_new.astype(jnp.float32).reshape(shaped), cosine, sine_table).astype(
        jnp.bfloat16
    )
    seg_ends = jnp.cumsum(my_lengths)
    starts = (seg_ends - my_lengths).astype(jnp.int32)
    attention = attend_local(
        query_rot.reshape(owned, groups * HD),
        key_rot.reshape(owned, groups * HD),
        value_new,
        key_pool,
        value_pool,
        starts[:, None],
        seg_ends.astype(jnp.int32)[:, None],
    )
    partial_sums = jnp.dot(
        lax.all_gather(attention, "req", axis=0, tiled=True),
        out_proj,
        preferred_element_type=jnp.float32,
    )
    summed = lax.psum_scatter(partial_sums, "head", scatter_dimension=0, tiled=True)
    quarter = summed.shape[0]
    quarter_slots = lax.dynamic_slice_in_dim(
        slot_request, lax.axis_index("head") * quarter, quarter, 0
    )
    attended = (jnp.take(residual, quarter_slots, axis=0).astype(jnp.float32) + summed).astype(
        jnp.bfloat16
    )
    column_width = attended.shape[1]
    widened = attended.astype(jnp.float32)
    squares = lax.psum(jnp.sum(widened * widened, axis=1), "req")
    inverse = lax.rsqrt(squares / D + 1e-05)
    gain = lax.dynamic_slice_in_dim(
        norm_gain, lax.axis_index("req") * column_width, column_width, 0
    ).astype(jnp.float32)
    scaled = (widened * inverse[:, None] * gain[None, :]).astype(jnp.bfloat16)
    hidden_t = lax.all_gather(scaled.T[None], ("req", "head"), axis=0, tiled=True).reshape(
        req_count, head_count, column_width, quarter
    )
    col_block = gate_proj.shape[1]
    gate_t = gate_proj.reshape(req_count, column_width, col_block).transpose(0, 2, 1)
    up_t = up_proj.reshape(req_count, column_width, col_block).transpose(0, 2, 1)
    active_t = gate_up(hidden_t, gate_t, up_t)
    active_all = lax.all_gather(active_t, "head", axis=0, tiled=True)
    down_sums = lax.dot_general(
        active_all, down_proj, (((0,), (0,)), ((), ())), preferred_element_type=jnp.float32
    )
    ffn_out = lax.psum_scatter(
        down_sums.astype(jnp.bfloat16), "req", scatter_dimension=0, tiled=True
    )
    return (attended, ffn_out)


def solution(mesh):
    placed = (
        P("req", "head"),
        P("req", "head"),
        P("req", "head"),
        P("req", "head"),
        P("req", "head"),
        P(),
        P(),
        P(None, "req"),
        P("head", "req"),
        P(),
        P(None, ("req", "head")),
        P(None, ("req", "head")),
        P("req", "head"),
    )
    return jax.shard_map(
        body,
        mesh=mesh,
        in_specs=placed,
        out_specs=(P("head", "req"), P("req", "head")),
        check_vma=False,
    )
```

time: 516 us -> 401 us (0.78); the launches traced: 505 us -> 401 us
  matrix products: 107 us -> 10.1 us
  local copies, waits for them, and re-layouts: 84.6 us -> 18.2 us
  blocking collectives: 0 us -> 64.8 us
  Pallas kernels: 0 us -> 30.3 us
  other arithmetic: 22.1 us -> 6.22 us
  starting transfers between devices: 14.6 us -> 0.21 us
  waiting for transfers between devices: 263 us -> 257 us
    dot_general x5 -> x1, matrix products: 102 us -> 4.7 us  [body(): lax.dot_general(active_all, down_proj, (((0,), (0,)), ((), ())), preferre...]
    psum x0 -> x1, blocking collectives: none -> 64.8 us  [body(): squares = lax.psum(jnp.sum(widened * widened, axis=1), 'req')]
    convert_element_type x2 -> x0, local copies, waits for them, and re-layouts: 40.3 us -> none  [the longest x1 39.2 us: body(): everywhere.reshape(req_count, head_count, quarter, column_width)]
    pallas_call x0 -> x2, Pallas kernels: none -> 30.3 us  [the longest x1 16.9 us: gate_up(): pl.pallas_call(gate_up_kernel, grid=(chunks // R_PER_STEP,), in_specs=[pl...]
    unnamed x18 -> x16, local copies, waits for them, and re-layouts: 35.9 us -> 8.08 us
    reduce_sum x4 -> x1, other arithmetic: 16.9 us -> 1.05 us  [body(): squares = lax.psum(jnp.sum(widened * widened, axis=1), 'req')]
    all_gather x2, starting transfers between devices: 14.5 us -> 0.08 us  [the longest x1 0.04 us: body(): active_all = lax.all_gather(active_t, 'head', axis=0, tiled=True)]
    all_gather x2, waiting for transfers between devices: 110 us -> 103 us  [the longest x1 75 us: body(): lax.all_gather(scaled.T[None], ('req', 'head'), axis=0, tiled=True)]
  transfers between devices with their start and end apart: 5 -> 5, of which waited for: 5 -> 5; matrix products, arithmetic and copies ran while one was open for 2% -> 3% of each run, Pallas kernels for 0% -> 0%
where the time goes in v1:
time: 401 us
  waiting for transfers between devices  257 us (64%)
  blocking collectives  64.8 us (16%)
  Pallas kernels  30.3 us (8%)
  local copies, waits for them, and re-layouts  18.2 us (5%)
  between operations  13.9 us (3%)
  matrix products  10.1 us (3%)
  other arithmetic  6.22 us (2%)
    reduce_scatter x1, waiting for transfers between devices, body(): lax.psum_scatter(down_sums.astype(jnp.bfloat16), 'req', scatter_dimension...  84.9 us
    all_gather x1, waiting for transfers between devices, body(): lax.all_gather(scaled.T[None], ('req', 'head'), axis=0, tiled=True)  75 us
    psum x1, blocking collectives, body(): squares = lax.psum(jnp.sum(widened * widened, axis=1), 'req')  64.8 us
    all_gather x1, waiting for transfers between devices, body(): lax.all_gather(attention, 'req', axis=0, tiled=True)  49.9 us
    all_gather x1, waiting for transfers between devices, body(): active_all = lax.all_gather(active_t, 'head', axis=0, tiled=True)  28.2 us
    reduce_scatter x1, waiting for transfers between devices, body(): lax.psum_scatter(partial_sums, 'head', scatter_dimension=0, tiled=True)  18.7 us
    pallas_call x1, Pallas kernels, gate_up(): pl.pallas_call(gate_up_kernel, grid=(chunks // R_PER_STEP,), in_specs=[pl...  16.9 us
    pallas_call x1, Pallas kernels, attend_local(): pl.pallas_call(attention_kernel, grid=(steps,), in_specs=[bound_spec, bou...  13.4 us
  transfers between devices with their start and end apart: 5, of which 5 were waited for; matrix products, arithmetic and copies ran while one was open for 3% of the time, Pallas kernels for 0%

profile of v1, /device:TPU:0, one launch (start us, length us, event | category | flops | bytes accessed | tf_op | source)
XLA Modules:
  0.0 400.5 jit_solution(10651427332047500900)
XLA Ops:
  7.2 0.0 copy-start
  7.2 0.0 all-gather.6.cloned.1.call-start
  7.2 0.8 compare_select_fusion.1
  8.1 1.5 gather_fusion.1
  9.6 0.8 fusion.4
  10.3 0.1 copy.29
  10.4 0.1 broadcast_in_dim.44.end_ref
  10.5 0.0 copy-start.4
  10.5 0.1 reduce
  10.7 0.7 copy.30.start_ref
  11.4 1.0 reshape.114
  12.4 1.0 reshape.116
  13.4 0.2 multiply_cosine_fusion
  13.6 0.5 subtract_convert_fusion
  14.1 0.0 copy-done.4
  14.1 0.3 pad_maximum_fusion
  14.4 0.7 copy.40
  15.1 0.7 copy.39
  15.8 0.0 copy-start.3
  15.8 13.4 %shard_map.140 = bf16[64,1280]{1,0:T(8,128)(2,1)} custom-call(s32[64,1]{1,0:T(8,128)} %copy.30.start_ref, s32[64,1]{1,0:T(8,128)} %copy-done.4, bf16[64,1280]{1,0:T(8,128)(2,1)} %bitcast.31, bf16[64,1280]{1,0:T(8,128)(2,1)} %bitcast.32, bf16[64,1280]{1,0:T(8,128)(2,1)} %vn_ref.1, bf16[3536,1280]{1,0:T(8,128)(2,1)} %kp_ref.1, bf16[3536,1280]{1,0:T(8,128)(2,1)} %vp_ref.1), custom_call_target="tpu_custom_call" | custom-call | flops 1158676480 | bytes 18759680 | tf_op jit(solution)/shard_map/pallas_call | solution.py:84
  29.3 0.0 all-gather.6.cloned.1.call-update
  29.3 0.0 reduce-scatter.3.cloned.1.call-start
  29.3 49.9 %all-gather.6.cloned.1.call-done = bf16[2048,1280]{1,0:T(8,128)(2,1)} async-done(((bf16[64,1280]{1,0:T(8,128)(2,1)}), bf16[2048,1280]{1,0:T(8,128)(2,1)}) %all-gather.6.cloned.1.call-update) | async-done | bytes 5242896 | tf_op jit(solution)/shard_map/all_gather | solution.py:196
  79.3 0.0 copy-done.3
  79.3 5.4 %fusion.5 = f32[2048,160]{0,1:T(8,128)} fusion(bf16[2048,1280]{1,0:T(8,128)(2,1)} %all-gather.6.cloned.1.call-done, bf16[1280,160]{0,1:T(8,128)(2,1)S(1)} %copy-done.3), kind=kOutput, calls=%fused_computation.31 | convolution fusion | flops 838860800 | bytes 6963200 | tf_op jit(solution)/shard_map/dot_general | solution.py:195
  84.7 0.0 copy-start.1
  84.7 0.0 reduce-scatter.3.cloned.1.call-update
  84.7 0.0 all-gather.8.cloned.1.call-start
  84.8 1.0 copy-done.1
  85.8 0.5 copy.27
  86.3 0.8 compare_and_fusion
  87.1 2.0 gather_fusion
  89.0 0.1 copy.28
  89.2 0.8 dynamic-slice_convert_fusion
  89.9 18.7 %reduce-scatter.3.cloned.1.call-done = f32[512,160]{0,1:T(8,128)} async-done(((f32[2048,160]{0,1:T(8,128)}), f32[512,160]{0,1:T(8,128)}) %reduce-scatter.3.cloned.1.call-update) | async-done | bytes 327696 | tf_op jit(solution)/shard_map/reduce_scatter | solution.py:200
  108.6 1.1 fusion
  109.7 0.0 copy-start.2
  109.7 64.8 %psum.7 = f32[512]{0:T(512)S(1)} all-reduce(f32[512]{0:T(512)S(1)} %get-tuple-element.2), channel_id=1, replica_groups=mesh['req'=32,'head'=4] {'req'}, use_global_device_ids=true, to_apply=%region_3.4 | all-reduce | flops 512 | bytes 4096 | tf_op jit(solution)/shard_map/psum | solution.py:210
  174.5 0.8 fusion.3
  175.3 0.0 all-gather.8.cloned.1.call-update
  175.3 0.0 all-gather.10.cloned.1.call-start
  175.4 1.7 copy.31
  177.1 1.9 copy.32
  179.0 0.0 copy-done.2
  179.0 1.7 copy.33
  180.8 1.9 copy.34
  182.7 75.0 %all-gather.8.cloned.1.call-done = bf16[20480,512]{1,0:T(8,128)(2,1)} async-done(((bf16[160,512]{1,0:T(8,128)(2,1)}), bf16[20480,512]{1,0:T(8,128)(2,1)}) %all-gather.8.cloned.1.call-update) | async-done | bytes 20971536 | tf_op jit(solution)/shard_map/all_gather | solution.py:216
  257.6 16.9 %shard_map.141 = bf16[108,2048]{1,0:T(8,128)(2,1)} custom-call(bf16[32,4,160,512]{3,2,1,0:T(8,128)(2,1)} %bitcast.23, bf16[32,108,160]{2,1,0:T(8,128)(2,1)} %bitcast.24, bf16[32,108,160]{2,1,0:T(8,128)(2,1)} %bitcast.25), custom_call_target="tpu_custom_call" | custom-call | flops 4529848320 | bytes 23625728 | tf_op jit(solution)/shard_map/pallas_call | solution.py:131
  274.5 0.0 all-gather.10.cloned.1.call-update
  274.5 0.0 reduce-scatter.5.cloned.1.call-start
  274.6 28.2 %all-gather.10.cloned.1.call-done = bf16[4,108,2048]{2,1,0:T(8,128)(2,1)} async-done(((bf16[1,108,2048]{2,1,0:T(8,128)(2,1)}), bf16[4,108,2048]{2,1,0:T(8,128)(2,1)}) %all-gather.10.cloned.1.call-update) | async-done | bytes 1769488 | tf_op jit(solution)/shard_map/all_gather | solution.py:223
  302.7 1.6 reshape.138
  304.4 0.0 copy-done
  304.4 4.7 %convolution_convert_fusion = bf16[2048,1280]{1,0:T(8,128)(2,1)} fusion(bf16[432,2048]{1,0:T(8,128)(2,1)S(1)} %reshape.138, bf16[432,1280]{1,0:T(8,128)(2,1)S(1)} %copy-done), kind=kOutput, calls=%fused_computation.2 | convolution fusion | flops 2267545600 | bytes 8118272 | tf_op jit(solution)/shard_map/dot_general | solution.py:224
  309.1 0.0 reduce-scatter.5.cloned.1.call-update
  309.1 84.9 %reduce-scatter.5.cloned.1.call-done = bf16[64,1280]{1,0:T(8,128)(2,1)} async-done(((bf16[2048,1280]{1,0:T(8,128)(2,1)}), bf16[64,1280]{1,0:T(8,128)(2,1)}) %reduce-scatter.5.cloned.1.call-update) | async-done | bytes 163856 | tf_op jit(solution)/shard_map/reduce_scatter | solution.py:227
  (5 shorter events, 0.0 us)
Async XLA Ops:
  7.2 297.2 %copy-start = (bf16[432,1280]{1,0:T(8,128)(2,1)S(1)}, bf16[432,1280]{1,0:T(8,128)(2,1)}, u32[]{:S(2)}) copy-start(bf16[432,1280]{1,0:T(8,128)(2,1)} %param.25) | copy-start | bytes 3317764
  7.2 72.1 %all-gather.6.cloned.1.call-start = ((), (), s32[]{:S(2)}) async-start(), calls=%async_computation.2 | async-start | bytes 5406720 | tf_op jit(solution)/shard_map/all_gather | solution.py:196
  10.5 3.6 copy-start.4
  15.8 63.4 %copy-start.3 = (bf16[1280,160]{0,1:T(8,128)(2,1)S(1)}, bf16[1280,160]{0,1:T(8,128)(2,1)}, u32[]{:S(2)}) copy-start(bf16[1280,160]{0,1:T(8,128)(2,1)} %param.21) | copy-start | bytes 1228804
  29.3 79.3 %reduce-scatter.3.cloned.1.call-start = ((), (), s32[]{:S(2)}) async-start(), calls=%async_computation.3 | async-start | bytes 1638400 | tf_op jit(solution)/shard_map/reduce_scatter | solution.py:200
  84.7 1.1 copy-start.1
  84.7 172.9 %all-gather.8.cloned.1.call-start = ((), (), s32[]{:S(2)}) async-start(), calls=%async_computation.5 | async-start | bytes 21135360 | tf_op jit(solution)/shard_map/all_gather | solution.py:216
  109.7 69.3 %copy-start.2 = (bf16[512,160]{0,1:T(8,128)(2,1)}, bf16[512,160]{0,1:T(8,128)(2,1)S(1)}, u32[]{:S(2)}) copy-start(bf16[512,160]{0,1:T(8,128)(2,1)S(1)} %get-tuple-element.3) | copy-start | bytes 491524
  175.3 127.4 %all-gather.10.cloned.1.call-start = ((), (), s32[]{:S(2)}) async-start(), calls=%async_computation.6 | async-start | bytes 2293760 | tf_op jit(solution)/shard_map/all_gather | solution.py:223
  274.5 119.5 %reduce-scatter.5.cloned.1.call-start = ((), (), s32[]{:S(2)}) async-start(), calls=%async_computation.4 | async-start | bytes 5406720 | tf_op jit(solution)/shard_map/reduce_scatter | solution.py:227
Sparse Core Ops, SparseCore 0:
  29.4 49.8 all-gather.5
  84.9 23.7 reduce-scatter.2
  175.4 82.1 all-gather.7
  274.6 28.0 all-gather.9
  309.2 84.7 reduce-scatter.4

commit v2 on v1

--- a/solution.py
+++ b/solution.py
@@ -207,7 +207,9 @@
     )
     column_width = attended.shape[1]
     widened = attended.astype(jnp.float32)
-    squares = lax.psum(jnp.sum(widened * widened, axis=1), "req")
+    squares = jnp.sum(
+        lax.all_gather(jnp.sum(widened * widened, axis=1), "req", axis=0), axis=0
+    )
     inverse = lax.rsqrt(squares / D + 1e-05)
     gain = lax.dynamic_slice_in_dim(
         norm_gain, lax.axis_index("req") * column_width, column_width, 0

time: 401 us -> 363 us (0.905)
  blocking collectives: 64.8 us -> 24.5 us
    psum x1 -> x0, blocking collectives: 64.8 us -> none  [body(): squares = lax.psum(jnp.sum(widened * widened, axis=1), 'req')]
    all_gather x0 -> x1, blocking collectives: none -> 24.5 us  [body(): lax.all_gather(jnp.sum(widened * widened, axis=1), 'req', axis=0)]
where the time goes in v2:
time: 363 us
  waiting for transfers between devices  259 us (71%)
  Pallas kernels  30.3 us (8%)
  blocking collectives  24.5 us (7%)
  local copies, waits for them, and re-layouts  18.2 us (5%)
  between operations  13.9 us (4%)
  matrix products  10.1 us (3%)
  other arithmetic  6.29 us (2%)
    reduce_scatter x1, waiting for transfers between devices, body(): lax.psum_scatter(down_sums.astype(jnp.bfloat16), 'req', scatter_dimension...  84.9 us
    all_gather x1, waiting for transfers between devices, body(): lax.all_gather(scaled.T[None], ('req', 'head'), axis=0, tiled=True)  77.2 us
    all_gather x1, waiting for transfers between devices, body(): lax.all_gather(attention, 'req', axis=0, tiled=True)  49.9 us
    all_gather x1, waiting for transfers between devices, body(): active_all = lax.all_gather(active_t, 'head', axis=0, tiled=True)  28.2 us
    all_gather x1, blocking collectives, body(): lax.all_gather(jnp.sum(widened * widened, axis=1), 'req', axis=0)  24.5 us
    reduce_scatter x1, waiting for transfers between devices, body(): lax.psum_scatter(partial_sums, 'head', scatter_dimension=0, tiled=True)  18.7 us
    pallas_call x1, Pallas kernels, gate_up(): pl.pallas_call(gate_up_kernel, grid=(chunks // R_PER_STEP,), in_specs=[pl...  16.9 us
    pallas_call x1, Pallas kernels, attend_local(): pl.pallas_call(attention_kernel, grid=(steps,), in_specs=[bound_spec, bou...  13.4 us
  transfers between devices with their start and end apart: 5, of which 5 were waited for; matrix products, arithmetic and copies ran while one was open for 3% of the time, Pallas kernels for 0%

profile of v2, /device:TPU:0, one launch (start us, length us, event | category | flops | bytes accessed | tf_op | source)
XLA Modules:
  0.0 362.5 jit_solution(5574762464072312465)
XLA Ops:
  7.2 0.0 copy-start
  7.2 0.0 all-gather.8.cloned.1.call-start
  7.2 0.8 compare_select_fusion.1
  8.1 1.5 gather_fusion.1
  9.6 0.8 fusion.4
  10.3 0.1 copy.29
  10.4 0.1 broadcast_in_dim.44.end_ref
  10.5 0.0 copy-start.4
  10.5 0.1 reduce.1
  10.7 0.7 copy.30.start_ref
  11.4 1.0 reshape.118
  12.4 1.0 reshape.120
  13.4 0.2 multiply_cosine_fusion
  13.6 0.5 subtract_convert_fusion
  14.1 0.0 copy-done.4
  14.1 0.3 pad_maximum_fusion
  14.4 0.7 copy.40
  15.1 0.7 copy.39
  15.8 0.0 copy-start.3
  15.8 13.4 %shard_map.140 = bf16[64,1280]{1,0:T(8,128)(2,1)} custom-call(s32[64,1]{1,0:T(8,128)} %copy.30.start_ref, s32[64,1]{1,0:T(8,128)} %copy-done.4, bf16[64,1280]{1,0:T(8,128)(2,1)} %bitcast.32, bf16[64,1280]{1,0:T(8,128)(2,1)} %bitcast.33, bf16[64,1280]{1,0:T(8,128)(2,1)} %vn_ref.1, bf16[3536,1280]{1,0:T(8,128)(2,1)} %kp_ref.1, bf16[3536,1280]{1,0:T(8,128)(2,1)} %vp_ref.1), custom_call_target="tpu_custom_call" | custom-call | flops 1158676480 | bytes 18759680 | tf_op jit(solution)/shard_map/pallas_call | solution.py:84
  29.3 0.0 all-gather.8.cloned.1.call-update
  29.3 0.0 reduce-scatter.3.cloned.1.call-start
  29.3 49.9 %all-gather.8.cloned.1.call-done = bf16[2048,1280]{1,0:T(8,128)(2,1)} async-done(((bf16[64,1280]{1,0:T(8,128)(2,1)}), bf16[2048,1280]{1,0:T(8,128)(2,1)}) %all-gather.8.cloned.1.call-update) | async-done | bytes 5242896 | tf_op jit(solution)/shard_map/all_gather | solution.py:196
  79.3 0.0 copy-done.3
  79.3 5.4 %fusion.5 = f32[2048,160]{0,1:T(8,128)} fusion(bf16[2048,1280]{1,0:T(8,128)(2,1)} %all-gather.8.cloned.1.call-done, bf16[1280,160]{0,1:T(8,128)(2,1)S(1)} %copy-done.3), kind=kOutput, calls=%fused_computation.31 | convolution fusion | flops 838860800 | bytes 6963200 | tf_op jit(solution)/shard_map/dot_general | solution.py:195
  84.7 0.0 copy-start.1
  84.7 0.0 reduce-scatter.3.cloned.1.call-update
  84.7 0.0 all-gather.10.cloned.1.call-start
  84.8 1.0 copy-done.1
  85.8 0.5 copy.27
  86.3 0.8 compare_and_fusion
  87.1 2.0 gather_fusion
  89.0 0.1 copy.28
  89.2 0.8 dynamic-slice_convert_fusion
  89.9 18.7 %reduce-scatter.3.cloned.1.call-done = f32[512,160]{0,1:T(8,128)} async-done(((f32[2048,160]{0,1:T(8,128)}), f32[512,160]{0,1:T(8,128)}) %reduce-scatter.3.cloned.1.call-update) | async-done | bytes 327696 | tf_op jit(solution)/shard_map/reduce_scatter | solution.py:200
  108.6 1.1 fusion
  109.7 0.0 copy-start.2
  109.7 24.5 %all-gather.2 = f32[32,1,512]{2,1,0:T(1,128)S(1)} all-gather(f32[1,1,512]{2,1,0:T(1,128)S(1)} %bitcast.34), channel_id=2, replica_groups=mesh['req'=32,'head'=4] {'req'}, dimensions={0}, use_global_device_ids=true | all-gather | bytes 67584 | tf_op jit(solution)/shard_map/all_gather | solution.py:211
  134.2 0.1 reduce_sum.19
  134.3 0.8 fusion.3
  135.0 0.0 all-gather.10.cloned.1.call-update
  135.1 0.0 all-gather.12.cloned.1.call-start
  135.1 1.7 copy.31
  136.9 1.9 copy.32
  138.8 0.0 copy-done.2
  138.8 1.7 copy.33
  140.5 1.9 copy.34
  142.4 77.2 %all-gather.10.cloned.1.call-done = bf16[20480,512]{1,0:T(8,128)(2,1)} async-done(((bf16[160,512]{1,0:T(8,128)(2,1)}), bf16[20480,512]{1,0:T(8,128)(2,1)}) %all-gather.10.cloned.1.call-update) | async-done | bytes 20971536 | tf_op jit(solution)/shard_map/all_gather | solution.py:218
  219.6 16.9 %shard_map.141 = bf16[108,2048]{1,0:T(8,128)(2,1)} custom-call(bf16[32,4,160,512]{3,2,1,0:T(8,128)(2,1)} %bitcast.24, bf16[32,108,160]{2,1,0:T(8,128)(2,1)} %bitcast.25, bf16[32,108,160]{2,1,0:T(8,128)(2,1)} %bitcast.26), custom_call_target="tpu_custom_call" | custom-call | flops 4529848320 | bytes 23625728 | tf_op jit(solution)/shard_map/pallas_call | solution.py:131
  236.5 0.0 all-gather.12.cloned.1.call-update
  236.5 0.0 reduce-scatter.5.cloned.1.call-start
  236.5 28.2 %all-gather.12.cloned.1.call-done = bf16[4,108,2048]{2,1,0:T(8,128)(2,1)} async-done(((bf16[1,108,2048]{2,1,0:T(8,128)(2,1)}), bf16[4,108,2048]{2,1,0:T(8,128)(2,1)}) %all-gather.12.cloned.1.call-update) | async-done | bytes 1769488 | tf_op jit(solution)/shard_map/all_gather | solution.py:225
  264.7 1.6 reshape.145
  266.4 0.0 copy-done
  266.4 4.7 %convolution_convert_fusion = bf16[2048,1280]{1,0:T(8,128)(2,1)} fusion(bf16[432,2048]{1,0:T(8,128)(2,1)S(1)} %reshape.145, bf16[432,1280]{1,0:T(8,128)(2,1)S(1)} %copy-done), kind=kOutput, calls=%fused_computation.2 | convolution fusion | flops 2267545600 | bytes 8118272 | tf_op jit(solution)/shard_map/dot_general | solution.py:226
  271.1 0.0 reduce-scatter.5.cloned.1.call-update
  271.1 84.9 %reduce-scatter.5.cloned.1.call-done = bf16[64,1280]{1,0:T(8,128)(2,1)} async-done(((bf16[2048,1280]{1,0:T(8,128)(2,1)}), bf16[64,1280]{1,0:T(8,128)(2,1)}) %reduce-scatter.5.cloned.1.call-update) | async-done | bytes 163856 | tf_op jit(solution)/shard_map/reduce_scatter | solution.py:229
  (5 shorter events, 0.0 us)
Async XLA Ops:
  7.2 259.2 %copy-start = (bf16[432,1280]{1,0:T(8,128)(2,1)S(1)}, bf16[432,1280]{1,0:T(8,128)(2,1)}, u32[]{:S(2)}) copy-start(bf16[432,1280]{1,0:T(8,128)(2,1)} %param.25) | copy-start | bytes 3317764
  7.2 72.1 %all-gather.8.cloned.1.call-start = ((), (), s32[]{:S(2)}) async-start(), calls=%async_computation.2 | async-start | bytes 5406720 | tf_op jit(solution)/shard_map/all_gather | solution.py:196
  10.5 3.6 copy-start.4
  15.8 63.4 %copy-start.3 = (bf16[1280,160]{0,1:T(8,128)(2,1)S(1)}, bf16[1280,160]{0,1:T(8,128)(2,1)}, u32[]{:S(2)}) copy-start(bf16[1280,160]{0,1:T(8,128)(2,1)} %param.21) | copy-start | bytes 1228804
  29.3 79.3 %reduce-scatter.3.cloned.1.call-start = ((), (), s32[]{:S(2)}) async-start(), calls=%async_computation.3 | async-start | bytes 1638400 | tf_op jit(solution)/shard_map/reduce_scatter | solution.py:200
  84.7 1.1 copy-start.1
  84.7 134.9 %all-gather.10.cloned.1.call-start = ((), (), s32[]{:S(2)}) async-start(), calls=%async_computation.5 | async-start | bytes 21135360 | tf_op jit(solution)/shard_map/all_gather | solution.py:218
  109.7 29.1 %copy-start.2 = (bf16[512,160]{0,1:T(8,128)(2,1)}, bf16[512,160]{0,1:T(8,128)(2,1)S(1)}, u32[]{:S(2)}) copy-start(bf16[512,160]{0,1:T(8,128)(2,1)S(1)} %get-tuple-element.3) | copy-start | bytes 491524
  135.1 129.7 %all-gather.12.cloned.1.call-start = ((), (), s32[]{:S(2)}) async-start(), calls=%async_computation.6 | async-start | bytes 2293760 | tf_op jit(solution)/shard_map/all_gather | solution.py:225
  236.5 119.5 %reduce-scatter.5.cloned.1.call-start = ((), (), s32[]{:S(2)}) async-start(), calls=%async_computation.4 | async-start | bytes 5406720 | tf_op jit(solution)/shard_map/reduce_scatter | solution.py:229
Sparse Core Ops, SparseCore 0:
  29.4 49.8 all-gather.7
  84.9 23.7 reduce-scatter.2
  135.2 84.3 all-gather.9
  236.6 28.0 all-gather.11
  271.2 84.7 reduce-scatter.4

commit v3 on v2

--- a/solution.py
+++ b/solution.py
@@ -11,6 +11,7 @@
 HD = 128
 HEADS_PER_STEP = 2
 R_PER_STEP = 8
+SQ_ROWS = 16
 
 
 def rope_tables(positions):
@@ -95,44 +96,49 @@
     )(starts, ends, query_rot, key_rot, value_new, key_pool, value_pool)
 
 
-def gate_up_kernel(x_ref, wg_ref, wu_ref, o_ref, acc_gate, acc_up):
+def gate_up_kernel(x_ref, wg_ref, wu_ref, o_ref, acc_gate, acc_up, acc_sq):
     step = pl.program_id(0)
     quarters = x_ref.shape[1]
     width = x_ref.shape[3]
+    columns = wg_ref.shape[2]
 
     @pl.when(step == 0)
     def _():
         acc_gate[...] = jnp.zeros_like(acc_gate)
         acc_up[...] = jnp.zeros_like(acc_up)
+        acc_sq[...] = jnp.zeros_like(acc_sq)
 
     def body(i, carry):
         w_gate = wg_ref[i]
         w_up = wu_ref[i]
         for quarter in range(quarters):
             cols = slice(quarter * width, (quarter + 1) * width)
-            block = x_ref[i, quarter]
+            block = x_ref[i, quarter, :columns, :]
             acc_gate[:, cols] += jnp.dot(w_gate, block, preferred_element_type=jnp.float32)
             acc_up[:, cols] += jnp.dot(w_up, block, preferred_element_type=jnp.float32)
+            acc_sq[:, cols] += x_ref[i, quarter, columns:, :].astype(jnp.float32)
         return carry
 
     lax.fori_loop(0, x_ref.shape[0], body, 0)
 
     @pl.when(step == pl.num_programs(0) - 1)
     def _():
-        gate_pre = acc_gate[...]
+        squares = acc_sq[0:1, :] + acc_sq[1:2, :]
+        inverse = lax.rsqrt(squares / D + 1e-05)
+        gate_pre = acc_gate[...] * inverse
         silu = gate_pre / (1.0 + jnp.exp(-gate_pre))
-        o_ref[...] = (silu * acc_up[...]).astype(o_ref.dtype)
+        o_ref[...] = (silu * (acc_up[...] * inverse)).astype(o_ref.dtype)
 
 
 def gate_up(hidden_t, gate_t, up_t):
-    chunks, quarters, columns, width = hidden_t.shape
-    units = gate_t.shape[1]
+    chunks, quarters, rows, width = hidden_t.shape
+    units, columns = gate_t.shape[1], gate_t.shape[2]
     slots = quarters * width
     return pl.pallas_call(
         gate_up_kernel,
         grid=(chunks // R_PER_STEP,),
         in_specs=[
-            pl.BlockSpec((R_PER_STEP, quarters, columns, width), lambda s: (s, 0, 0, 0)),
+            pl.BlockSpec((R_PER_STEP, quarters, rows, width), lambda s: (s, 0, 0, 0)),
             pl.BlockSpec((R_PER_STEP, units, columns), lambda s: (s, 0, 0)),
             pl.BlockSpec((R_PER_STEP, units, columns), lambda s: (s, 0, 0)),
         ],
@@ -141,6 +147,7 @@
         scratch_shapes=[
             pltpu.VMEM((units, slots), jnp.float32),
             pltpu.VMEM((units, slots), jnp.float32),
+            pltpu.VMEM((rows - columns, slots), jnp.float32),
         ],
         compiler_params=pltpu.CompilerParams(dimension_semantics=("arbitrary",)),
         cost_estimate=pl.CostEstimate(
@@ -207,20 +214,30 @@
     )
     column_width = attended.shape[1]
     widened = attended.astype(jnp.float32)
-    squares = jnp.sum(
-        lax.all_gather(jnp.sum(widened * widened, axis=1), "req", axis=0), axis=0
-    )
-    inverse = lax.rsqrt(squares / D + 1e-05)
-    gain = lax.dynamic_slice_in_dim(
-        norm_gain, lax.axis_index("req") * column_width, column_width, 0
-    ).astype(jnp.float32)
-    scaled = (widened * inverse[:, None] * gain[None, :]).astype(jnp.bfloat16)
-    hidden_t = lax.all_gather(scaled.T[None], ("req", "head"), axis=0, tiled=True).reshape(
-        req_count, head_count, column_width, quarter
+    partial_squares = jnp.sum(widened * widened, axis=1)
+    high = partial_squares.astype(jnp.bfloat16)
+    low = (partial_squares - high.astype(jnp.float32)).astype(jnp.bfloat16)
+    pad_rows = SQ_ROWS - 2
+    block_t = jnp.concatenate(
+        [attended.T, high[None], low[None], jnp.zeros((pad_rows, quarter), jnp.bfloat16)], axis=0
+    )
+    hidden_t = lax.all_gather(block_t[None], ("req", "head"), axis=0, tiled=True).reshape(
+        req_count, head_count, column_width + SQ_ROWS, quarter
     )
     col_block = gate_proj.shape[1]
-    gate_t = gate_proj.reshape(req_count, column_width, col_block).transpose(0, 2, 1)
-    up_t = up_proj.reshape(req_count, column_width, col_block).transpose(0, 2, 1)
+    gain = norm_gain.astype(jnp.float32)[:, None]
+    gate_t = (
+        (gate_proj.astype(jnp.float32) * gain)
+        .astype(jnp.bfloat16)
+        .reshape(req_count, column_width, col_block)
+        .transpose(0, 2, 1)
+    )
+    up_t = (
+        (up_proj.astype(jnp.float32) * gain)
+        .astype(jnp.bfloat16)
+        .reshape(req_count, column_width, col_block)
+        .transpose(0, 2, 1)
+    )
     active_t = gate_up(hidden_t, gate_t, up_t)
     active_all = lax.all_gather(active_t, "head", axis=0, tiled=True)
     down_sums = lax.dot_general(

time: 363 us -> 345 us (0.950)
  blocking collectives: 24.5 us -> 0 us
    all_gather x1 -> x0, blocking collectives: 24.5 us -> none  [body(): lax.all_gather(jnp.sum(widened * widened, axis=1), 'req', axis=0)]
    unnamed x16 -> x20, local copies, waits for them, and re-layouts: 8.08 us -> 8.62 us
  transfers between devices with their start and end apart: 5 -> 5, of which waited for: 5 -> 5; matrix products, arithmetic and copies ran while one was open for 3% -> 5% of each run, Pallas kernels for 0% -> 0%
where the time goes in v3:
time: 345 us
  waiting for transfers between devices  259 us (75%)
  Pallas kernels  30.5 us (9%)
  local copies, waits for them, and re-layouts  21.4 us (6%)
  between operations  14 us (4%)
  matrix products  10.2 us (3%)
  other arithmetic  9.81 us (3%)
    reduce_scatter x1, waiting for transfers between devices, body(): lax.psum_scatter(down_sums.astype(jnp.bfloat16), 'req', scatter_dimension...  84.9 us
    all_gather x1, waiting for transfers between devices, body(): lax.all_gather(block_t[None], ('req', 'head'), axis=0, tiled=True)  77.7 us
    all_gather x1, waiting for transfers between devices, body(): lax.all_gather(attention, 'req', axis=0, tiled=True)  49.9 us
    all_gather x1, waiting for transfers between devices, body(): active_all = lax.all_gather(active_t, 'head', axis=0, tiled=True)  28.2 us
    reduce_scatter x1, waiting for transfers between devices, body(): lax.psum_scatter(partial_sums, 'head', scatter_dimension=0, tiled=True)  17.8 us
    pallas_call x1, Pallas kernels, gate_up(): pl.pallas_call(gate_up_kernel, grid=(chunks // R_PER_STEP,), in_specs=[pl...  17.1 us
    pallas_call x1, Pallas kernels, attend_local(): pl.pallas_call(attention_kernel, grid=(steps,), in_specs=[bound_spec, bou...  13.4 us
    unnamed x20, local copies, waits for them, and re-layouts  8.62 us
  transfers between devices with their start and end apart: 5, of which 5 were waited for; matrix products, arithmetic and copies ran while one was open for 5% of the time, Pallas kernels for 0%

profile of v3, /device:TPU:0, one launch (start us, length us, event | category | flops | bytes accessed | tf_op | source)
XLA Modules:
  0.0 344.6 jit_solution(432287477638478030)
XLA Ops:
  7.2 0.0 copy-start
  7.2 0.0 all-gather.6.cloned.1.call-start
  7.2 0.8 compare_select_fusion.1
  8.1 1.5 gather_fusion.1
  9.6 0.8 fusion
  10.3 0.1 copy.29
  10.4 0.1 broadcast_in_dim.48.end_ref
  10.5 0.0 copy-start.5
  10.5 0.1 reduce
  10.7 0.7 copy.30.start_ref
  11.4 1.0 reshape.133
  12.4 1.0 reshape.135
  13.4 0.2 multiply_cosine_fusion
  13.6 0.5 subtract_convert_fusion
  14.1 0.0 copy-done.5
  14.1 0.3 pad_maximum_fusion
  14.4 0.7 copy.40
  15.1 0.7 copy.39
  15.9 0.0 copy-start.4
  15.9 13.4 %shard_map.140 = bf16[64,1280]{1,0:T(8,128)(2,1)} custom-call(s32[64,1]{1,0:T(8,128)} %copy.30.start_ref, s32[64,1]{1,0:T(8,128)} %copy-done.5, bf16[64,1280]{1,0:T(8,128)(2,1)} %bitcast.31, bf16[64,1280]{1,0:T(8,128)(2,1)} %bitcast.32, bf16[64,1280]{1,0:T(8,128)(2,1)} %vn_ref.1, bf16[3536,1280]{1,0:T(8,128)(2,1)} %kp_ref.1, bf16[3536,1280]{1,0:T(8,128)(2,1)} %vp_ref.1), custom_call_target="tpu_custom_call" | custom-call | flops 1158676480 | bytes 18759680 | tf_op jit(solution)/shard_map/pallas_call | solution.py:85
  29.3 0.0 all-gather.6.cloned.1.call-update
  29.3 0.0 reduce-scatter.3.cloned.1.call-start
  29.3 49.9 %all-gather.6.cloned.1.call-done = bf16[2048,1280]{1,0:T(8,128)(2,1)} async-done(((bf16[64,1280]{1,0:T(8,128)(2,1)}), bf16[2048,1280]{1,0:T(8,128)(2,1)}) %all-gather.6.cloned.1.call-update) | async-done | bytes 5242896 | tf_op jit(solution)/shard_map/all_gather | solution.py:203
  79.3 0.0 copy-done.4
  79.3 5.4 %fusion.1 = f32[2048,160]{0,1:T(8,128)} fusion(bf16[2048,1280]{1,0:T(8,128)(2,1)} %all-gather.6.cloned.1.call-done, bf16[1280,160]{0,1:T(8,128)(2,1)S(1)} %copy-done.4), kind=kOutput, calls=%fused_computation.28 | convolution fusion | flops 838860800 | bytes 6963200 | tf_op jit(solution)/shard_map/dot_general | solution.py:202
  84.7 0.0 copy-start.2
  84.7 0.0 reduce-scatter.3.cloned.1.call-update
  84.8 0.0 all-gather.8.cloned.1.call-start
  84.8 1.0 copy-done.2
  85.8 0.5 copy.27
  86.3 0.8 compare_and_fusion
  87.1 0.0 copy-start.6
  87.1 0.0 copy-start.1
  87.1 2.6 gather_fusion
  89.7 1.1 copy.28
  90.8 0.1 pad.3.clone
  90.9 17.8 %reduce-scatter.3.cloned.1.call-done = f32[512,160]{0,1:T(8,128)} async-done(((f32[2048,160]{0,1:T(8,128)}), f32[512,160]{0,1:T(8,128)}) %reduce-scatter.3.cloned.1.call-update) | async-done | bytes 327696 | tf_op jit(solution)/shard_map/reduce_scatter | solution.py:207
  108.7 1.1 multiply_reduce_fusion
  109.7 0.0 copy-start.3
  109.7 0.8 maximum_maximum_fusion
  110.5 0.0 all-gather.8.cloned.1.call-update
  110.5 0.0 all-gather.10.cloned.1.call-start
  110.6 0.0 copy-done.6
  110.6 0.0 copy-done.1
  110.6 1.5 copy.31
  112.1 2.5 copy.33
  114.6 0.0 copy-done.3
  114.7 4.3 %multiply_convert_fusion = (bf16[5120,108]{1,0:T(8,128)(2,1)S(1)}, bf16[5120,108]{1,0:T(8,128)(2,1)}) fusion(bf16[5120,108]{1,0:T(8,128)(2,1)} %copy.33, f32[5120]{0:T(1024)S(1)} %convert_element_type.88, bf16[5120,108]{1,0:T(8,128)(2,1)} %copy.31), kind=kLoop, calls=%fused_computation.3 | loop fusion | flops 3317760 | bytes 4444160 | tf_op jit(solution)/shard_map/convert_element_type | solution.py:237
  119.0 2.9 copy.32
  121.9 1.9 copy.34
  123.7 77.7 %all-gather.8.cloned.1.call-done = bf16[22528,512]{1,0:T(8,128)(2,1)} async-done(((bf16[176,512]{1,0:T(8,128)(2,1)}), bf16[22528,512]{1,0:T(8,128)(2,1)}) %all-gather.8.cloned.1.call-update) | async-done | bytes 23068688 | tf_op jit(solution)/shard_map/all_gather | solution.py:224
  201.5 17.1 %shard_map.141 = bf16[108,2048]{1,0:T(8,128)(2,1)} custom-call(bf16[32,4,176,512]{3,2,1,0:T(8,128)(2,1)} %bitcast.23, bf16[32,108,160]{2,1,0:T(8,128)(2,1)} %bitcast.24, bf16[32,108,160]{2,1,0:T(8,128)(2,1)} %bitcast.25), custom_call_target="tpu_custom_call" | custom-call | flops 4529848320 | bytes 25722880 | tf_op jit(solution)/shard_map/pallas_call | solution.py:137
  218.5 0.0 all-gather.10.cloned.1.call-update
  218.6 0.0 reduce-scatter.5.cloned.1.call-start
  218.6 28.2 %all-gather.10.cloned.1.call-done = bf16[4,108,2048]{2,1,0:T(8,128)(2,1)} async-done(((bf16[1,108,2048]{2,1,0:T(8,128)(2,1)}), bf16[4,108,2048]{2,1,0:T(8,128)(2,1)}) %all-gather.10.cloned.1.call-update) | async-done | bytes 1769488 | tf_op jit(solution)/shard_map/all_gather | solution.py:242
  246.8 1.6 reshape.157
  248.4 0.0 copy-done
  248.4 4.7 %convolution_convert_fusion = bf16[2048,1280]{1,0:T(8,128)(2,1)} fusion(bf16[432,2048]{1,0:T(8,128)(2,1)S(1)} %reshape.157, bf16[432,1280]{1,0:T(8,128)(2,1)S(1)} %copy-done), kind=kOutput, calls=%fused_computation.2 | convolution fusion | flops 2267545600 | bytes 8118272 | tf_op jit(solution)/shard_map/dot_general | solution.py:243
  253.2 0.0 reduce-scatter.5.cloned.1.call-update
  253.2 84.9 %reduce-scatter.5.cloned.1.call-done = bf16[64,1280]{1,0:T(8,128)(2,1)} async-done(((bf16[2048,1280]{1,0:T(8,128)(2,1)}), bf16[64,1280]{1,0:T(8,128)(2,1)}) %reduce-scatter.5.cloned.1.call-update) | async-done | bytes 163856 | tf_op jit(solution)/shard_map/reduce_scatter | solution.py:246
  (8 shorter events, 0.0 us)
Async XLA Ops:
  7.2 241.3 %copy-start = (bf16[432,1280]{1,0:T(8,128)(2,1)S(1)}, bf16[432,1280]{1,0:T(8,128)(2,1)}, u32[]{:S(2)}) copy-start(bf16[432,1280]{1,0:T(8,128)(2,1)} %param.25) | copy-start | bytes 3317764
  7.2 72.1 %all-gather.6.cloned.1.call-start = ((), (), s32[]{:S(2)}) async-start(), calls=%async_computation.2 | async-start | bytes 5406720 | tf_op jit(solution)/shard_map/all_gather | solution.py:203
  10.5 3.6 %copy-start.5 = (s32[64,1]{1,0:T(8,128)}, s32[64,1]{1,0:T(8,128)S(1)}, u32[]{:S(2)}) copy-start(s32[64,1]{1,0:T(8,128)S(1)} %broadcast_in_dim.48.end_ref) | copy-start | bytes 772
  15.9 63.4 %copy-start.4 = (bf16[1280,160]{0,1:T(8,128)(2,1)S(1)}, bf16[1280,160]{0,1:T(8,128)(2,1)}, u32[]{:S(2)}) copy-start(bf16[1280,160]{0,1:T(8,128)(2,1)} %param.21) | copy-start | bytes 1228804
  29.3 79.4 %reduce-scatter.3.cloned.1.call-start = ((), (), s32[]{:S(2)}) async-start(), calls=%async_computation.3 | async-start | bytes 1638400 | tf_op jit(solution)/shard_map/reduce_scatter | solution.py:207
  84.7 1.1 copy-start.2
  84.8 116.7 %all-gather.8.cloned.1.call-start = ((), (), s32[]{:S(2)}) async-start(), calls=%async_computation.5 | async-start | bytes 23248896 | tf_op jit(solution)/shard_map/all_gather | solution.py:224
  87.1 23.5 %copy-start.6 = (bf16[5120]{0:T(1024)(128)(2,1)S(1)}, bf16[5120]{0:T(1024)(128)(2,1)}, u32[]{:S(2)}) copy-start(bf16[5120]{0:T(1024)(128)(2,1)} %param.22) | copy-start | bytes 30724
  87.1 23.5 %copy-start.1 = (bf16[5120,108]{0,1:T(8,128)(2,1)S(1)}, bf16[5120,108]{0,1:T(8,128)(2,1)}, u32[]{:S(2)}) copy-start(bf16[5120,108]{0,1:T(8,128)(2,1)} %param.23) | copy-start | bytes 3317764
  109.7 4.9 %copy-start.3 = (bf16[512,160]{0,1:T(8,128)(2,1)}, bf16[512,160]{0,1:T(8,128)(2,1)S(1)}, u32[]{:S(2)}) copy-start(bf16[512,160]{0,1:T(8,128)(2,1)S(1)} %get-tuple-element.3) | copy-start | bytes 491524
  110.5 136.2 %all-gather.10.cloned.1.call-start = ((), (), s32[]{:S(2)}) async-start(), calls=%async_computation.6 | async-start | bytes 2293760 | tf_op jit(solution)/shard_map/all_gather | solution.py:242
  218.6 119.5 %reduce-scatter.5.cloned.1.call-start = ((), (), s32[]{:S(2)}) async-start(), calls=%async_computation.4 | async-start | bytes 5406720 | tf_op jit(solution)/shard_map/reduce_scatter | solution.py:246
Sparse Core Ops, SparseCore 0:
  29.4 49.8 all-gather.5
  84.9 23.7 reduce-scatter.2
  111.8 89.6 all-gather.7
  218.7 28.0 all-gather.9
  253.3 84.7 reduce-scatter.4

commit v4 on v3

--- a/solution.py
+++ b/solution.py
@@ -96,26 +96,25 @@
     )(starts, ends, query_rot, key_rot, value_new, key_pool, value_pool)
 
 
-def gate_up_kernel(x_ref, wg_ref, wu_ref, o_ref, acc_gate, acc_up, acc_sq):
+def gate_up_kernel(x_ref, w_ref, o_ref, acc, acc_sq):
     step = pl.program_id(0)
     quarters = x_ref.shape[1]
     width = x_ref.shape[3]
-    columns = wg_ref.shape[2]
+    columns = w_ref.shape[2]
+    half = w_ref.shape[1] // 2
+    units = o_ref.shape[0]
 
     @pl.when(step == 0)
     def _():
-        acc_gate[...] = jnp.zeros_like(acc_gate)
-        acc_up[...] = jnp.zeros_like(acc_up)
+        acc[...] = jnp.zeros_like(acc)
         acc_sq[...] = jnp.zeros_like(acc_sq)
 
     def body(i, carry):
-        w_gate = wg_ref[i]
-        w_up = wu_ref[i]
+        weights = w_ref[i]
         for quarter in range(quarters):
             cols = slice(quarter * width, (quarter + 1) * width)
             block = x_ref[i, quarter, :columns, :]
-            acc_gate[:, cols] += jnp.dot(w_gate, block, preferred_element_type=jnp.float32)
-            acc_up[:, cols] += jnp.dot(w_up, block, preferred_element_type=jnp.float32)
+            acc[:, cols] += jnp.dot(weights, block, preferred_element_type=jnp.float32)
             acc_sq[:, cols] += x_ref[i, quarter, columns:, :].astype(jnp.float32)
         return carry
 
@@ -125,37 +124,36 @@
     def _():
         squares = acc_sq[0:1, :] + acc_sq[1:2, :]
         inverse = lax.rsqrt(squares / D + 1e-05)
-        gate_pre = acc_gate[...] * inverse
+        gate_pre = acc[:half, :] * inverse
         silu = gate_pre / (1.0 + jnp.exp(-gate_pre))
-        o_ref[...] = (silu * (acc_up[...] * inverse)).astype(o_ref.dtype)
-
-
-def gate_up(hidden_t, gate_t, up_t):
+        active = silu * (acc[half:, :] * inverse)
+        o_ref[...] = active[:units].astype(o_ref.dtype)
+
+
+def gate_up(hidden_t, weights_t, units):
     chunks, quarters, rows, width = hidden_t.shape
-    units, columns = gate_t.shape[1], gate_t.shape[2]
+    both, columns = weights_t.shape[1], weights_t.shape[2]
     slots = quarters * width
     return pl.pallas_call(
         gate_up_kernel,
         grid=(chunks // R_PER_STEP,),
         in_specs=[
             pl.BlockSpec((R_PER_STEP, quarters, rows, width), lambda s: (s, 0, 0, 0)),
-            pl.BlockSpec((R_PER_STEP, units, columns), lambda s: (s, 0, 0)),
-            pl.BlockSpec((R_PER_STEP, units, columns), lambda s: (s, 0, 0)),
+            pl.BlockSpec((R_PER_STEP, both, columns), lambda s: (s, 0, 0)),
         ],
         out_specs=pl.BlockSpec((units, slots), lambda s: (0, 0)),
         out_shape=jax.ShapeDtypeStruct((units, slots), jnp.bfloat16),
         scratch_shapes=[
-            pltpu.VMEM((units, slots), jnp.float32),
-            pltpu.VMEM((units, slots), jnp.float32),
+            pltpu.VMEM((both, slots), jnp.float32),
             pltpu.VMEM((rows - columns, slots), jnp.float32),
         ],
         compiler_params=pltpu.CompilerParams(dimension_semantics=("arbitrary",)),
         cost_estimate=pl.CostEstimate(
-            flops=4 * units * slots * chunks * columns,
+            flops=2 * both * slots * chunks * columns,
             transcendentals=units * slots,
-            bytes_accessed=hidden_t.size * 2 + 2 * gate_t.size * 2 + units * slots * 2,
+            bytes_accessed=hidden_t.size * 2 + weights_t.size * 2 + units * slots * 2,
         ),
-    )(hidden_t, gate_t, up_t)
+    )(hidden_t, weights_t)
 
 
 def body(
@@ -226,26 +224,22 @@
     )
     col_block = gate_proj.shape[1]
     gain = norm_gain.astype(jnp.float32)[:, None]
-    gate_t = (
-        (gate_proj.astype(jnp.float32) * gain)
-        .astype(jnp.bfloat16)
-        .reshape(req_count, column_width, col_block)
-        .transpose(0, 2, 1)
-    )
-    up_t = (
-        (up_proj.astype(jnp.float32) * gain)
-        .astype(jnp.bfloat16)
-        .reshape(req_count, column_width, col_block)
-        .transpose(0, 2, 1)
-    )
-    active_t = gate_up(hidden_t, gate_t, up_t)
+    padded = -(-col_block // 8) * 8
+
+    def prepared(weights):
+        scaled_w = (weights.astype(jnp.float32) * gain).astype(jnp.bfloat16)
+        shaped_w = scaled_w.reshape(req_count, column_width, col_block).transpose(0, 2, 1)
+        return jnp.pad(shaped_w, ((0, 0), (0, padded - col_block), (0, 0)))
+
+    weights_t = jnp.concatenate([prepared(gate_proj), prepared(up_proj)], axis=1)
+    active_t = gate_up(hidden_t, weights_t, col_block)
     active_all = lax.all_gather(active_t, "head", axis=0, tiled=True)
     down_sums = lax.dot_general(
         active_all, down_proj, (((0,), (0,)), ((), ())), preferred_element_type=jnp.float32
     )
-    ffn_out = lax.psum_scatter(
-        down_sums.astype(jnp.bfloat16), "req", scatter_dimension=0, tiled=True
-    )
+    pieces = down_sums.astype(jnp.bfloat16).reshape(req_count, owned, down_sums.shape[1])
+    received = lax.all_to_all(pieces, "req", 0, 0, tiled=True)
+    ffn_out = jnp.sum(received.astype(jnp.float32), axis=0).astype(jnp.bfloat16)
     return (attended, ffn_out)
 
 

time: 345 us -> 333 us (0.965)
  waiting for transfers between devices: 259 us -> 172 us
  blocking collectives: 0 us -> 69.3 us
  other arithmetic: 9.81 us -> 17.2 us
    reduce_scatter x1 -> x0, waiting for transfers between devices: 84.9 us -> none  [body(): lax.psum_scatter(down_sums.astype(jnp.bfloat16), 'req', scatter_dimension...]
    all_to_all x0 -> x1, blocking collectives: none -> 69.3 us  [body(): received = lax.all_to_all(pieces, 'req', 0, 0, tiled=True)]
    reduce_sum x0 -> x1, other arithmetic: none -> 3.97 us  [body(): ffn_out = jnp.sum(received.astype(jnp.float32), axis=0).astype(jnp.bfloat16)]
    all_gather x1, waiting for transfers between devices: 77.7 us -> 74 us  [body(): lax.all_gather(block_t[None], ('req', 'head'), axis=0, tiled=True)]
    unnamed x20 -> x18, local copies, waits for them, and re-layouts: 8.62 us -> 7.88 us
  transfers between devices with their start and end apart: 5 -> 4, of which waited for: 5 -> 4; matrix products, arithmetic and copies ran while one was open for 5% -> 6% of each run, Pallas kernels for 0% -> 0%
where the time goes in v4:
time: 333 us; the launch traced here: 331 us
  waiting for transfers between devices  172 us (52%)
  blocking collectives  69.3 us (21%)
  Pallas kernels  30.5 us (9%)
  local copies, waits for them, and re-layouts  19.1 us (6%)
  other arithmetic  17.2 us (5%)
  between operations  14 us (4%)
  matrix products  8.62 us (3%)
    all_gather x1, waiting for transfers between devices, body(): lax.all_gather(block_t[None], ('req', 'head'), axis=0, tiled=True)  74 us
    all_to_all x1, blocking collectives, body(): received = lax.all_to_all(pieces, 'req', 0, 0, tiled=True)  69.3 us
    all_gather x1, waiting for transfers between devices, body(): lax.all_gather(attention, 'req', axis=0, tiled=True)  49.9 us
    all_gather x1, waiting for transfers between devices, body(): active_all = lax.all_gather(active_t, 'head', axis=0, tiled=True)  28.2 us
    reduce_scatter x1, waiting for transfers between devices, body(): lax.psum_scatter(partial_sums, 'head', scatter_dimension=0, tiled=True)  20.3 us
    pallas_call x1, Pallas kernels, gate_up(): pl.pallas_call(gate_up_kernel, grid=(chunks // R_PER_STEP,), in_specs=[pl...  17 us
    pallas_call x1, Pallas kernels, attend_local(): pl.pallas_call(attention_kernel, grid=(steps,), in_specs=[bound_spec, bou...  13.4 us
    unnamed x18, local copies, waits for them, and re-layouts  7.88 us
  transfers between devices with their start and end apart: 4, of which 4 were waited for; matrix products, arithmetic and copies ran while one was open for 6% of the time, Pallas kernels for 0%

profile of v4, /device:TPU:0, one launch (start us, length us, event | category | flops | bytes accessed | tf_op | source)
XLA Modules:
  0.0 331.3 jit_solution(13071279989313788870)
XLA Ops:
  7.2 0.0 copy-start
  7.2 0.0 all-gather.6.cloned.1.call-start
  7.2 0.8 compare_select_fusion.1
  8.1 1.5 gather_fusion.1
  9.6 0.8 fusion.3
  10.3 0.1 copy.29
  10.4 0.1 broadcast_in_dim.48.end_ref
  10.5 0.0 copy-start.4
  10.5 0.1 reduce.1
  10.7 0.7 copy.30.start_ref
  11.4 1.0 reshape.137
  12.4 1.0 reshape.139
  13.4 0.2 multiply_cosine_fusion
  13.6 0.5 subtract_convert_fusion
  14.1 0.3 pad_maximum_fusion
  14.4 0.0 copy-done.4
  14.4 0.7 copy.40
  15.1 0.7 copy.39
  15.9 0.0 copy-start.3
  15.9 13.4 %shard_map.140 = bf16[64,1280]{1,0:T(8,128)(2,1)} custom-call(s32[64,1]{1,0:T(8,128)} %copy.30.start_ref, s32[64,1]{1,0:T(8,128)} %copy-done.4, bf16[64,1280]{1,0:T(8,128)(2,1)} %bitcast.33, bf16[64,1280]{1,0:T(8,128)(2,1)} %bitcast.34, bf16[64,1280]{1,0:T(8,128)(2,1)} %vn_ref.1, bf16[3536,1280]{1,0:T(8,128)(2,1)} %kp_ref.1, bf16[3536,1280]{1,0:T(8,128)(2,1)} %vp_ref.1), custom_call_target="tpu_custom_call" | custom-call | flops 1158676480 | bytes 18759680 | tf_op jit(solution)/shard_map/pallas_call | solution.py:85
  29.3 0.0 all-gather.6.cloned.1.call-update
  29.3 0.0 copy-start.1
  29.3 0.0 reduce-scatter.2.cloned.1.call-start
  29.4 49.9 %all-gather.6.cloned.1.call-done = bf16[2048,1280]{1,0:T(8,128)(2,1)} async-done(((bf16[64,1280]{1,0:T(8,128)(2,1)}), bf16[2048,1280]{1,0:T(8,128)(2,1)}) %all-gather.6.cloned.1.call-update) | async-done | bytes 5242896 | tf_op jit(solution)/shard_map/all_gather | solution.py:201
  79.3 0.0 copy-done.3
  79.3 5.4 %fusion.4 = f32[2048,160]{0,1:T(8,128)} fusion(bf16[2048,1280]{1,0:T(8,128)(2,1)} %all-gather.6.cloned.1.call-done, bf16[1280,160]{0,1:T(8,128)(2,1)S(1)} %copy-done.3), kind=kOutput, calls=%fused_computation.33 | convolution fusion | flops 838860800 | bytes 6963200 | tf_op jit(solution)/shard_map/dot_general | solution.py:200
  84.7 0.0 reduce-scatter.2.cloned.1.call-update
  84.8 0.0 all-gather.8.cloned.1.call-start
  84.8 0.0 copy-done.1
  84.8 0.0 copy-start.5
  84.8 0.5 copy.27
  85.4 0.8 compare_and_fusion
  86.1 2.0 gather_fusion
  88.1 0.1 copy.28
  88.2 0.1 pad.14.clone
  88.3 20.3 %reduce-scatter.2.cloned.1.call-done = f32[512,160]{0,1:T(8,128)} async-done(((f32[2048,160]{0,1:T(8,128)}), f32[512,160]{0,1:T(8,128)}) %reduce-scatter.2.cloned.1.call-update) | async-done | bytes 327696 | tf_op jit(solution)/shard_map/reduce_scatter | solution.py:205
  108.6 1.1 multiply_reduce_fusion
  109.7 0.0 copy-start.2
  109.7 0.8 maximum_maximum_fusion
  110.5 0.0 all-gather.8.cloned.1.call-update
  110.5 0.0 all-gather.10.cloned.1.call-start
  110.5 0.0 copy-done.5
  110.6 1.7 copy.31
  112.3 2.5 copy.33
  114.9 0.0 copy-done.2
  114.9 4.4 %multiply_convert_fusion.1 = (bf16[5120,108]{1,0:T(8,128)(2,1)}, bf16[5120,108]{1,0:T(8,128)(2,1)}) fusion(bf16[5120,108]{1,0:T(8,128)(2,1)S(1)} %copy.31, f32[5120]{0:T(1024)S(1)} %convert_element_type.93, bf16[5120,108]{1,0:T(8,128)(2,1)} %copy.33), kind=kLoop, calls=%fused_computation.9 | loop fusion | flops 3317760 | bytes 4444160 | tf_op jit(solution)/shard_map/convert_element_type | solution.py:230
  119.3 1.9 copy.34
  121.2 2.9 copy.32
  124.1 3.4 %fusion.2.w_ref = bf16[32,224,160]{2,1,0:T(8,128)(2,1)} fusion(bf16[32,108,160]{2,1,0:T(8,128)(2,1)S(1)} %bitcast.25, bf16[32,108,160]{2,1,0:T(8,128)(2,1)} %bitcast.26), kind=kLoop, calls=%fused_computation.7 | loop fusion | flops 9175040 | bytes 4505600 | tf_op jit(solution)/shard_map/concatenate | solution.py:234
  127.5 74.0 %all-gather.8.cloned.1.call-done = bf16[22528,512]{1,0:T(8,128)(2,1)} async-done(((bf16[176,512]{1,0:T(8,128)(2,1)}), bf16[22528,512]{1,0:T(8,128)(2,1)}) %all-gather.8.cloned.1.call-update) | async-done | bytes 23068688 | tf_op jit(solution)/shard_map/all_gather | solution.py:222
  201.4 17.0 %shard_map.141 = bf16[108,2048]{1,0:T(8,128)(2,1)} custom-call(bf16[32,4,176,512]{3,2,1,0:T(8,128)(2,1)} %bitcast.24, bf16[32,224,160]{2,1,0:T(8,128)(2,1)} %fusion.2.w_ref), custom_call_target="tpu_custom_call" | custom-call | flops 4697620480 | bytes 25804800 | tf_op jit(solution)/shard_map/pallas_call | solution.py:137
  218.4 0.0 all-gather.10.cloned.1.call-update
  218.5 28.2 %all-gather.10.cloned.1.call-done = bf16[4,108,2048]{2,1,0:T(8,128)(2,1)} async-done(((bf16[1,108,2048]{2,1,0:T(8,128)(2,1)}), bf16[4,108,2048]{2,1,0:T(8,128)(2,1)}) %all-gather.10.cloned.1.call-update) | async-done | bytes 1769488 | tf_op jit(solution)/shard_map/all_gather | solution.py:236
  246.7 1.6 reshape.161
  248.3 0.0 copy-done
  248.4 3.2 convolution_convert_fusion
  251.6 69.3 %all_to_all.5 = bf16[32,64,1280]{2,1,0:T(8,128)(2,1)} all-to-all(bf16[32,64,1280]{2,1,0:T(8,128)(2,1)S(1)} %bitcast.27), channel_id=1, replica_groups=mesh['req'=32,'head'=4] {'req'}, dimensions={0} | all-to-all | bytes 10485760 | tf_op jit(solution)/shard_map/all_to_all | solution.py:241
  320.8 4.0 %reduce_sum.25 = bf16[64,1280]{1,0:T(8,128)(2,1)} reduce(bf16[32,64,1280]{2,1,0:T(8,128)(2,1)} %all_to_all.5, bf16[]{:T(256)} %constant.54.clone.1), dimensions={0}, to_apply=%region_3.4 | reduce | flops 2539520 | bytes 5406722 | tf_op jit(solution)/shard_map/reduce_sum | solution.py:242
  (8 shorter events, 0.0 us)
Async XLA Ops:
  7.2 241.2 %copy-start = (bf16[432,1280]{1,0:T(8,128)(2,1)S(1)}, bf16[432,1280]{1,0:T(8,128)(2,1)}, u32[]{:S(2)}) copy-start(bf16[432,1280]{1,0:T(8,128)(2,1)} %param.25) | copy-start | bytes 3317764
  7.2 72.1 %all-gather.6.cloned.1.call-start = ((), (), s32[]{:S(2)}) async-start(), calls=%async_computation.2 | async-start | bytes 5406720 | tf_op jit(solution)/shard_map/all_gather | solution.py:201
  10.5 3.9 %copy-start.4 = (s32[64,1]{1,0:T(8,128)}, s32[64,1]{1,0:T(8,128)S(1)}, u32[]{:S(2)}) copy-start(s32[64,1]{1,0:T(8,128)S(1)} %broadcast_in_dim.48.end_ref) | copy-start | bytes 772
  15.9 63.5 %copy-start.3 = (bf16[1280,160]{0,1:T(8,128)(2,1)S(1)}, bf16[1280,160]{0,1:T(8,128)(2,1)}, u32[]{:S(2)}) copy-start(bf16[1280,160]{0,1:T(8,128)(2,1)} %param.21) | copy-start | bytes 1228804
  29.3 55.5 %copy-start.1 = (bf16[2048,160]{0,1:T(8,128)(2,1)S(1)}, bf16[2048,160]{0,1:T(8,128)(2,1)}, u32[]{:S(2)}) copy-start(bf16[2048,160]{0,1:T(8,128)(2,1)} %param.20) | copy-start | bytes 1966084
  29.3 79.3 %reduce-scatter.2.cloned.1.call-start = ((), (), s32[]{:S(2)}) async-start(), calls=%async_computation.3 | async-start | bytes 1638400 | tf_op jit(solution)/shard_map/reduce_scatter | solution.py:205
  84.8 116.7 %all-gather.8.cloned.1.call-start = ((), (), s32[]{:S(2)}) async-start(), calls=%async_computation.4 | async-start | bytes 23248896 | tf_op jit(solution)/shard_map/all_gather | solution.py:222
  84.8 25.7 %copy-start.5 = (bf16[5120]{0:T(1024)(128)(2,1)S(1)}, bf16[5120]{0:T(1024)(128)(2,1)}, u32[]{:S(2)}) copy-start(bf16[5120]{0:T(1024)(128)(2,1)} %param.22) | copy-start | bytes 30724
  109.7 5.2 %copy-start.2 = (bf16[512,160]{0,1:T(8,128)(2,1)}, bf16[512,160]{0,1:T(8,128)(2,1)S(1)}, u32[]{:S(2)}) copy-start(bf16[512,160]{0,1:T(8,128)(2,1)S(1)} %get-tuple-element.3) | copy-start | bytes 491524
  110.5 136.2 %all-gather.10.cloned.1.call-start = ((), (), s32[]{:S(2)}) async-start(), calls=%async_computation.5 | async-start | bytes 2293760 | tf_op jit(solution)/shard_map/all_gather | solution.py:236
Sparse Core Ops, SparseCore 0:
  29.5 49.8 all-gather.5
  84.9 23.6 reduce-scatter.1
  111.8 89.6 all-gather.7
  218.6 28.0 all-gather.9

commit v5 on v4

--- a/solution.py
+++ b/solution.py
@@ -12,6 +12,7 @@
 HEADS_PER_STEP = 2
 R_PER_STEP = 8
 SQ_ROWS = 16
+FFN_PARTS = 2
 
 
 def rope_tables(positions):
@@ -219,9 +220,6 @@
     block_t = jnp.concatenate(
         [attended.T, high[None], low[None], jnp.zeros((pad_rows, quarter), jnp.bfloat16)], axis=0
     )
-    hidden_t = lax.all_gather(block_t[None], ("req", "head"), axis=0, tiled=True).reshape(
-        req_count, head_count, column_width + SQ_ROWS, quarter
-    )
     col_block = gate_proj.shape[1]
     gain = norm_gain.astype(jnp.float32)[:, None]
     padded = -(-col_block // 8) * 8
@@ -232,14 +230,25 @@
         return jnp.pad(shaped_w, ((0, 0), (0, padded - col_block), (0, 0)))
 
     weights_t = jnp.concatenate([prepared(gate_proj), prepared(up_proj)], axis=1)
-    active_t = gate_up(hidden_t, weights_t, col_block)
-    active_all = lax.all_gather(active_t, "head", axis=0, tiled=True)
-    down_sums = lax.dot_general(
-        active_all, down_proj, (((0,), (0,)), ((), ())), preferred_element_type=jnp.float32
-    )
-    pieces = down_sums.astype(jnp.bfloat16).reshape(req_count, owned, down_sums.shape[1])
-    received = lax.all_to_all(pieces, "req", 0, 0, tiled=True)
-    ffn_out = jnp.sum(received.astype(jnp.float32), axis=0).astype(jnp.bfloat16)
+    owners = quarter // owned
+    split = owned // FFN_PARTS
+    rows = block_t.shape[0]
+    parts = block_t.reshape(rows, owners, FFN_PARTS, split)
+    outputs = []
+    for part in range(FFN_PARTS):
+        piece = parts[:, :, part, :].reshape(rows, owners * split)
+        hidden_t = lax.all_gather(piece[None], ("req", "head"), axis=0, tiled=True).reshape(
+            req_count, head_count, rows, owners * split
+        )
+        active_t = gate_up(hidden_t, weights_t, col_block)
+        active_all = lax.all_gather(active_t, "head", axis=0, tiled=True)
+        down_sums = lax.dot_general(
+            active_all, down_proj, (((0,), (0,)), ((), ())), preferred_element_type=jnp.float32
+        )
+        pieces = down_sums.astype(jnp.bfloat16).reshape(req_count, split, down_sums.shape[1])
+        received = lax.all_to_all(pieces, "req", 0, 0, tiled=True)
+        outputs.append(jnp.sum(received.astype(jnp.float32), axis=0))
+    ffn_out = jnp.concatenate(outputs, axis=0).astype(jnp.bfloat16)
     return (attended, ffn_out)
 
 

time: 333 us -> 358 us (1.075)
  waiting for transfers between devices: 172 us -> 215 us
  blocking collectives: 69.3 us -> 29.1 us
  starting transfers between devices: 0.16 us -> 12.8 us
  Pallas kernels: 30.5 us -> 36.8 us
    all_to_all x1 -> x0, blocking collectives: 69.3 us -> none  [body(): received = lax.all_to_all(pieces, 'req', 0, 0, tiled=True)]
    all_to_all x0 -> x2, waiting for transfers between devices: none -> 34.1 us  [body(): received = lax.all_to_all(pieces, 'req', 0, 0, tiled=True)]
    all_gather x0 -> x2, blocking collectives: none -> 29.1 us  [body(): active_all = lax.all_gather(active_t, 'head', axis=0, tiled=True)]
    all_to_all x0 -> x2, starting transfers between devices: none -> 12.6 us  [body(): received = lax.all_to_all(pieces, 'req', 0, 0, tiled=True)]
    all_gather x2, waiting for transfers between devices: 102 us -> 111 us  [body(): lax.all_gather(piece[None], ('req', 'head'), axis=0, tiled=True)]
    pallas_call x1 -> x2, Pallas kernels: 17 us -> 23.4 us  [gate_up(): pl.pallas_call(gate_up_kernel, grid=(chunks // R_PER_STEP,), in_specs=[pl...]
    unnamed x18 -> x19, local copies, waits for them, and re-layouts: 7.88 us -> 6.55 us
  transfers between devices with their start and end apart: 4 -> 6, of which waited for: 4 -> 5; matrix products, arithmetic and copies ran while one was open for 6% -> 8% of each run, Pallas kernels for 0% -> 7%
where the time goes in v5:
time: 358 us; the launch traced here: 357 us
  waiting for transfers between devices  215 us (60%)
  Pallas kernels  36.8 us (10%)
  blocking collectives  29.1 us (8%)
  local copies, waits for them, and re-layouts  19.9 us (6%)
  other arithmetic  17.4 us (5%)
  between operations  14 us (4%)
  starting transfers between devices  12.8 us (4%)
  matrix products  11.6 us (3%)
    all_gather x2, waiting for transfers between devices, body(): lax.all_gather(piece[None], ('req', 'head'), axis=0, tiled=True)  111 us
    all_gather x1, waiting for transfers between devices, body(): lax.all_gather(attention, 'req', axis=0, tiled=True)  49.9 us
    all_to_all x2, waiting for transfers between devices, body(): received = lax.all_to_all(pieces, 'req', 0, 0, tiled=True)  34.1 us
    all_gather x2, blocking collectives, body(): active_all = lax.all_gather(active_t, 'head', axis=0, tiled=True)  29.1 us
    pallas_call x2, Pallas kernels, gate_up(): pl.pallas_call(gate_up_kernel, grid=(chunks // R_PER_STEP,), in_specs=[pl...  23.4 us
    reduce_scatter x1, waiting for transfers between devices, body(): lax.psum_scatter(partial_sums, 'head', scatter_dimension=0, tiled=True)  20.4 us
    pallas_call x1, Pallas kernels, attend_local(): pl.pallas_call(attention_kernel, grid=(steps,), in_specs=[bound_spec, bou...  13.4 us
    all_to_all x2, starting transfers between devices, body(): received = lax.all_to_all(pieces, 'req', 0, 0, tiled=True)  12.6 us
  transfers between devices with their start and end apart: 6, of which 5 were waited for; matrix products, arithmetic and copies ran while one was open for 8% of the time, Pallas kernels for 7%

profile of v5, /device:TPU:0, one launch (start us, length us, event | category | flops | bytes accessed | tf_op | source)
XLA Modules:
  0.0 356.8 jit_solution(13032493804394778796)
XLA Ops:
  7.2 0.0 copy-start
  7.2 0.0 all-gather.6.cloned.1.call-start
  7.2 0.8 compare_select_fusion.1
  8.1 1.5 gather_fusion.1
  9.6 0.8 fusion.3
  10.3 1.0 reshape.161
  11.3 1.0 reshape.163
  12.4 0.2 multiply_cosine_fusion
  12.6 0.5 subtract_convert_fusion
  13.1 0.3 pad_maximum_fusion
  13.4 0.7 copy.80
  14.1 0.7 copy.81
  14.8 0.1 copy.58
  14.9 0.1 broadcast_in_dim.45.end_ref
  15.0 0.1 reduce.2
  15.1 0.7 copy.59.start_ref
  15.8 13.4 %shard_map.140 = bf16[64,1280]{1,0:T(8,128)(2,1)} custom-call(s32[64,1]{1,0:T(8,128)} %copy.59.start_ref, s32[64,1]{1,0:T(8,128)} %copy-done.4, bf16[64,1280]{1,0:T(8,128)(2,1)} %bitcast.45, bf16[64,1280]{1,0:T(8,128)(2,1)} %bitcast.44, bf16[64,1280]{1,0:T(8,128)(2,1)} %vn_ref.1, bf16[3536,1280]{1,0:T(8,128)(2,1)} %kp_ref.1, bf16[3536,1280]{1,0:T(8,128)(2,1)} %vp_ref.1), custom_call_target="tpu_custom_call" | custom-call | flops 1158676480 | bytes 18759680 | tf_op jit(solution)/shard_map/pallas_call | solution.py:86
  29.3 0.0 all-gather.6.cloned.1.call-update
  29.3 0.0 copy-start.1
  29.3 0.0 reduce-scatter.2.cloned.1.call-start
  29.4 49.9 %all-gather.6.cloned.1.call-done = bf16[2048,1280]{1,0:T(8,128)(2,1)} async-done(((bf16[64,1280]{1,0:T(8,128)(2,1)}), bf16[2048,1280]{1,0:T(8,128)(2,1)}) %all-gather.6.cloned.1.call-update) | async-done | bytes 5242896 | tf_op jit(solution)/shard_map/all_gather | solution.py:202
  79.3 5.4 %fusion.5 = f32[2048,160]{0,1:T(8,128)} fusion(bf16[2048,1280]{1,0:T(8,128)(2,1)} %all-gather.6.cloned.1.call-done, bf16[1280,160]{0,1:T(8,128)(2,1)S(1)} %copy-done.3), kind=kOutput, calls=%fused_computation.37 | convolution fusion | flops 838860800 | bytes 6963200 | tf_op jit(solution)/shard_map/dot_general | solution.py:201
  84.7 0.0 reduce-scatter.2.cloned.1.call-update
  84.7 0.0 all-gather.8.cloned.1.call-start
  84.8 0.5 copy.56
  85.3 0.8 compare_and_fusion
  86.1 2.0 gather_fusion
  88.1 0.1 copy.57
  88.2 0.1 pad.16.clone
  88.3 20.4 %reduce-scatter.2.cloned.1.call-done = f32[512,160]{0,1:T(8,128)} async-done(((f32[2048,160]{0,1:T(8,128)}), f32[512,160]{0,1:T(8,128)}) %reduce-scatter.2.cloned.1.call-update) | async-done | bytes 327696 | tf_op jit(solution)/shard_map/reduce_scatter | solution.py:206
  108.6 1.1 multiply_reduce_fusion
  109.7 0.1 reduce_sum.30
  109.8 0.1 copy.60
  109.9 0.2 copy.63
  110.2 0.2 copy.64
  110.4 0.1 maximum_maximum_fusion
  110.5 0.7 copy.65
  111.3 0.0 all-gather.8.cloned.1.call-update
  111.3 0.0 copy-start.5
  111.3 0.0 all-gather.10.cloned.1.call-start
  111.4 0.7 copy.70
  112.1 0.0 all-gather.10.cloned.1.call-update
  112.1 1.7 copy.66
  113.9 2.5 copy.68
  116.4 4.3 %multiply_convert_fusion.1 = (bf16[5120,108]{1,0:T(8,128)(2,1)}, bf16[5120,108]{1,0:T(8,128)(2,1)}) fusion(bf16[5120,108]{1,0:T(8,128)(2,1)S(1)} %copy.66, f32[5120]{0:T(1024)S(1)} %convert_element_type.105, bf16[5120,108]{1,0:T(8,128)(2,1)} %copy.68), kind=kLoop, calls=%fused_computation.10 | loop fusion | flops 3317760 | bytes 4444160 | tf_op jit(solution)/shard_map/convert_element_type | solution.py:228
  120.7 1.9 copy.67
  122.7 2.9 copy.69
  125.5 3.3 fusion.2.w_ref
  128.9 54.6 %all-gather.8.cloned.1.call-done = bf16[128,176,256]{2,1,0:T(8,128)(2,1)} async-done(((bf16[1,176,256]{2,1,0:T(8,128)(2,1)}), bf16[128,176,256]{2,1,0:T(8,128)(2,1)}) %all-gather.8.cloned.1.call-update) | async-done | bytes 11534352 | tf_op jit(solution)/shard_map/all_gather | solution.py:240
  183.5 11.7 %shard_map.141 = bf16[108,1024]{1,0:T(8,128)(2,1)} custom-call(bf16[32,4,176,256]{3,2,1,0:T(8,128)(2,1)} %bitcast.32, bf16[32,224,160]{2,1,0:T(8,128)(2,1)} %fusion.2.w_ref), custom_call_target="tpu_custom_call" | custom-call | flops 2348810240 | bytes 14049280 | tf_op jit(solution)/shard_map/pallas_call | solution.py:138
  195.2 14.8 %all-gather = bf16[4,108,1024]{2,1,0:T(8,128)(2,1)S(1)} all-gather(bf16[1,108,1024]{2,1,0:T(8,128)(2,1)} %bitcast.43), channel_id=1, replica_groups=mesh['req'=32,'head'=4] {'head'}, dimensions={0}, use_global_device_ids=true | all-gather | bytes 1105920 | tf_op jit(solution)/shard_map/all_gather | solution.py:244
  210.0 0.2 reshape.183
  210.2 3.0 convolution_convert_fusion.1
  213.2 6.3 %all-to-all-start = ((bf16[32,32,1280]{2,1,0:T(8,128)(2,1)}), bf16[32,32,1280]{2,1,0:T(8,128)(2,1)}, u32[]{:S(2)}, u32[]{:S(2)}) async-start(bf16[32,32,1280]{2,1,0:T(8,128)(2,1)} %bitcast.37), calls=%async_computation.1 | async-start | bytes 5242880 | tf_op jit(solution)/shard_map/all_to_all | solution.py:249
  219.5 56.2 %all-gather.10.cloned.1.call-done = bf16[128,176,256]{2,1,0:T(8,128)(2,1)} async-done(((bf16[1,176,256]{2,1,0:T(8,128)(2,1)}), bf16[128,176,256]{2,1,0:T(8,128)(2,1)}) %all-gather.10.cloned.1.call-update) | async-done | bytes 11534352 | tf_op jit(solution)/shard_map/all_gather | solution.py:240
  275.7 11.7 %shard_map.142 = bf16[108,1024]{1,0:T(8,128)(2,1)} custom-call(bf16[32,4,176,256]{3,2,1,0:T(8,128)(2,1)} %bitcast.31, bf16[32,224,160]{2,1,0:T(8,128)(2,1)} %fusion.2.w_ref), custom_call_target="tpu_custom_call" | custom-call | flops 2348810240 | bytes 14049280 | tf_op jit(solution)/shard_map/pallas_call | solution.py:138
  287.4 14.3 %all-gather.1 = bf16[4,108,1024]{2,1,0:T(8,128)(2,1)S(1)} all-gather(bf16[1,108,1024]{2,1,0:T(8,128)(2,1)} %bitcast.42), channel_id=1, replica_groups=mesh['req'=32,'head'=4] {'head'}, dimensions={0}, use_global_device_ids=true | all-gather | bytes 1105920 | tf_op jit(solution)/shard_map/all_gather | solution.py:244
  301.7 0.2 reshape.185
  301.9 3.1 convolution_convert_fusion
  305.0 6.4 %all-to-all-start.1 = ((bf16[32,32,1280]{2,1,0:T(8,128)(2,1)}), bf16[32,32,1280]{2,1,0:T(8,128)(2,1)}, u32[]{:S(2)}, u32[]{:S(2)}) async-start(bf16[32,32,1280]{2,1,0:T(8,128)(2,1)} %bitcast.38), calls=%async_computation.2 | async-start | bytes 5242880 | tf_op jit(solution)/shard_map/all_to_all | solution.py:249
  311.4 2.1 reduce
  313.5 34.1 %all-to-all-done.1 = bf16[32,32,1280]{2,1,0:T(8,128)(2,1)} async-done(((bf16[32,32,1280]{2,1,0:T(8,128)(2,1)}), bf16[32,32,1280]{2,1,0:T(8,128)(2,1)}, u32[]{:S(2)}, u32[]{:S(2)}) %all-to-all-start.1) | async-done | bytes 2621472 | tf_op jit(solution)/shard_map/all_to_all | solution.py:249
  347.5 2.1 reduce.1
  349.6 0.7 pad_maximum_fusion.2
  (19 shorter events, 0.1 us)
Async XLA Ops:
  7.2 203.0 %copy-start = (bf16[432,1280]{1,0:T(8,128)(2,1)S(1)}, bf16[432,1280]{1,0:T(8,128)(2,1)}, u32[]{:S(2)}) copy-start(bf16[432,1280]{1,0:T(8,128)(2,1)} %param.25) | copy-start | bytes 3317764
  7.2 72.1 %all-gather.6.cloned.1.call-start = ((), (), s32[]{:S(2)}) async-start(), calls=%async_computation.3 | async-start | bytes 5406720 | tf_op jit(solution)/shard_map/all_gather | solution.py:202
  15.0 0.8 copy-start.4
  15.8 63.5 %copy-start.3 = (bf16[1280,160]{0,1:T(8,128)(2,1)S(1)}, bf16[1280,160]{0,1:T(8,128)(2,1)}, u32[]{:S(2)}) copy-start(bf16[1280,160]{0,1:T(8,128)(2,1)} %param.21) | copy-start | bytes 1228804
  29.3 55.5 %copy-start.1 = (bf16[2048,160]{0,1:T(8,128)(2,1)S(1)}, bf16[2048,160]{0,1:T(8,128)(2,1)}, u32[]{:S(2)}) copy-start(bf16[2048,160]{0,1:T(8,128)(2,1)} %param.20) | copy-start | bytes 1966084
  29.3 79.3 %reduce-scatter.2.cloned.1.call-start = ((), (), s32[]{:S(2)}) async-start(), calls=%async_computation.4 | async-start | bytes 1638400 | tf_op jit(solution)/shard_map/reduce_scatter | solution.py:206
  84.7 98.8 %all-gather.8.cloned.1.call-start = ((), (), s32[]{:S(2)}) async-start(), calls=%async_computation.5 | async-start | bytes 11624448 | tf_op jit(solution)/shard_map/all_gather | solution.py:240
  109.7 6.7 %copy-start.2 = (bf16[512,160]{0,1:T(8,128)(2,1)}, bf16[512,160]{0,1:T(8,128)(2,1)S(1)}, u32[]{:S(2)}) copy-start(bf16[512,160]{0,1:T(8,128)(2,1)S(1)} %get-tuple-element.3) | copy-start | bytes 491524
  111.3 5.1 %copy-start.5 = (bf16[5120]{0:T(1024)(128)(2,1)S(1)}, bf16[5120]{0:T(1024)(128)(2,1)}, u32[]{:S(2)}) copy-start(bf16[5120]{0:T(1024)(128)(2,1)} %param.22) | copy-start | bytes 30724
  111.3 164.4 %all-gather.10.cloned.1.call-start = ((), (), s32[]{:S(2)}) async-start(), calls=%async_computation.6 | async-start | bytes 11624448 | tf_op jit(solution)/shard_map/all_gather | solution.py:240
  213.2 91.8 %all-to-all-start = ((bf16[32,32,1280]{2,1,0:T(8,128)(2,1)}), bf16[32,32,1280]{2,1,0:T(8,128)(2,1)}, u32[]{:S(2)}, u32[]{:S(2)}) async-start(bf16[32,32,1280]{2,1,0:T(8,128)(2,1)} %bitcast.37), calls=%async_computation.1 | async-start | bytes 5242880 | tf_op jit(solution)/shard_map/all_to_all | solution.py:249
  305.0 42.6 %all-to-all-start.1 = ((bf16[32,32,1280]{2,1,0:T(8,128)(2,1)}), bf16[32,32,1280]{2,1,0:T(8,128)(2,1)}, u32[]{:S(2)}, u32[]{:S(2)}) async-start(bf16[32,32,1280]{2,1,0:T(8,128)(2,1)} %bitcast.38), calls=%async_computation.2 | async-start | bytes 5242880 | tf_op jit(solution)/shard_map/all_to_all | solution.py:249
Sparse Core Ops, SparseCore 0:
  29.4 49.8 all-gather.5
  84.9 23.7 reduce-scatter.1
  111.6 71.8 all-gather.7
  186.9 88.7 all-gather.9

commit v6 on v4

--- a/solution.py
+++ b/solution.py
@@ -9,6 +9,11 @@
 
 D = 5120
 HD = 128
+CHIPS = "chip"
+CORE = "core"
+REQ = (CHIPS, CORE)
+CORES_PER_CHIP = 2
+HEAD = "y"
 HEADS_PER_STEP = 2
 R_PER_STEP = 8
 SQ_ROWS = 16
@@ -173,9 +178,9 @@
 ):
     owned = query_new.shape[0]
     groups = query_new.shape[1] // HD
-    req_count = lax.axis_size("req")
-    head_count = lax.axis_size("head")
-    first_slot = lax.axis_index("req") * owned
+    req_count = lax.axis_size(REQ)
+    head_count = lax.axis_size(HEAD)
+    first_slot = lax.axis_index(REQ) * owned
     my_requests = lax.dynamic_slice_in_dim(slot_request, first_slot, owned, 0)
     my_lengths = jnp.take(lengths, my_requests, axis=0)
     cosine, sine_table = rope_tables(my_lengths)
@@ -198,14 +203,14 @@
         seg_ends.astype(jnp.int32)[:, None],
     )
     partial_sums = jnp.dot(
-        lax.all_gather(attention, "req", axis=0, tiled=True),
+        lax.all_gather(attention, REQ, axis=0, tiled=True),
         out_proj,
         preferred_element_type=jnp.float32,
     )
-    summed = lax.psum_scatter(partial_sums, "head", scatter_dimension=0, tiled=True)
+    summed = lax.psum_scatter(partial_sums, HEAD, scatter_dimension=0, tiled=True)
     quarter = summed.shape[0]
     quarter_slots = lax.dynamic_slice_in_dim(
-        slot_request, lax.axis_index("head") * quarter, quarter, 0
+        slot_request, lax.axis_index(HEAD) * quarter, quarter, 0
     )
     attended = (jnp.take(residual, quarter_slots, axis=0).astype(jnp.float32) + summed).astype(
         jnp.bfloat16
@@ -219,7 +224,7 @@
     block_t = jnp.concatenate(
         [attended.T, high[None], low[None], jnp.zeros((pad_rows, quarter), jnp.bfloat16)], axis=0
     )
-    hidden_t = lax.all_gather(block_t[None], ("req", "head"), axis=0, tiled=True).reshape(
+    hidden_t = lax.all_gather(block_t[None], REQ + (HEAD,), axis=0, tiled=True).reshape(
         req_count, head_count, column_width + SQ_ROWS, quarter
     )
     col_block = gate_proj.shape[1]
@@ -233,36 +238,45 @@
 
     weights_t = jnp.concatenate([prepared(gate_proj), prepared(up_proj)], axis=1)
     active_t = gate_up(hidden_t, weights_t, col_block)
-    active_all = lax.all_gather(active_t, "head", axis=0, tiled=True)
+    active_all = lax.all_gather(active_t, HEAD, axis=0, tiled=True)
     down_sums = lax.dot_general(
         active_all, down_proj, (((0,), (0,)), ((), ())), preferred_element_type=jnp.float32
     )
-    pieces = down_sums.astype(jnp.bfloat16).reshape(req_count, owned, down_sums.shape[1])
-    received = lax.all_to_all(pieces, "req", 0, 0, tiled=True)
+    cores = lax.axis_size(CORE)
+    chips = req_count // cores
+    pieces = down_sums.astype(jnp.bfloat16).reshape(chips, cores, owned, down_sums.shape[1])
+    on_chip = lax.all_to_all(pieces, CORE, 1, 1, tiled=True)
+    chip_sums = jnp.sum(on_chip.astype(jnp.float32), axis=1).astype(jnp.bfloat16)
+    received = lax.all_to_all(chip_sums, CHIPS, 0, 0, tiled=True)
     ffn_out = jnp.sum(received.astype(jnp.float32), axis=0).astype(jnp.bfloat16)
     return (attended, ffn_out)
 
 
 def solution(mesh):
     placed = (
-        P("req", "head"),
-        P("req", "head"),
-        P("req", "head"),
-        P("req", "head"),
-        P("req", "head"),
+        P(REQ, HEAD),
+        P(REQ, HEAD),
+        P(REQ, HEAD),
+        P(REQ, HEAD),
+        P(REQ, HEAD),
         P(),
         P(),
-        P(None, "req"),
-        P("head", "req"),
+        P(None, REQ),
+        P(HEAD, REQ),
         P(),
-        P(None, ("req", "head")),
-        P(None, ("req", "head")),
-        P("req", "head"),
+        P(None, REQ + (HEAD,)),
+        P(None, REQ + (HEAD,)),
+        P(REQ, HEAD),
+    )
+    req_size, head_size = mesh.devices.shape
+    named = jax.sharding.Mesh(
+        mesh.devices.reshape(req_size // CORES_PER_CHIP, CORES_PER_CHIP, head_size),
+        (CHIPS, CORE, HEAD),
     )
     return jax.shard_map(
         body,
-        mesh=mesh,
+        mesh=named,
         in_specs=placed,
-        out_specs=(P("head", "req"), P("req", "head")),
+        out_specs=(P(HEAD, REQ), P(REQ, HEAD)),
         check_vma=False,
     )

time: 333 us -> 318 us (0.955)
  blocking collectives: 69.3 us -> 50.5 us
  other arithmetic: 17.2 us -> 21.8 us
    all_to_all x1 -> x2, blocking collectives: 69.3 us -> 50.5 us  [the longest x1 41.4 us: body(): received = lax.all_to_all(chip_sums, CHIPS, 0, 0, tiled=True)]
    reduce_sum x0 -> x1, other arithmetic: none -> 5.75 us  [body(): jnp.sum(on_chip.astype(jnp.float32), axis=1).astype(jnp.bfloat16)]
where the time goes in v6:
time: 318 us
  waiting for transfers between devices  173 us (54%)
  blocking collectives  50.5 us (16%)
  Pallas kernels  30.5 us (10%)
  other arithmetic  21.8 us (7%)
  local copies, waits for them, and re-layouts  19.7 us (6%)
  between operations  14 us (4%)
  matrix products  8.63 us (3%)
    all_gather x1, waiting for transfers between devices, body(): lax.all_gather(block_t[None], REQ + (HEAD,), axis=0, tiled=True)  74 us
    all_gather x1, waiting for transfers between devices, body(): lax.all_gather(attention, REQ, axis=0, tiled=True)  49.9 us
    all_to_all x1, blocking collectives, body(): received = lax.all_to_all(chip_sums, CHIPS, 0, 0, tiled=True)  41.4 us
    all_gather x1, waiting for transfers between devices, body(): active_all = lax.all_gather(active_t, HEAD, axis=0, tiled=True)  28.2 us
    reduce_scatter x1, waiting for transfers between devices, body(): lax.psum_scatter(partial_sums, HEAD, scatter_dimension=0, tiled=True)  20.4 us
    pallas_call x1, Pallas kernels, gate_up(): pl.pallas_call(gate_up_kernel, grid=(chunks // R_PER_STEP,), in_specs=[pl...  17 us
    pallas_call x1, Pallas kernels, attend_local(): pl.pallas_call(attention_kernel, grid=(steps,), in_specs=[bound_spec, bou...  13.4 us
    all_to_all x1, blocking collectives, body(): on_chip = lax.all_to_all(pieces, CORE, 1, 1, tiled=True)  9.09 us
  transfers between devices with their start and end apart: 4, of which 4 were waited for; matrix products, arithmetic and copies ran while one was open for 6% of the time, Pallas kernels for 0%

profile of v6, /device:TPU:0, one launch (start us, length us, event | category | flops | bytes accessed | tf_op | source)
XLA Modules:
  0.0 317.8 jit_solution(132108858447277056)
XLA Ops:
  7.2 0.0 copy-start
  7.2 0.0 all-gather.6.cloned.1.call-start
  7.2 0.8 compare_select_fusion.1
  8.1 1.5 gather_fusion.1
  9.6 0.8 fusion.3
  10.3 0.1 copy.38
  10.4 0.1 broadcast_in_dim.48.end_ref
  10.5 0.0 copy-start.4
  10.5 0.1 reduce.2
  10.7 0.7 copy.39.start_ref
  11.4 1.0 reshape.137
  12.4 1.0 reshape.139
  13.4 0.2 multiply_cosine_fusion
  13.6 0.5 subtract_convert_fusion
  14.1 0.3 pad_maximum_fusion
  14.4 0.0 copy-done.4
  14.4 0.7 copy.50
  15.1 0.7 copy.49
  15.8 0.0 copy-start.3
  15.8 13.4 %shard_map.140 = bf16[64,1280]{1,0:T(8,128)(2,1)} custom-call(s32[64,1]{1,0:T(8,128)} %copy.39.start_ref, s32[64,1]{1,0:T(8,128)} %copy-done.4, bf16[64,1280]{1,0:T(8,128)(2,1)} %bitcast.33, bf16[64,1280]{1,0:T(8,128)(2,1)} %bitcast.34, bf16[64,1280]{1,0:T(8,128)(2,1)} %vn_ref.1, bf16[3536,1280]{1,0:T(8,128)(2,1)} %kp_ref.1, bf16[3536,1280]{1,0:T(8,128)(2,1)} %vp_ref.1), custom_call_target="tpu_custom_call" | custom-call | flops 1158676480 | bytes 18759680 | tf_op jit(solution)/shard_map/pallas_call | solution.py:90
  29.3 0.0 all-gather.6.cloned.1.call-update
  29.3 0.0 copy-start.1
  29.3 0.0 reduce-scatter.2.cloned.1.call-start
  29.4 49.9 %all-gather.6.cloned.1.call-done = bf16[2048,1280]{1,0:T(8,128)(2,1)} async-done(((bf16[64,1280]{1,0:T(8,128)(2,1)}), bf16[2048,1280]{1,0:T(8,128)(2,1)}) %all-gather.6.cloned.1.call-update) | async-done | bytes 5242896 | tf_op jit(solution)/shard_map/all_gather | solution.py:206
  79.3 0.0 copy-done.3
  79.3 5.4 %fusion.4 = f32[2048,160]{0,1:T(8,128)} fusion(bf16[2048,1280]{1,0:T(8,128)(2,1)} %all-gather.6.cloned.1.call-done, bf16[1280,160]{0,1:T(8,128)(2,1)S(1)} %copy-done.3), kind=kOutput, calls=%fused_computation.33 | convolution fusion | flops 838860800 | bytes 6963200 | tf_op jit(solution)/shard_map/dot_general | solution.py:205
  84.7 0.0 reduce-scatter.2.cloned.1.call-update
  84.7 0.0 all-gather.8.cloned.1.call-start
  84.8 0.0 copy-done.1
  84.8 0.0 copy-start.5
  84.8 0.5 copy.36
  85.3 0.8 compare_and_fusion
  86.1 2.0 gather_fusion
  88.1 0.1 copy.37
  88.2 0.1 pad.14.clone
  88.3 20.4 %reduce-scatter.2.cloned.1.call-done = f32[512,160]{0,1:T(8,128)} async-done(((f32[2048,160]{0,1:T(8,128)}), f32[512,160]{0,1:T(8,128)}) %reduce-scatter.2.cloned.1.call-update) | async-done | bytes 327696 | tf_op jit(solution)/shard_map/reduce_scatter | solution.py:210
  108.6 1.1 multiply_reduce_fusion
  109.7 0.0 copy-start.2
  109.7 0.8 maximum_maximum_fusion
  110.5 0.0 all-gather.8.cloned.1.call-update
  110.5 0.0 all-gather.10.cloned.1.call-start
  110.6 0.0 copy-done.5
  110.6 1.7 copy.40
  112.3 2.5 copy.42
  114.9 0.0 copy-done.2
  114.9 4.4 %multiply_convert_fusion.1 = (bf16[5120,108]{1,0:T(8,128)(2,1)}, bf16[5120,108]{1,0:T(8,128)(2,1)}) fusion(bf16[5120,108]{1,0:T(8,128)(2,1)S(1)} %copy.40, f32[5120]{0:T(1024)S(1)} %convert_element_type.95, bf16[5120,108]{1,0:T(8,128)(2,1)} %copy.42), kind=kLoop, calls=%fused_computation.9 | loop fusion | flops 3317760 | bytes 4444160 | tf_op jit(solution)/shard_map/convert_element_type | solution.py:235
  119.2 1.9 copy.43
  121.2 2.9 copy.41
  124.1 3.4 %fusion.2.w_ref = bf16[32,224,160]{2,1,0:T(8,128)(2,1)} fusion(bf16[32,108,160]{2,1,0:T(8,128)(2,1)S(1)} %bitcast.25, bf16[32,108,160]{2,1,0:T(8,128)(2,1)} %bitcast.26), kind=kLoop, calls=%fused_computation.7 | loop fusion | flops 9175040 | bytes 4505600 | tf_op jit(solution)/shard_map/concatenate | solution.py:239
  127.4 74.0 %all-gather.8.cloned.1.call-done = bf16[22528,512]{1,0:T(8,128)(2,1)} async-done(((bf16[176,512]{1,0:T(8,128)(2,1)}), bf16[22528,512]{1,0:T(8,128)(2,1)}) %all-gather.8.cloned.1.call-update) | async-done | bytes 23068688 | tf_op jit(solution)/shard_map/all_gather | solution.py:227
  201.4 17.0 %shard_map.141 = bf16[108,2048]{1,0:T(8,128)(2,1)} custom-call(bf16[32,4,176,512]{3,2,1,0:T(8,128)(2,1)} %bitcast.24, bf16[32,224,160]{2,1,0:T(8,128)(2,1)} %fusion.2.w_ref), custom_call_target="tpu_custom_call" | custom-call | flops 4697620480 | bytes 25804800 | tf_op jit(solution)/shard_map/pallas_call | solution.py:142
  218.5 0.0 all-gather.10.cloned.1.call-update
  218.5 28.2 %all-gather.10.cloned.1.call-done = bf16[4,108,2048]{2,1,0:T(8,128)(2,1)} async-done(((bf16[1,108,2048]{2,1,0:T(8,128)(2,1)}), bf16[4,108,2048]{2,1,0:T(8,128)(2,1)}) %all-gather.10.cloned.1.call-update) | async-done | bytes 1769488 | tf_op jit(solution)/shard_map/all_gather | solution.py:241
  246.7 1.6 reshape.161
  248.4 0.0 copy-done
  248.4 3.2 %convolution_convert_fusion = bf16[2048,1280]{1,0:T(8,128)(2,1)S(1)} fusion(bf16[432,2048]{1,0:T(8,128)(2,1)S(1)} %reshape.161, bf16[432,1280]{1,0:T(8,128)(2,1)S(1)} %copy-done), kind=kOutput, calls=%fused_computation.2 | convolution fusion | flops 2267545600 | bytes 8118272 | tf_op jit(solution)/shard_map/dot_general | solution.py:242
  251.6 0.6 copy.44
  252.2 9.1 %all_to_all.10 = bf16[16,2,64,1280]{3,2,0,1:T(8,128)(2,1)} all-to-all(bf16[16,2,64,1280]{3,2,0,1:T(8,128)(2,1)S(1)} %copy.44), channel_id=1, replica_groups=mesh['chip'=16,'core'=2,'y'=4] {'core'}, dimensions={1} | all-to-all | bytes 10485760 | tf_op jit(solution)/shard_map/all_to_all | solution.py:248
  261.2 5.7 %reduce_sum.37 = bf16[16,64,1280]{2,1,0:T(8,128)(2,1)} reduce(bf16[16,2,64,1280]{3,2,0,1:T(8,128)(2,1)} %all_to_all.10, bf16[]{:T(256)} %constant.62.clone.1), dimensions={1}, to_apply=%region_3.4 | reduce | flops 1310720 | bytes 7864322 | tf_op jit(solution)/shard_map/reduce_sum | solution.py:249
  267.0 41.4 %all_to_all.11 = bf16[16,64,1280]{2,1,0:T(8,128)(2,1)} all-to-all(bf16[16,64,1280]{2,1,0:T(8,128)(2,1)} %reduce_sum.37), channel_id=1, replica_groups=mesh['chip'=16,'core'=2,'y'=4] {'chip'}, dimensions={0} | all-to-all | bytes 5242880 | tf_op jit(solution)/shard_map/all_to_all | solution.py:250
  308.4 2.8 reduce_sum.38
  (8 shorter events, 0.0 us)
Async XLA Ops:
  7.2 241.2 %copy-start = (bf16[432,1280]{1,0:T(8,128)(2,1)S(1)}, bf16[432,1280]{1,0:T(8,128)(2,1)}, u32[]{:S(2)}) copy-start(bf16[432,1280]{1,0:T(8,128)(2,1)} %param.25) | copy-start | bytes 3317764
  7.2 72.1 %all-gather.6.cloned.1.call-start = ((), (), s32[]{:S(2)}) async-start(), calls=%async_computation.3 | async-start | bytes 5406720 | tf_op jit(solution)/shard_map/all_gather | solution.py:206
  10.5 3.9 %copy-start.4 = (s32[64,1]{1,0:T(8,128)}, s32[64,1]{1,0:T(8,128)S(1)}, u32[]{:S(2)}) copy-start(s32[64,1]{1,0:T(8,128)S(1)} %broadcast_in_dim.48.end_ref) | copy-start | bytes 772
  15.8 63.4 %copy-start.3 = (bf16[1280,160]{0,1:T(8,128)(2,1)S(1)}, bf16[1280,160]{0,1:T(8,128)(2,1)}, u32[]{:S(2)}) copy-start(bf16[1280,160]{0,1:T(8,128)(2,1)} %param.21) | copy-start | bytes 1228804
  29.3 55.5 %copy-start.1 = (bf16[2048,160]{0,1:T(8,128)(2,1)S(1)}, bf16[2048,160]{0,1:T(8,128)(2,1)}, u32[]{:S(2)}) copy-start(bf16[2048,160]{0,1:T(8,128)(2,1)} %param.20) | copy-start | bytes 1966084
  29.3 79.3 %reduce-scatter.2.cloned.1.call-start = ((), (), s32[]{:S(2)}) async-start(), calls=%async_computation.4 | async-start | bytes 1638400 | tf_op jit(solution)/shard_map/reduce_scatter | solution.py:210
  84.7 116.7 %all-gather.8.cloned.1.call-start = ((), (), s32[]{:S(2)}) async-start(), calls=%async_computation.5 | async-start | bytes 23248896 | tf_op jit(solution)/shard_map/all_gather | solution.py:227
  84.8 25.8 %copy-start.5 = (bf16[5120]{0:T(1024)(128)(2,1)S(1)}, bf16[5120]{0:T(1024)(128)(2,1)}, u32[]{:S(2)}) copy-start(bf16[5120]{0:T(1024)(128)(2,1)} %param.22) | copy-start | bytes 30724
  109.7 5.2 %copy-start.2 = (bf16[512,160]{0,1:T(8,128)(2,1)}, bf16[512,160]{0,1:T(8,128)(2,1)S(1)}, u32[]{:S(2)}) copy-start(bf16[512,160]{0,1:T(8,128)(2,1)S(1)} %get-tuple-element.3) | copy-start | bytes 491524
  110.5 136.2 %all-gather.10.cloned.1.call-start = ((), (), s32[]{:S(2)}) async-start(), calls=%async_computation.6 | async-start | bytes 2293760 | tf_op jit(solution)/shard_map/all_gather | solution.py:241
Sparse Core Ops, SparseCore 0:
  29.4 49.8 all-gather.5
  84.8 23.7 reduce-scatter.1
  111.8 89.6 all-gather.7
  218.6 28.0 all-gather.9

commit v7 on v6

--- a/solution.py
+++ b/solution.py
@@ -9,10 +9,11 @@
 
 D = 5120
 HD = 128
-CHIPS = "chip"
+CHIP_AXES = ("z", "x")
 CORE = "core"
-REQ = (CHIPS, CORE)
+REQ = CHIP_AXES + (CORE,)
 CORES_PER_CHIP = 2
+X_CHIPS = 4
 HEAD = "y"
 HEADS_PER_STEP = 2
 R_PER_STEP = 8
@@ -242,13 +243,15 @@
     down_sums = lax.dot_general(
         active_all, down_proj, (((0,), (0,)), ((), ())), preferred_element_type=jnp.float32
     )
-    cores = lax.axis_size(CORE)
-    chips = req_count // cores
-    pieces = down_sums.astype(jnp.bfloat16).reshape(chips, cores, owned, down_sums.shape[1])
-    on_chip = lax.all_to_all(pieces, CORE, 1, 1, tiled=True)
-    chip_sums = jnp.sum(on_chip.astype(jnp.float32), axis=1).astype(jnp.bfloat16)
-    received = lax.all_to_all(chip_sums, CHIPS, 0, 0, tiled=True)
-    ffn_out = jnp.sum(received.astype(jnp.float32), axis=0).astype(jnp.bfloat16)
+    width = down_sums.shape[1]
+    stages = (CORE,) + CHIP_AXES[::-1]
+    sizes = [lax.axis_size(name) for name in REQ]
+    running = down_sums.astype(jnp.bfloat16).reshape(*sizes, owned, width)
+    for name in stages:
+        place = REQ.index(name)
+        swapped = lax.all_to_all(running, name, place, place, tiled=True)
+        running = jnp.sum(swapped.astype(jnp.float32), axis=place).astype(jnp.bfloat16)
+    ffn_out = running
     return (attended, ffn_out)
 
 
@@ -269,9 +272,10 @@
         P(REQ, HEAD),
     )
     req_size, head_size = mesh.devices.shape
+    z_chips = req_size // (CORES_PER_CHIP * X_CHIPS)
     named = jax.sharding.Mesh(
-        mesh.devices.reshape(req_size // CORES_PER_CHIP, CORES_PER_CHIP, head_size),
-        (CHIPS, CORE, HEAD),
+        mesh.devices.reshape(z_chips, X_CHIPS, CORES_PER_CHIP, head_size),
+        CHIP_AXES + (CORE, HEAD),
     )
     return jax.shard_map(
         body,

time: 318 us -> 330 us (1.038)
  blocking collectives: 50.5 us -> 59.6 us
    all_to_all x2 -> x3, blocking collectives: 50.5 us -> 59.6 us  [body(): swapped = lax.all_to_all(running, name, place, place, tiled=True)]
    reduce_sum x2 -> x3, other arithmetic: 8.56 us -> 8.76 us  [body(): jnp.sum(swapped.astype(jnp.float32), axis=place).astype(jnp.bfloat16)]
where the time goes in v7:
time: 330 us; the launch traced here: 329 us
  waiting for transfers between devices  172 us (52%)
  blocking collectives  59.6 us (18%)
  Pallas kernels  30.5 us (9%)
  other arithmetic  22 us (7%)
  local copies, waits for them, and re-layouts  21.6 us (7%)
  between operations  14 us (4%)
  matrix products  8.63 us (3%)
    all_gather x1, waiting for transfers between devices, body(): lax.all_gather(block_t[None], REQ + (HEAD,), axis=0, tiled=True)  73.9 us
    all_to_all x3, blocking collectives, body(): swapped = lax.all_to_all(running, name, place, place, tiled=True)  59.6 us
    all_gather x1, waiting for transfers between devices, body(): lax.all_gather(attention, REQ, axis=0, tiled=True)  49.9 us
    all_gather x1, waiting for transfers between devices, body(): active_all = lax.all_gather(active_t, HEAD, axis=0, tiled=True)  28.2 us
    reduce_scatter x1, waiting for transfers between devices, body(): lax.psum_scatter(partial_sums, HEAD, scatter_dimension=0, tiled=True)  20.4 us
    pallas_call x1, Pallas kernels, gate_up(): pl.pallas_call(gate_up_kernel, grid=(chunks // R_PER_STEP,), in_specs=[pl...  17 us
    pallas_call x1, Pallas kernels, attend_local(): pl.pallas_call(attention_kernel, grid=(steps,), in_specs=[bound_spec, bou...  13.4 us
    reduce_sum x3, other arithmetic, body(): jnp.sum(swapped.astype(jnp.float32), axis=place).astype(jnp.bfloat16)  8.76 us
  transfers between devices with their start and end apart: 4, of which 4 were waited for; matrix products, arithmetic and copies ran while one was open for 6% of the time, Pallas kernels for 0%

profile of v7, /device:TPU:0, one launch (start us, length us, event | category | flops | bytes accessed | tf_op | source)
XLA Modules:
  0.0 328.9 jit_solution(2756011882785369879)
XLA Ops:
  7.2 0.0 copy-start
  7.2 0.0 all-gather.6.cloned.1.call-start
  7.3 0.8 compare_select_fusion.1
  8.1 1.5 gather_fusion.1
  9.6 0.8 fusion.3
  10.3 0.1 copy.48
  10.4 0.1 broadcast_in_dim.48.end_ref
  10.5 0.0 copy-start.4
  10.5 0.1 reduce.3
  10.7 0.7 copy.49.start_ref
  11.4 1.0 reshape.137
  12.4 1.0 reshape.139
  13.4 0.2 multiply_cosine_fusion
  13.6 0.5 subtract_convert_fusion
  14.1 0.3 pad_maximum_fusion
  14.4 0.0 copy-done.4
  14.4 0.7 copy.61
  15.1 0.7 copy.60
  15.8 0.0 copy-start.3
  15.9 13.4 %shard_map.140 = bf16[64,1280]{1,0:T(8,128)(2,1)} custom-call(s32[64,1]{1,0:T(8,128)} %copy.49.start_ref, s32[64,1]{1,0:T(8,128)} %copy-done.4, bf16[64,1280]{1,0:T(8,128)(2,1)} %bitcast.33, bf16[64,1280]{1,0:T(8,128)(2,1)} %bitcast.34, bf16[64,1280]{1,0:T(8,128)(2,1)} %vn_ref.1, bf16[3536,1280]{1,0:T(8,128)(2,1)} %kp_ref.1, bf16[3536,1280]{1,0:T(8,128)(2,1)} %vp_ref.1), custom_call_target="tpu_custom_call" | custom-call | flops 1158676480 | bytes 18759680 | tf_op jit(solution)/shard_map/pallas_call | solution.py:91
  29.3 0.0 all-gather.6.cloned.1.call-update
  29.3 0.0 copy-start.1
  29.3 0.0 reduce-scatter.2.cloned.1.call-start
  29.4 49.9 %all-gather.6.cloned.1.call-done = bf16[2048,1280]{1,0:T(8,128)(2,1)} async-done(((bf16[64,1280]{1,0:T(8,128)(2,1)}), bf16[2048,1280]{1,0:T(8,128)(2,1)}) %all-gather.6.cloned.1.call-update) | async-done | bytes 5242896 | tf_op jit(solution)/shard_map/all_gather | solution.py:207
  79.3 0.0 copy-done.3
  79.3 5.4 %fusion.4 = f32[2048,160]{0,1:T(8,128)} fusion(bf16[2048,1280]{1,0:T(8,128)(2,1)} %all-gather.6.cloned.1.call-done, bf16[1280,160]{0,1:T(8,128)(2,1)S(1)} %copy-done.3), kind=kOutput, calls=%fused_computation.33 | convolution fusion | flops 838860800 | bytes 6963200 | tf_op jit(solution)/shard_map/dot_general | solution.py:206
  84.7 0.0 reduce-scatter.2.cloned.1.call-update
  84.7 0.0 all-gather.8.cloned.1.call-start
  84.8 0.0 copy-done.1
  84.8 0.0 copy-start.5
  84.8 0.5 copy.46
  85.3 0.8 compare_and_fusion
  86.1 2.0 gather_fusion
  88.1 0.1 copy.47
  88.2 0.1 pad.14.clone
  88.3 20.4 %reduce-scatter.2.cloned.1.call-done = f32[512,160]{0,1:T(8,128)} async-done(((f32[2048,160]{0,1:T(8,128)}), f32[512,160]{0,1:T(8,128)}) %reduce-scatter.2.cloned.1.call-update) | async-done | bytes 327696 | tf_op jit(solution)/shard_map/reduce_scatter | solution.py:211
  108.6 1.1 multiply_reduce_fusion
  109.7 0.0 copy-start.2
  109.7 0.8 maximum_maximum_fusion
  110.5 0.0 all-gather.8.cloned.1.call-update
  110.5 0.0 all-gather.10.cloned.1.call-start
  110.6 0.0 copy-done.5
  110.6 1.7 copy.50
  112.3 2.5 copy.52
  114.9 0.0 copy-done.2
  114.9 4.4 %multiply_convert_fusion.1 = (bf16[5120,108]{1,0:T(8,128)(2,1)}, bf16[5120,108]{1,0:T(8,128)(2,1)}) fusion(bf16[5120,108]{1,0:T(8,128)(2,1)S(1)} %copy.50, f32[5120]{0:T(1024)S(1)} %convert_element_type.97, bf16[5120,108]{1,0:T(8,128)(2,1)} %copy.52), kind=kLoop, calls=%fused_computation.9 | loop fusion | flops 3317760 | bytes 4444160 | tf_op jit(solution)/shard_map/convert_element_type | solution.py:236
  119.3 1.9 copy.53
  121.2 2.9 copy.51
  124.1 3.4 %fusion.2.w_ref = bf16[32,224,160]{2,1,0:T(8,128)(2,1)} fusion(bf16[32,108,160]{2,1,0:T(8,128)(2,1)S(1)} %bitcast.25, bf16[32,108,160]{2,1,0:T(8,128)(2,1)} %bitcast.26), kind=kLoop, calls=%fused_computation.7 | loop fusion | flops 9175040 | bytes 4505600 | tf_op jit(solution)/shard_map/concatenate | solution.py:240
  127.5 73.9 %all-gather.8.cloned.1.call-done = bf16[22528,512]{1,0:T(8,128)(2,1)} async-done(((bf16[176,512]{1,0:T(8,128)(2,1)}), bf16[22528,512]{1,0:T(8,128)(2,1)}) %all-gather.8.cloned.1.call-update) | async-done | bytes 23068688 | tf_op jit(solution)/shard_map/all_gather | solution.py:228
  201.4 17.0 %shard_map.141 = bf16[108,2048]{1,0:T(8,128)(2,1)} custom-call(bf16[32,4,176,512]{3,2,1,0:T(8,128)(2,1)} %bitcast.24, bf16[32,224,160]{2,1,0:T(8,128)(2,1)} %fusion.2.w_ref), custom_call_target="tpu_custom_call" | custom-call | flops 4697620480 | bytes 25804800 | tf_op jit(solution)/shard_map/pallas_call | solution.py:143
  218.4 0.0 all-gather.10.cloned.1.call-update
  218.5 28.2 %all-gather.10.cloned.1.call-done = bf16[4,108,2048]{2,1,0:T(8,128)(2,1)} async-done(((bf16[1,108,2048]{2,1,0:T(8,128)(2,1)}), bf16[4,108,2048]{2,1,0:T(8,128)(2,1)}) %all-gather.10.cloned.1.call-update) | async-done | bytes 1769488 | tf_op jit(solution)/shard_map/all_gather | solution.py:242
  246.7 1.6 reshape.161
  248.3 0.0 copy-done
  248.3 3.2 convolution_convert_fusion
  251.5 0.6 copy.54
  252.1 9.1 %all_to_all.15 = bf16[4,4,2,64,1280]{4,3,1,0,2:T(8,128)(2,1)} all-to-all(bf16[4,4,2,64,1280]{4,3,1,0,2:T(8,128)(2,1)S(1)} %copy.54), channel_id=1, replica_groups=mesh['z'=4,'x'=4,'core'=2,'y'=4] {'core'}, dimensions={2} | all-to-all | bytes 10485760 | tf_op jit(solution)/shard_map/all_to_all | solution.py:252
  261.2 5.8 %reduce_sum.49 = bf16[4,4,64,1280]{3,2,1,0:T(8,128)(2,1)} reduce(bf16[4,4,2,64,1280]{4,3,1,0,2:T(8,128)(2,1)} %all_to_all.15, bf16[]{:T(256)} %constant.67.clone.1), dimensions={2}, to_apply=%region_3.4 | reduce | flops 1310720 | bytes 7864322 | tf_op jit(solution)/shard_map/reduce_sum | solution.py:253
  266.9 1.9 copy.55
  268.9 36.5 %all_to_all.16 = bf16[4,4,64,1280]{3,2,0,1:T(8,128)(2,1)} all-to-all(bf16[4,4,64,1280]{3,2,0,1:T(8,128)(2,1)S(1)} %copy.55), channel_id=1, replica_groups=mesh['z'=4,'x'=4,'core'=2,'y'=4] {'x'}, dimensions={1} | all-to-all | bytes 5242880 | tf_op jit(solution)/shard_map/all_to_all | solution.py:252
  305.3 2.2 reduce_sum.50
  307.5 14.0 %all_to_all.17 = bf16[4,64,1280]{2,1,0:T(8,128)(2,1)S(1)} all-to-all(bf16[4,64,1280]{2,1,0:T(8,128)(2,1)S(1)} %reduce_sum.50), channel_id=1, replica_groups=mesh['z'=4,'x'=4,'core'=2,'y'=4] {'z'}, dimensions={0} | all-to-all | bytes 1310720 | tf_op jit(solution)/shard_map/all_to_all | solution.py:252
  321.6 0.8 reduce_sum.51
  (8 shorter events, 0.0 us)
Async XLA Ops:
  7.2 241.2 %copy-start = (bf16[432,1280]{1,0:T(8,128)(2,1)S(1)}, bf16[432,1280]{1,0:T(8,128)(2,1)}, u32[]{:S(2)}) copy-start(bf16[432,1280]{1,0:T(8,128)(2,1)} %param.25) | copy-start | bytes 3317764
  7.2 72.1 %all-gather.6.cloned.1.call-start = ((), (), s32[]{:S(2)}) async-start(), calls=%async_computation.4 | async-start | bytes 5406720 | tf_op jit(solution)/shard_map/all_gather | solution.py:207
  10.5 3.9 %copy-start.4 = (s32[64,1]{1,0:T(8,128)}, s32[64,1]{1,0:T(8,128)S(1)}, u32[]{:S(2)}) copy-start(s32[64,1]{1,0:T(8,128)S(1)} %broadcast_in_dim.48.end_ref) | copy-start | bytes 772
  15.8 63.4 %copy-start.3 = (bf16[1280,160]{0,1:T(8,128)(2,1)S(1)}, bf16[1280,160]{0,1:T(8,128)(2,1)}, u32[]{:S(2)}) copy-start(bf16[1280,160]{0,1:T(8,128)(2,1)} %param.21) | copy-start | bytes 1228804
  29.3 55.5 %copy-start.1 = (bf16[2048,160]{0,1:T(8,128)(2,1)S(1)}, bf16[2048,160]{0,1:T(8,128)(2,1)}, u32[]{:S(2)}) copy-start(bf16[2048,160]{0,1:T(8,128)(2,1)} %param.20) | copy-start | bytes 1966084
  29.3 79.3 %reduce-scatter.2.cloned.1.call-start = ((), (), s32[]{:S(2)}) async-start(), calls=%async_computation.5 | async-start | bytes 1638400 | tf_op jit(solution)/shard_map/reduce_scatter | solution.py:211
  84.7 116.7 %all-gather.8.cloned.1.call-start = ((), (), s32[]{:S(2)}) async-start(), calls=%async_computation.6 | async-start | bytes 23248896 | tf_op jit(solution)/shard_map/all_gather | solution.py:228
  84.8 25.8 %copy-start.5 = (bf16[5120]{0:T(1024)(128)(2,1)S(1)}, bf16[5120]{0:T(1024)(128)(2,1)}, u32[]{:S(2)}) copy-start(bf16[5120]{0:T(1024)(128)(2,1)} %param.22) | copy-start | bytes 30724
  109.7 5.2 %copy-start.2 = (bf16[512,160]{0,1:T(8,128)(2,1)}, bf16[512,160]{0,1:T(8,128)(2,1)S(1)}, u32[]{:S(2)}) copy-start(bf16[512,160]{0,1:T(8,128)(2,1)S(1)} %get-tuple-element.3) | copy-start | bytes 491524
  110.5 136.2 %all-gather.10.cloned.1.call-start = ((), (), s32[]{:S(2)}) async-start(), calls=%async_computation.7 | async-start | bytes 2293760 | tf_op jit(solution)/shard_map/all_gather | solution.py:242
Sparse Core Ops, SparseCore 0:
  29.4 49.8 all-gather.5
  84.9 23.7 reduce-scatter.1
  111.8 89.5 all-gather.7
  218.6 28.0 all-gather.9

commit v8 on v6

--- a/solution.py
+++ b/solution.py
@@ -245,8 +245,11 @@
     cores = lax.axis_size(CORE)
     chips = req_count // cores
     pieces = down_sums.astype(jnp.bfloat16).reshape(chips, cores, owned, down_sums.shape[1])
-    on_chip = lax.all_to_all(pieces, CORE, 1, 1, tiled=True)
-    chip_sums = jnp.sum(on_chip.astype(jnp.float32), axis=1).astype(jnp.bfloat16)
+    my_core = lax.axis_index(CORE)
+    kept = lax.dynamic_index_in_dim(pieces, my_core, axis=1, keepdims=False)
+    sent = lax.dynamic_index_in_dim(pieces, cores - 1 - my_core, axis=1, keepdims=False)
+    arrived = lax.ppermute(sent, CORE, [(core, cores - 1 - core) for core in range(cores)])
+    chip_sums = (kept.astype(jnp.float32) + arrived.astype(jnp.float32)).astype(jnp.bfloat16)
     received = lax.all_to_all(chip_sums, CHIPS, 0, 0, tiled=True)
     ffn_out = jnp.sum(received.astype(jnp.float32), axis=0).astype(jnp.bfloat16)
     return (attended, ffn_out)

time: 318 us -> 314 us (0.987)
  blocking collectives: 50.5 us -> 41.2 us
  waiting for transfers between devices: 173 us -> 178 us
    all_to_all x1 -> x0, blocking collectives: 9.09 us -> none  [body(): on_chip = lax.all_to_all(pieces, CORE, 1, 1, tiled=True)]
    reduce_sum x1 -> x0, other arithmetic: 5.75 us -> none  [body(): jnp.sum(on_chip.astype(jnp.float32), axis=1).astype(jnp.bfloat16)]
    ppermute x0 -> x1, waiting for transfers between devices: none -> 5.25 us  [body(): lax.ppermute(sent, CORE, [(core, cores - 1 - core) for core in range(core...]
    convert_element_type x0 -> x1, other arithmetic: none -> 3.27 us  [body(): (kept.astype(jnp.float32) + arrived.astype(jnp.float32)).astype(jnp.bfloa...]
    unnamed x18 -> x20, local copies, waits for them, and re-layouts: 7.88 us -> 9.16 us
  transfers between devices with their start and end apart: 4 -> 5, of which waited for: 4 -> 5; matrix products, arithmetic and copies ran while one was open for 6% -> 6% of each run, Pallas kernels for 0% -> 0%
where the time goes in v8:
time: 314 us
  waiting for transfers between devices  178 us (57%)
  blocking collectives  41.2 us (13%)
  Pallas kernels  30.5 us (10%)
  local copies, waits for them, and re-layouts  22.4 us (7%)
  other arithmetic  19.2 us (6%)
  between operations  14 us (4%)
  matrix products  8.62 us (3%)
    all_gather x1, waiting for transfers between devices, body(): lax.all_gather(block_t[None], REQ + (HEAD,), axis=0, tiled=True)  74.1 us
    all_gather x1, waiting for transfers between devices, body(): lax.all_gather(attention, REQ, axis=0, tiled=True)  49.9 us
    all_to_all x1, blocking collectives, body(): received = lax.all_to_all(chip_sums, CHIPS, 0, 0, tiled=True)  41.2 us
    all_gather x1, waiting for transfers between devices, body(): active_all = lax.all_gather(active_t, HEAD, axis=0, tiled=True)  28.2 us
    reduce_scatter x1, waiting for transfers between devices, body(): lax.psum_scatter(partial_sums, HEAD, scatter_dimension=0, tiled=True)  20.4 us
    pallas_call x1, Pallas kernels, gate_up(): pl.pallas_call(gate_up_kernel, grid=(chunks // R_PER_STEP,), in_specs=[pl...  17 us
    pallas_call x1, Pallas kernels, attend_local(): pl.pallas_call(attention_kernel, grid=(steps,), in_specs=[bound_spec, bou...  13.4 us
    unnamed x20, local copies, waits for them, and re-layouts  9.16 us
  transfers between devices with their start and end apart: 5, of which 5 were waited for; matrix products, arithmetic and copies ran while one was open for 6% of the time, Pallas kernels for 0%

profile of v8, /device:TPU:0, one launch (start us, length us, event | category | flops | bytes accessed | tf_op | source)
XLA Modules:
  0.0 313.9 jit_solution(2443390136751346900)
XLA Ops:
  7.2 0.0 copy-start
  7.2 0.0 all-gather.6.cloned.1.call-start
  7.3 0.8 compare_select_fusion.1
  8.1 1.5 gather_fusion.1
  9.6 0.8 fusion.4
  10.3 1.0 reshape.139
  11.3 1.0 reshape.141
  12.4 0.2 multiply_cosine_fusion
  12.6 0.5 subtract_convert_fusion
  13.1 0.3 pad_maximum_fusion
  13.4 0.7 copy.39
  14.1 0.7 copy.40
  14.8 0.1 copy.29
  14.9 0.1 broadcast_in_dim.48.end_ref
  15.0 0.0 copy-start.5
  15.0 0.1 reduce.1
  15.1 0.7 copy.30.start_ref
  15.8 0.0 copy-done.5
  15.8 0.0 copy-start.4
  15.8 13.4 %shard_map.140 = bf16[64,1280]{1,0:T(8,128)(2,1)} custom-call(s32[64,1]{1,0:T(8,128)} %copy.30.start_ref, s32[64,1]{1,0:T(8,128)} %copy-done.5, bf16[64,1280]{1,0:T(8,128)(2,1)} %bitcast.40, bf16[64,1280]{1,0:T(8,128)(2,1)} %bitcast.39, bf16[64,1280]{1,0:T(8,128)(2,1)} %vn_ref.1, bf16[3536,1280]{1,0:T(8,128)(2,1)} %kp_ref.1, bf16[3536,1280]{1,0:T(8,128)(2,1)} %vp_ref.1), custom_call_target="tpu_custom_call" | custom-call | flops 1158676480 | bytes 18759680 | tf_op jit(solution)/shard_map/pallas_call | solution.py:90
  29.3 0.0 all-gather.6.cloned.1.call-update
  29.3 0.0 copy-start.2
  29.3 0.0 reduce-scatter.2.cloned.1.call-start
  29.4 49.9 %all-gather.6.cloned.1.call-done = bf16[2048,1280]{1,0:T(8,128)(2,1)} async-done(((bf16[64,1280]{1,0:T(8,128)(2,1)}), bf16[2048,1280]{1,0:T(8,128)(2,1)}) %all-gather.6.cloned.1.call-update) | async-done | bytes 5242896 | tf_op jit(solution)/shard_map/all_gather | solution.py:206
  79.3 0.0 copy-done.4
  79.3 5.4 %fusion.5 = f32[2048,160]{0,1:T(8,128)} fusion(bf16[2048,1280]{1,0:T(8,128)(2,1)} %all-gather.6.cloned.1.call-done, bf16[1280,160]{0,1:T(8,128)(2,1)S(1)} %copy-done.4), kind=kOutput, calls=%fused_computation.36 | convolution fusion | flops 838860800 | bytes 6963200 | tf_op jit(solution)/shard_map/dot_general | solution.py:205
  84.7 0.0 reduce-scatter.2.cloned.1.call-update
  84.7 0.0 all-gather.8.cloned.1.call-start
  84.8 0.0 copy-done.2
  84.8 0.5 copy.27
  85.3 0.8 compare_and_fusion
  86.1 2.0 gather_fusion
  88.0 0.1 copy.28
  88.2 0.1 pad.14.clone
  88.3 20.4 %reduce-scatter.2.cloned.1.call-done = f32[512,160]{0,1:T(8,128)} async-done(((f32[2048,160]{0,1:T(8,128)}), f32[512,160]{0,1:T(8,128)}) %reduce-scatter.2.cloned.1.call-update) | async-done | bytes 327696 | tf_op jit(solution)/shard_map/reduce_scatter | solution.py:210
  108.6 1.1 multiply_reduce_fusion
  109.7 0.0 copy-start.3
  109.7 0.8 maximum_maximum_fusion
  110.5 0.0 copy-start.6
  110.5 0.0 all-gather.8.cloned.1.call-update
  110.5 0.0 all-gather.10.cloned.1.call-start
  110.6 1.7 copy.31
  112.3 2.5 copy.33
  114.8 0.0 copy-done.3
  114.8 0.0 copy-done.6
  114.8 4.3 %multiply_convert_fusion.1 = (bf16[5120,108]{1,0:T(8,128)(2,1)}, bf16[5120,108]{1,0:T(8,128)(2,1)}) fusion(bf16[5120,108]{1,0:T(8,128)(2,1)S(1)} %copy.31, f32[5120]{0:T(1024)S(1)} %convert_element_type.105, bf16[5120,108]{1,0:T(8,128)(2,1)} %copy.33), kind=kLoop, calls=%fused_computation.12 | loop fusion | flops 3317760 | bytes 4444160 | tf_op jit(solution)/shard_map/convert_element_type | solution.py:235
  119.2 1.9 copy.32
  121.1 2.9 copy.34
  124.0 3.3 %fusion.3.w_ref = bf16[32,224,160]{2,1,0:T(8,128)(2,1)} fusion(bf16[32,108,160]{2,1,0:T(8,128)(2,1)} %bitcast.31, bf16[32,108,160]{2,1,0:T(8,128)(2,1)S(1)} %bitcast.30), kind=kLoop, calls=%fused_computation.9 | loop fusion | flops 9175040 | bytes 4505600 | tf_op jit(solution)/shard_map/concatenate | solution.py:239
  127.3 74.1 %all-gather.8.cloned.1.call-done = bf16[22528,512]{1,0:T(8,128)(2,1)} async-done(((bf16[176,512]{1,0:T(8,128)(2,1)}), bf16[22528,512]{1,0:T(8,128)(2,1)}) %all-gather.8.cloned.1.call-update) | async-done | bytes 23068688 | tf_op jit(solution)/shard_map/all_gather | solution.py:227
  201.4 17.0 %shard_map.141 = bf16[108,2048]{1,0:T(8,128)(2,1)} custom-call(bf16[32,4,176,512]{3,2,1,0:T(8,128)(2,1)} %bitcast.29, bf16[32,224,160]{2,1,0:T(8,128)(2,1)} %fusion.3.w_ref), custom_call_target="tpu_custom_call" | custom-call | flops 4697620480 | bytes 25804800 | tf_op jit(solution)/shard_map/pallas_call | solution.py:142
  218.5 0.0 all-gather.10.cloned.1.call-update
  218.5 28.2 %all-gather.10.cloned.1.call-done = bf16[4,108,2048]{2,1,0:T(8,128)(2,1)} async-done(((bf16[1,108,2048]{2,1,0:T(8,128)(2,1)}), bf16[4,108,2048]{2,1,0:T(8,128)(2,1)}) %all-gather.10.cloned.1.call-update) | async-done | bytes 1769488 | tf_op jit(solution)/shard_map/all_gather | solution.py:241
  246.7 1.6 reshape.164
  248.4 0.0 copy-done
  248.4 3.2 %convolution_convert_fusion = bf16[2048,1280]{1,0:T(8,128)(2,1)S(1)} fusion(bf16[432,2048]{1,0:T(8,128)(2,1)S(1)} %reshape.164, bf16[432,1280]{1,0:T(8,128)(2,1)S(1)} %copy-done), kind=kOutput, calls=%fused_computation.2 | convolution fusion | flops 2267545600 | bytes 8118272 | tf_op jit(solution)/shard_map/dot_general | solution.py:242
  251.6 0.0 copy-start.1
  251.6 2.0 dynamic-slice_bitcast_fusion
  253.6 1.3 copy-done.1
  254.9 0.0 collective-permute-start
  254.9 5.2 %collective-permute-done = bf16[16,64,1280]{2,1,0:T(8,128)(2,1)} collective-permute-done((bf16[16,64,1280]{2,1,0:T(8,128)(2,1)}, bf16[16,64,1280]{2,1,0:T(8,128)(2,1)}, u32[]{:S(2)}, u32[]{:S(2)}) %collective-permute-start) | collective-permute-done | bytes 2621472 | tf_op jit(solution)/shard_map/ppermute | solution.py:251
  260.1 3.3 %fusion.2 = bf16[16,64,1280]{2,1,0:T(8,128)(2,1)S(1)} fusion(bf16[16,64,1280]{2,1,0:T(8,128)(2,1)} %collective-permute-done, bf16[16,2,64,1280]{3,2,1,0:T(8,128)(2,1)} %bitcast.33, s32[]{:T(128)S(6)} %select_n.44), kind=kLoop, calls=%fused_computation.8 | loop fusion | flops 5242880 | bytes 7864324 | tf_op jit(solution)/shard_map/convert_element_type | solution.py:252
  263.4 41.2 %all_to_all.5 = bf16[16,64,1280]{2,1,0:T(8,128)(2,1)} all-to-all(bf16[16,64,1280]{2,1,0:T(8,128)(2,1)S(1)} %fusion.2), channel_id=1, replica_groups=mesh['chip'=16,'core'=2,'y'=4] {'chip'}, dimensions={0} | all-to-all | bytes 5242880 | tf_op jit(solution)/shard_map/all_to_all | solution.py:253
  304.5 2.8 reduce_sum.25
  (8 shorter events, 0.0 us)
Async XLA Ops:
  7.2 241.2 %copy-start = (bf16[432,1280]{1,0:T(8,128)(2,1)S(1)}, bf16[432,1280]{1,0:T(8,128)(2,1)}, u32[]{:S(2)}) copy-start(bf16[432,1280]{1,0:T(8,128)(2,1)} %param.25) | copy-start | bytes 3317764
  7.2 72.1 %all-gather.6.cloned.1.call-start = ((), (), s32[]{:S(2)}) async-start(), calls=%async_computation.2 | async-start | bytes 5406720 | tf_op jit(solution)/shard_map/all_gather | solution.py:206
  15.0 0.8 copy-start.5
  15.8 63.4 %copy-start.4 = (bf16[1280,160]{0,1:T(8,128)(2,1)S(1)}, bf16[1280,160]{0,1:T(8,128)(2,1)}, u32[]{:S(2)}) copy-start(bf16[1280,160]{0,1:T(8,128)(2,1)} %param.21) | copy-start | bytes 1228804
  29.3 55.5 %copy-start.2 = (bf16[2048,160]{0,1:T(8,128)(2,1)S(1)}, bf16[2048,160]{0,1:T(8,128)(2,1)}, u32[]{:S(2)}) copy-start(bf16[2048,160]{0,1:T(8,128)(2,1)} %param.20) | copy-start | bytes 1966084
  29.3 79.3 %reduce-scatter.2.cloned.1.call-start = ((), (), s32[]{:S(2)}) async-start(), calls=%async_computation.3 | async-start | bytes 1638400 | tf_op jit(solution)/shard_map/reduce_scatter | solution.py:210
  84.7 116.7 %all-gather.8.cloned.1.call-start = ((), (), s32[]{:S(2)}) async-start(), calls=%async_computation.4 | async-start | bytes 23248896 | tf_op jit(solution)/shard_map/all_gather | solution.py:227
  109.7 5.1 %copy-start.3 = (bf16[512,160]{0,1:T(8,128)(2,1)}, bf16[512,160]{0,1:T(8,128)(2,1)S(1)}, u32[]{:S(2)}) copy-start(bf16[512,160]{0,1:T(8,128)(2,1)S(1)} %get-tuple-element.3) | copy-start | bytes 491524
  110.5 4.4 %copy-start.6 = (bf16[5120]{0:T(1024)(128)(2,1)S(1)}, bf16[5120]{0:T(1024)(128)(2,1)}, u32[]{:S(2)}) copy-start(bf16[5120]{0:T(1024)(128)(2,1)} %param.22) | copy-start | bytes 30724
  110.5 136.2 %all-gather.10.cloned.1.call-start = ((), (), s32[]{:S(2)}) async-start(), calls=%async_computation.5 | async-start | bytes 2293760 | tf_op jit(solution)/shard_map/all_gather | solution.py:241
  251.6 3.3 %copy-start.1 = (bf16[2048,1280]{1,0:T(8,128)(2,1)}, bf16[2048,1280]{1,0:T(8,128)(2,1)S(1)}, u32[]{:S(2)}) copy-start(bf16[2048,1280]{1,0:T(8,128)(2,1)S(1)} %convolution_convert_fusion) | copy-start | bytes 15728644
  254.9 5.3 %collective-permute-start = (bf16[16,64,1280]{2,1,0:T(8,128)(2,1)}, bf16[16,64,1280]{2,1,0:T(8,128)(2,1)}, u32[]{:S(2)}, u32[]{:S(2)}) collective-permute-start(bf16[16,64,1280]{2,1,0:T(8,128)(2,1)} %dynamic-slice_bitcast_fusion), channel_id=1, source_target_pairs={{0,4},{4,0},{1,5},{5,1},{2,6},{6,2},{3,7},{7,3},{8,12},{12,8},{9,1... | collective-permute-start | bytes 7864328 | tf_op jit(solution)/shard_map/ppermute | solution.py:251
Sparse Core Ops, SparseCore 0:
  29.4 49.7 all-gather.5
  84.9 23.7 reduce-scatter.1
  111.8 89.6 all-gather.7
  218.6 28.0 all-gather.9

commit v9 on v8

--- a/solution.py
+++ b/solution.py
@@ -250,8 +250,14 @@
     sent = lax.dynamic_index_in_dim(pieces, cores - 1 - my_core, axis=1, keepdims=False)
     arrived = lax.ppermute(sent, CORE, [(core, cores - 1 - core) for core in range(cores)])
     chip_sums = (kept.astype(jnp.float32) + arrived.astype(jnp.float32)).astype(jnp.bfloat16)
-    received = lax.all_to_all(chip_sums, CHIPS, 0, 0, tiled=True)
-    ffn_out = jnp.sum(received.astype(jnp.float32), axis=0).astype(jnp.bfloat16)
+    my_chip = lax.axis_index(CHIPS)
+    order = (my_chip + jnp.arange(chips, dtype=jnp.int32)) % chips
+    rolled = jnp.take(chip_sums, order, axis=0)
+    total = rolled[0].astype(jnp.float32)
+    for shift in range(1, chips):
+        pairs = [(chip, (chip + shift) % chips) for chip in range(chips)]
+        total = total + lax.ppermute(rolled[shift], CHIPS, pairs).astype(jnp.float32)
+    ffn_out = total.astype(jnp.bfloat16)
     return (attended, ffn_out)
 
 

time: 314 us -> 337 us (1.073)
  blocking collectives: 41.2 us -> 0 us
  starting transfers between devices: 0.17 us -> 40.2 us
  waiting for transfers between devices: 178 us -> 195 us
  local copies, waits for them, and re-layouts: 22.4 us -> 26.6 us
    all_to_all x1 -> x0, blocking collectives: 41.2 us -> none  [body(): received = lax.all_to_all(chip_sums, CHIPS, 0, 0, tiled=True)]
    ppermute x0 -> x15, starting transfers between devices: none -> 40.1 us  [body(): lax.ppermute(rolled[shift], CHIPS, pairs).astype(jnp.float32)]
    ppermute x0 -> x15, waiting for transfers between devices: none -> 17.7 us  [body(): lax.ppermute(rolled[shift], CHIPS, pairs).astype(jnp.float32)]
    gather x0 -> x1, local copies, waits for them, and re-layouts: none -> 3.96 us  [body(): rolled = jnp.take(chip_sums, order, axis=0)]
  transfers between devices with their start and end apart: 5 -> 20, of which waited for: 5 -> 8; matrix products, arithmetic and copies ran while one was open for 6% -> 6% of each run, Pallas kernels for 0% -> 0%
where the time goes in v9:
time: 337 us; the launch traced here: 336 us
  waiting for transfers between devices  195 us (58%)
  starting transfers between devices  40.2 us (12%)
  Pallas kernels  30.5 us (9%)
  local copies, waits for them, and re-layouts  26.6 us (8%)
  other arithmetic  21.2 us (6%)
  between operations  14 us (4%)
  matrix products  8.59 us (3%)
    all_gather x1, waiting for transfers between devices, body(): lax.all_gather(block_t[None], REQ + (HEAD,), axis=0, tiled=True)  74 us
    all_gather x1, waiting for transfers between devices, body(): lax.all_gather(attention, REQ, axis=0, tiled=True)  49.9 us
    ppermute x15, starting transfers between devices, body(): lax.ppermute(rolled[shift], CHIPS, pairs).astype(jnp.float32)  40.1 us
    all_gather x1, waiting for transfers between devices, body(): active_all = lax.all_gather(active_t, HEAD, axis=0, tiled=True)  28.2 us
    reduce_scatter x1, waiting for transfers between devices, body(): lax.psum_scatter(partial_sums, HEAD, scatter_dimension=0, tiled=True)  20.4 us
    ppermute x15, waiting for transfers between devices, body(): lax.ppermute(rolled[shift], CHIPS, pairs).astype(jnp.float32)  17.7 us
    pallas_call x1, Pallas kernels, gate_up(): pl.pallas_call(gate_up_kernel, grid=(chunks // R_PER_STEP,), in_specs=[pl...  17.1 us
    pallas_call x1, Pallas kernels, attend_local(): pl.pallas_call(attention_kernel, grid=(steps,), in_specs=[bound_spec, bou...  13.4 us
  transfers between devices with their start and end apart: 20, of which 8 were waited for; matrix products, arithmetic and copies ran while one was open for 6% of the time, Pallas kernels for 0%

profile of v9, /device:TPU:0, one launch (start us, length us, event | category | flops | bytes accessed | tf_op | source)
XLA Modules:
  0.0 336.5 jit_solution(13733599212984081028)
XLA Ops:
  7.3 0.8 compare_select_fusion.3
  8.1 1.5 gather_fusion.1
  9.6 0.8 fusion.22
  10.3 1.0 reshape.195
  11.3 1.0 reshape.197
  12.4 0.2 multiply_cosine_fusion
  12.6 0.5 subtract_convert_fusion
  13.1 0.3 pad_maximum_fusion
  13.4 0.7 copy.39
  14.1 0.7 copy.40
  14.8 0.1 copy.29
  14.9 0.1 broadcast_in_dim.58.end_ref
  15.0 0.1 reduce
  15.1 0.7 copy.30.start_ref
  15.8 13.4 %shard_map.140 = bf16[64,1280]{1,0:T(8,128)(2,1)} custom-call(s32[64,1]{1,0:T(8,128)} %copy.30.start_ref, s32[64,1]{1,0:T(8,128)} %copy-done.5, bf16[64,1280]{1,0:T(8,128)(2,1)} %bitcast.77, bf16[64,1280]{1,0:T(8,128)(2,1)} %bitcast.76, bf16[64,1280]{1,0:T(8,128)(2,1)} %vn_ref.1, bf16[3536,1280]{1,0:T(8,128)(2,1)} %kp_ref.1, bf16[3536,1280]{1,0:T(8,128)(2,1)} %vp_ref.1), custom_call_target="tpu_custom_call" | custom-call | flops 1158676480 | bytes 18759680 | tf_op jit(solution)/shard_map/pallas_call | solution.py:90
  29.3 0.0 reduce-scatter.2.cloned.1.call-start
  29.4 49.9 %all-gather.6.cloned.1.call-done = bf16[2048,1280]{1,0:T(8,128)(2,1)} async-done(((bf16[64,1280]{1,0:T(8,128)(2,1)}), bf16[2048,1280]{1,0:T(8,128)(2,1)}) %all-gather.6.cloned.1.call-update) | async-done | bytes 5242896 | tf_op jit(solution)/shard_map/all_gather | solution.py:206
  79.3 5.4 %fusion.23 = f32[2048,160]{0,1:T(8,128)} fusion(bf16[2048,1280]{1,0:T(8,128)(2,1)} %all-gather.6.cloned.1.call-done, bf16[1280,160]{0,1:T(8,128)(2,1)S(1)} %copy-done.4), kind=kOutput, calls=%fused_computation.83 | convolution fusion | flops 838860800 | bytes 6963200 | tf_op jit(solution)/shard_map/dot_general | solution.py:205
  84.7 0.0 all-gather.8.cloned.1.call-start
  84.8 0.5 copy.27
  85.3 0.8 compare_and_fusion.1
  86.0 2.0 gather_fusion
  88.0 0.1 copy.28
  88.1 0.1 pad.14.clone
  88.2 20.4 %reduce-scatter.2.cloned.1.call-done = f32[512,160]{0,1:T(8,128)} async-done(((f32[2048,160]{0,1:T(8,128)}), f32[512,160]{0,1:T(8,128)}) %reduce-scatter.2.cloned.1.call-update) | async-done | bytes 327696 | tf_op jit(solution)/shard_map/reduce_scatter | solution.py:210
  108.6 1.1 multiply_reduce_fusion
  109.7 0.8 maximum_maximum_fusion
  110.5 0.0 all-gather.10.cloned.1.call-start
  110.5 1.7 copy.31
  112.3 2.6 copy.33
  114.8 4.4 %multiply_convert_fusion.1 = (bf16[5120,108]{1,0:T(8,128)(2,1)}, bf16[5120,108]{1,0:T(8,128)(2,1)}) fusion(bf16[5120,108]{1,0:T(8,128)(2,1)S(1)} %copy.31, f32[5120]{0:T(1024)S(1)} %convert_element_type.157, bf16[5120,108]{1,0:T(8,128)(2,1)} %copy.33), kind=kLoop, calls=%fused_computation.13 | loop fusion | flops 3317760 | bytes 4444160 | tf_op jit(solution)/shard_map/convert_element_type | solution.py:235
  119.2 1.9 copy.32
  121.1 2.9 copy.34
  124.0 3.4 %fusion.3.w_ref = bf16[32,224,160]{2,1,0:T(8,128)(2,1)} fusion(bf16[32,108,160]{2,1,0:T(8,128)(2,1)} %bitcast.68, bf16[32,108,160]{2,1,0:T(8,128)(2,1)S(1)} %bitcast.67), kind=kLoop, calls=%fused_computation.10 | loop fusion | flops 9175040 | bytes 4505600 | tf_op jit(solution)/shard_map/concatenate | solution.py:239
  127.4 74.0 %all-gather.8.cloned.1.call-done = bf16[22528,512]{1,0:T(8,128)(2,1)} async-done(((bf16[176,512]{1,0:T(8,128)(2,1)}), bf16[22528,512]{1,0:T(8,128)(2,1)}) %all-gather.8.cloned.1.call-update) | async-done | bytes 23068688 | tf_op jit(solution)/shard_map/all_gather | solution.py:227
  201.4 17.1 %shard_map.141 = bf16[108,2048]{1,0:T(8,128)(2,1)} custom-call(bf16[32,4,176,512]{3,2,1,0:T(8,128)(2,1)} %bitcast.66, bf16[32,224,160]{2,1,0:T(8,128)(2,1)} %fusion.3.w_ref), custom_call_target="tpu_custom_call" | custom-call | flops 4697620480 | bytes 25804800 | tf_op jit(solution)/shard_map/pallas_call | solution.py:142
  218.5 28.2 %all-gather.10.cloned.1.call-done = bf16[4,108,2048]{2,1,0:T(8,128)(2,1)} async-done(((bf16[1,108,2048]{2,1,0:T(8,128)(2,1)}), bf16[4,108,2048]{2,1,0:T(8,128)(2,1)}) %all-gather.10.cloned.1.call-update) | async-done | bytes 1769488 | tf_op jit(solution)/shard_map/all_gather | solution.py:241
  246.7 1.6 reshape.229
  248.3 3.2 convolution_convert_fusion
  251.6 2.0 dynamic-slice_bitcast_fusion
  253.5 1.3 copy-done.1
  254.8 5.2 %collective-permute-done = bf16[16,64,1280]{2,1,0:T(8,128)(2,1)} collective-permute-done((bf16[16,64,1280]{2,1,0:T(8,128)(2,1)}, bf16[16,64,1280]{2,1,0:T(8,128)(2,1)}, u32[]{:S(2)}, u32[]{:S(2)}) %collective-permute-start) | collective-permute-done | bytes 2621472 | tf_op jit(solution)/shard_map/ppermute | solution.py:251
  260.0 4.9 %fusion.2 = bf16[16,64,1280]{2,1,0:T(8,128)(2,1)} fusion(bf16[16,64,1280]{2,1,0:T(8,128)(2,1)} %collective-permute-done, bf16[16,2,64,1280]{3,2,1,0:T(8,128)(2,1)} %bitcast.70, s32[]{:T(128)S(6)} %select_n.84), kind=kLoop, calls=%fused_computation.9 | loop fusion | flops 5242880 | bytes 7864324 | tf_op jit(solution)/shard_map/convert_element_type | solution.py:252
  264.9 4.0 %gather_fusion.2 = bf16[16,64,1280]{2,1,0:T(8,128)(2,1)} fusion(bf16[16,64,1280]{2,1,0:T(8,128)(2,1)} %fusion.2, s32[1024]{0:T(1024)S(1)} %pad_clamp_fusion), kind=kCustom, calls=%fused_computation.2 | custom fusion | bytes 5242944 | tf_op jit(solution)/shard_map/jit(_take)/gather | solution.py:255
  268.9 2.1 broadcast_select_fusion
  270.9 0.2 slice_bitcast_fusion.14
  271.2 1.5 collective-permute-start.1
  272.7 5.3 %collective-permute-start.10 = (bf16[64,1280]{1,0:T(8,128)(2,1)S(1)}, bf16[64,1280]{1,0:T(8,128)(2,1)S(1)}, u32[]{:S(2)}, u32[]{:S(2)}) collective-permute-start(bf16[64,1280]{1,0:T(8,128)(2,1)S(1)} %get-tuple-element.14), channel_id=1, source_target_pairs={{0,80},{8,88},{16,96},{24,104},{32,112},{40,120},{48,0},{56,8},{64... | collective-permute-start | bytes 491528 | tf_op jit(solution)/shard_map/ppermute | solution.py:259
  278.0 1.4 collective-permute-start.11
  279.3 1.1 collective-permute-start.12
  280.4 1.7 collective-permute-start.13
  282.2 1.4 collective-permute-start.14
  283.6 2.6 collective-permute-done.10
  286.2 2.6 collective-permute-start.15
  288.8 2.8 collective-permute-start.2
  291.6 10.4 %collective-permute-start.3 = (bf16[64,1280]{1,0:T(8,128)(2,1)S(1)}, bf16[64,1280]{1,0:T(8,128)(2,1)S(1)}, u32[]{:S(2)}, u32[]{:S(2)}) collective-permute-start(bf16[64,1280]{1,0:T(8,128)(2,1)S(1)} %get-tuple-element.21), channel_id=1, source_target_pairs={{0,24},{8,32},{16,40},{24,48},{32,56},{40,64},{48,72},{56,80},{64,... | collective-permute-start | bytes 491528 | tf_op jit(solution)/shard_map/ppermute | solution.py:259
  302.0 0.7 collective-permute-start.4
  302.7 3.5 %collective-permute-start.6 = (bf16[64,1280]{1,0:T(8,128)(2,1)S(1)}, bf16[64,1280]{1,0:T(8,128)(2,1)S(1)}, u32[]{:S(2)}, u32[]{:S(2)}) collective-permute-start(bf16[64,1280]{1,0:T(8,128)(2,1)S(1)} %get-tuple-element.18), channel_id=1, source_target_pairs={{0,48},{8,56},{16,64},{24,72},{32,80},{40,88},{48,96},{56,104},{64... | collective-permute-start | bytes 491528 | tf_op jit(solution)/shard_map/ppermute | solution.py:259
  306.2 2.1 collective-permute-start.7
  308.3 0.8 collective-permute-start.8
  309.1 11.4 %collective-permute-done.4 = bf16[64,1280]{1,0:T(8,128)(2,1)S(1)} collective-permute-done((bf16[64,1280]{1,0:T(8,128)(2,1)S(1)}, bf16[64,1280]{1,0:T(8,128)(2,1)S(1)}, u32[]{:S(2)}, u32[]{:S(2)}) %collective-permute-start.4) | collective-permute-done | bytes 163872 | tf_op jit(solution)/shard_map/ppermute | solution.py:259
  320.5 4.8 %collective-permute-start.9 = (bf16[64,1280]{1,0:T(8,128)(2,1)S(1)}, bf16[64,1280]{1,0:T(8,128)(2,1)S(1)}, u32[]{:S(2)}, u32[]{:S(2)}) collective-permute-start(bf16[64,1280]{1,0:T(8,128)(2,1)S(1)} %get-tuple-element.15), channel_id=1, source_target_pairs={{0,72},{8,80},{16,88},{24,96},{32,104},{40,112},{48,120},{56,0},{6... | collective-permute-start | bytes 491528 | tf_op jit(solution)/shard_map/ppermute | solution.py:259
  325.3 3.6 %collective-permute-done.9 = bf16[64,1280]{1,0:T(8,128)(2,1)S(1)} collective-permute-done((bf16[64,1280]{1,0:T(8,128)(2,1)S(1)}, bf16[64,1280]{1,0:T(8,128)(2,1)S(1)}, u32[]{:S(2)}, u32[]{:S(2)}) %collective-permute-start.9) | collective-permute-done | bytes 163872 | tf_op jit(solution)/shard_map/ppermute | solution.py:259
  328.9 1.0 fusion.18
  (43 shorter events, 0.3 us)
Async XLA Ops:
  7.2 241.2 %copy-start = (bf16[432,1280]{1,0:T(8,128)(2,1)S(1)}, bf16[432,1280]{1,0:T(8,128)(2,1)}, u32[]{:S(2)}) copy-start(bf16[432,1280]{1,0:T(8,128)(2,1)} %param.25) | copy-start | bytes 3317764
  7.2 72.1 %all-gather.6.cloned.1.call-start = ((), (), s32[]{:S(2)}) async-start(), calls=%async_computation.1 | async-start | bytes 5406720 | tf_op jit(solution)/shard_map/all_gather | solution.py:206
  15.0 0.8 copy-start.5
  15.8 63.4 %copy-start.4 = (bf16[1280,160]{0,1:T(8,128)(2,1)S(1)}, bf16[1280,160]{0,1:T(8,128)(2,1)}, u32[]{:S(2)}) copy-start(bf16[1280,160]{0,1:T(8,128)(2,1)} %param.21) | copy-start | bytes 1228804
  29.3 55.5 %copy-start.2 = (bf16[2048,160]{0,1:T(8,128)(2,1)S(1)}, bf16[2048,160]{0,1:T(8,128)(2,1)}, u32[]{:S(2)}) copy-start(bf16[2048,160]{0,1:T(8,128)(2,1)} %param.20) | copy-start | bytes 1966084
  29.3 79.3 %reduce-scatter.2.cloned.1.call-start = ((), (), s32[]{:S(2)}) async-start(), calls=%async_computation.2 | async-start | bytes 1638400 | tf_op jit(solution)/shard_map/reduce_scatter | solution.py:210
  84.7 116.7 %all-gather.8.cloned.1.call-start = ((), (), s32[]{:S(2)}) async-start(), calls=%async_computation.3 | async-start | bytes 23248896 | tf_op jit(solution)/shard_map/all_gather | solution.py:227
  109.6 5.2 %copy-start.3 = (bf16[512,160]{0,1:T(8,128)(2,1)}, bf16[512,160]{0,1:T(8,128)(2,1)S(1)}, u32[]{:S(2)}) copy-start(bf16[512,160]{0,1:T(8,128)(2,1)S(1)} %get-tuple-element.3) | copy-start | bytes 491524
  110.4 4.4 %copy-start.6 = (bf16[5120]{0:T(1024)(128)(2,1)S(1)}, bf16[5120]{0:T(1024)(128)(2,1)}, u32[]{:S(2)}) copy-start(bf16[5120]{0:T(1024)(128)(2,1)} %param.22) | copy-start | bytes 30724
  110.5 136.2 %all-gather.10.cloned.1.call-start = ((), (), s32[]{:S(2)}) async-start(), calls=%async_computation.4 | async-start | bytes 2293760 | tf_op jit(solution)/shard_map/all_gather | solution.py:241
  251.5 3.2 copy-start.1
  254.8 5.3 %collective-permute-start = (bf16[16,64,1280]{2,1,0:T(8,128)(2,1)}, bf16[16,64,1280]{2,1,0:T(8,128)(2,1)}, u32[]{:S(2)}, u32[]{:S(2)}) collective-permute-start(bf16[16,64,1280]{2,1,0:T(8,128)(2,1)} %dynamic-slice_bitcast_fusion), channel_id=1, source_target_pairs={{0,4},{4,0},{1,5},{5,1},{2,6},{6,2},{3,7},{7,3},{8,12},{12,8},{9,1... | collective-permute-start | bytes 7864328 | tf_op jit(solution)/shard_map/ppermute | solution.py:251
  271.2 11.0 %collective-permute-start.1 = (bf16[64,1280]{1,0:T(8,128)(2,1)S(1)}, bf16[64,1280]{1,0:T(8,128)(2,1)S(1)}, u32[]{:S(2)}, u32[]{:S(2)}) collective-permute-start(bf16[64,1280]{1,0:T(8,128)(2,1)S(1)} %get-tuple-element.8), channel_id=1, source_target_pairs={{0,8},{8,16},{16,24},{24,32},{32,40},{40,48},{48,56},{56,64},{64,7... | collective-permute-start | bytes 491528 | tf_op jit(solution)/shard_map/ppermute | solution.py:259
  272.7 13.5 %collective-permute-start.10 = (bf16[64,1280]{1,0:T(8,128)(2,1)S(1)}, bf16[64,1280]{1,0:T(8,128)(2,1)S(1)}, u32[]{:S(2)}, u32[]{:S(2)}) collective-permute-start(bf16[64,1280]{1,0:T(8,128)(2,1)S(1)} %get-tuple-element.14), channel_id=1, source_target_pairs={{0,80},{8,88},{16,96},{24,104},{32,112},{40,120},{48,0},{56,8},{64... | collective-permute-start | bytes 491528 | tf_op jit(solution)/shard_map/ppermute | solution.py:259
  278.0 10.8 %collective-permute-start.11 = (bf16[64,1280]{1,0:T(8,128)(2,1)S(1)}, bf16[64,1280]{1,0:T(8,128)(2,1)S(1)}, u32[]{:S(2)}, u32[]{:S(2)}) collective-permute-start(bf16[64,1280]{1,0:T(8,128)(2,1)S(1)} %get-tuple-element.13), channel_id=1, source_target_pairs={{0,88},{8,96},{16,104},{24,112},{32,120},{40,0},{48,8},{56,16},{64... | collective-permute-start | bytes 491528 | tf_op jit(solution)/shard_map/ppermute | solution.py:259
  279.3 12.3 %collective-permute-start.12 = (bf16[64,1280]{1,0:T(8,128)(2,1)S(1)}, bf16[64,1280]{1,0:T(8,128)(2,1)S(1)}, u32[]{:S(2)}, u32[]{:S(2)}) collective-permute-start(bf16[64,1280]{1,0:T(8,128)(2,1)S(1)} %get-tuple-element.12), channel_id=1, source_target_pairs={{0,96},{8,104},{16,112},{24,120},{32,0},{40,8},{48,16},{56,24},{64... | collective-permute-start | bytes 491528 | tf_op jit(solution)/shard_map/ppermute | solution.py:259
  280.4 21.6 %collective-permute-start.13 = (bf16[64,1280]{1,0:T(8,128)(2,1)S(1)}, bf16[64,1280]{1,0:T(8,128)(2,1)S(1)}, u32[]{:S(2)}, u32[]{:S(2)}) collective-permute-start(bf16[64,1280]{1,0:T(8,128)(2,1)S(1)} %get-tuple-element.11), channel_id=1, source_target_pairs={{0,104},{8,112},{16,120},{24,0},{32,8},{40,16},{48,24},{56,32},{64... | collective-permute-start | bytes 491528 | tf_op jit(solution)/shard_map/ppermute | solution.py:259
  282.2 20.5 %collective-permute-start.14 = (bf16[64,1280]{1,0:T(8,128)(2,1)S(1)}, bf16[64,1280]{1,0:T(8,128)(2,1)S(1)}, u32[]{:S(2)}, u32[]{:S(2)}) collective-permute-start(bf16[64,1280]{1,0:T(8,128)(2,1)S(1)} %get-tuple-element.10), channel_id=1, source_target_pairs={{0,112},{8,120},{16,0},{24,8},{32,16},{40,24},{48,32},{56,40},{64,... | collective-permute-start | bytes 491528 | tf_op jit(solution)/shard_map/ppermute | solution.py:259
  286.2 16.5 %collective-permute-start.15 = (bf16[64,1280]{1,0:T(8,128)(2,1)S(1)}, bf16[64,1280]{1,0:T(8,128)(2,1)S(1)}, u32[]{:S(2)}, u32[]{:S(2)}) collective-permute-start(bf16[64,1280]{1,0:T(8,128)(2,1)S(1)} %get-tuple-element.9), channel_id=1, source_target_pairs={{0,120},{8,0},{16,8},{24,16},{32,24},{40,32},{48,40},{56,48},{64,5... | collective-permute-start | bytes 491528 | tf_op jit(solution)/shard_map/ppermute | solution.py:259
  288.8 17.5 %collective-permute-start.2 = (bf16[64,1280]{1,0:T(8,128)(2,1)S(1)}, bf16[64,1280]{1,0:T(8,128)(2,1)S(1)}, u32[]{:S(2)}, u32[]{:S(2)}) collective-permute-start(bf16[64,1280]{1,0:T(8,128)(2,1)S(1)} %get-tuple-element.22), channel_id=1, source_target_pairs={{0,16},{8,24},{16,32},{24,40},{32,48},{40,56},{48,64},{56,72},{64,... | collective-permute-start | bytes 491528 | tf_op jit(solution)/shard_map/ppermute | solution.py:259
  291.6 16.7 %collective-permute-start.3 = (bf16[64,1280]{1,0:T(8,128)(2,1)S(1)}, bf16[64,1280]{1,0:T(8,128)(2,1)S(1)}, u32[]{:S(2)}, u32[]{:S(2)}) collective-permute-start(bf16[64,1280]{1,0:T(8,128)(2,1)S(1)} %get-tuple-element.21), channel_id=1, source_target_pairs={{0,24},{8,32},{16,40},{24,48},{32,56},{40,64},{48,72},{56,80},{64,... | collective-permute-start | bytes 491528 | tf_op jit(solution)/shard_map/ppermute | solution.py:259
  302.0 18.5 %collective-permute-start.4 = (bf16[64,1280]{1,0:T(8,128)(2,1)S(1)}, bf16[64,1280]{1,0:T(8,128)(2,1)S(1)}, u32[]{:S(2)}, u32[]{:S(2)}) collective-permute-start(bf16[64,1280]{1,0:T(8,128)(2,1)S(1)} %get-tuple-element.20), channel_id=1, source_target_pairs={{0,32},{8,40},{16,48},{24,56},{32,64},{40,72},{48,80},{56,88},{64,... | collective-permute-start | bytes 491528 | tf_op jit(solution)/shard_map/ppermute | solution.py:259
  302.7 22.6 %collective-permute-start.5 = (bf16[64,1280]{1,0:T(8,128)(2,1)S(1)}, bf16[64,1280]{1,0:T(8,128)(2,1)S(1)}, u32[]{:S(2)}, u32[]{:S(2)}) collective-permute-start(bf16[64,1280]{1,0:T(8,128)(2,1)S(1)} %get-tuple-element.19), channel_id=1, source_target_pairs={{0,40},{8,48},{16,56},{24,64},{32,72},{40,80},{48,88},{56,96},{64,... | collective-permute-start | bytes 491528 | tf_op jit(solution)/shard_map/ppermute | solution.py:259
  302.7 22.6 %collective-permute-start.6 = (bf16[64,1280]{1,0:T(8,128)(2,1)S(1)}, bf16[64,1280]{1,0:T(8,128)(2,1)S(1)}, u32[]{:S(2)}, u32[]{:S(2)}) collective-permute-start(bf16[64,1280]{1,0:T(8,128)(2,1)S(1)} %get-tuple-element.18), channel_id=1, source_target_pairs={{0,48},{8,56},{16,64},{24,72},{32,80},{40,88},{48,96},{56,104},{64... | collective-permute-start | bytes 491528 | tf_op jit(solution)/shard_map/ppermute | solution.py:259
  306.2 19.1 %collective-permute-start.7 = (bf16[64,1280]{1,0:T(8,128)(2,1)S(1)}, bf16[64,1280]{1,0:T(8,128)(2,1)S(1)}, u32[]{:S(2)}, u32[]{:S(2)}) collective-permute-start(bf16[64,1280]{1,0:T(8,128)(2,1)S(1)} %get-tuple-element.17), channel_id=1, source_target_pairs={{0,56},{8,64},{16,72},{24,80},{32,88},{40,96},{48,104},{56,112},{6... | collective-permute-start | bytes 491528 | tf_op jit(solution)/shard_map/ppermute | solution.py:259
  308.3 17.0 %collective-permute-start.8 = (bf16[64,1280]{1,0:T(8,128)(2,1)S(1)}, bf16[64,1280]{1,0:T(8,128)(2,1)S(1)}, u32[]{:S(2)}, u32[]{:S(2)}) collective-permute-start(bf16[64,1280]{1,0:T(8,128)(2,1)S(1)} %get-tuple-element.16), channel_id=1, source_target_pairs={{0,64},{8,72},{16,80},{24,88},{32,96},{40,104},{48,112},{56,120},{... | collective-permute-start | bytes 491528 | tf_op jit(solution)/shard_map/ppermute | solution.py:259
  320.5 8.4 %collective-permute-start.9 = (bf16[64,1280]{1,0:T(8,128)(2,1)S(1)}, bf16[64,1280]{1,0:T(8,128)(2,1)S(1)}, u32[]{:S(2)}, u32[]{:S(2)}) collective-permute-start(bf16[64,1280]{1,0:T(8,128)(2,1)S(1)} %get-tuple-element.15), channel_id=1, source_target_pairs={{0,72},{8,80},{16,88},{24,96},{32,104},{40,112},{48,120},{56,0},{6... | collective-permute-start | bytes 491528 | tf_op jit(solution)/shard_map/ppermute | solution.py:259
Sparse Core Ops, SparseCore 0:
  29.4 49.8 all-gather.5
  84.8 23.7 reduce-scatter.1
  111.7 89.5 all-gather.7
  218.6 28.0 all-gather.9

commit v10 on v8

--- a/solution.py
+++ b/solution.py
@@ -27,27 +27,26 @@
     return (jnp.cos(angles), jnp.sin(angles))
 
 
-def rotate_half(vectors, cosine, sine_table):
-    half_dim = HD // 2
-    first_half = vectors[..., :half_dim]
-    second = vectors[..., half_dim:]
-    cos_grid = cosine[:, None, :]
-    sin_grid = sine_table[:, None, :]
-    return jnp.concatenate(
-        [first_half * cos_grid - second * sin_grid, second * cos_grid + first_half * sin_grid],
-        axis=-1,
-    )
-
-
-def attention_kernel(start_ref, end_ref, q_ref, k_ref, vn_ref, kp_ref, vp_ref, o_ref):
+def attention_kernel(
+    start_ref, end_ref, cos_ref, sin_ref, q_ref, k_ref, vn_ref, kp_ref, vp_ref, o_ref
+):
     score_scale = HD ** (-0.5)
+    cosine = cos_ref[...]
+    sine = sin_ref[...]
+
+    def rotated(block):
+        wide = block.astype(jnp.float32)
+        swapped = pltpu.roll(wide, HD // 2, 1)
+        return (wide * cosine + swapped * sine).astype(jnp.bfloat16)
+
     slots = q_ref.shape[0]
     rows = kp_ref.shape[0]
     places = lax.broadcasted_iota(jnp.int32, (slots, rows), 1)
     member = (places >= start_ref[...]) & (places < end_ref[...])
     for j in range(HEADS_PER_STEP):
         cols = slice(j * HD, (j + 1) * HD)
-        query = q_ref[:, cols]
+        query = rotated(q_ref[:, cols])
+        key_rot = rotated(k_ref[:, cols])
         scores = (
             lax.dot_general(
                 query,
@@ -59,7 +58,7 @@
         )
         own_score = (
             jnp.sum(
-                query.astype(jnp.float32) * k_ref[:, cols].astype(jnp.float32),
+                query.astype(jnp.float32) * key_rot.astype(jnp.float32),
                 axis=-1,
                 keepdims=True,
             )
@@ -78,19 +77,30 @@
         o_ref[:, cols] = (summed / row_total).astype(o_ref.dtype)
 
 
-def attend_local(query_rot, key_rot, value_new, key_pool, value_pool, starts, ends):
-    slots, width = query_rot.shape
+def attend_local(query_new, key_new, value_new, key_pool, value_pool, starts, ends, cos2, sin2):
+    slots, width = query_new.shape
     rows = key_pool.shape[0]
     block = HEADS_PER_STEP * HD
     steps = width // block
     slot_spec = pl.BlockSpec((slots, block), lambda g: (0, g))
     pool_spec = pl.BlockSpec((rows, block), lambda g: (0, g))
     bound_spec = pl.BlockSpec((slots, 1), lambda g: (0, 0))
+    table_spec = pl.BlockSpec((slots, HD), lambda g: (0, 0))
     flops = 4 * slots * rows * width
     return pl.pallas_call(
         attention_kernel,
         grid=(steps,),
-        in_specs=[bound_spec, bound_spec, slot_spec, slot_spec, slot_spec, pool_spec, pool_spec],
+        in_specs=[
+            bound_spec,
+            bound_spec,
+            table_spec,
+            table_spec,
+            slot_spec,
+            slot_spec,
+            slot_spec,
+            pool_spec,
+            pool_spec,
+        ],
         out_specs=slot_spec,
         out_shape=jax.ShapeDtypeStruct((slots, width), jnp.bfloat16),
         cost_estimate=pl.CostEstimate(
@@ -98,7 +108,7 @@
             transcendentals=slots * rows * (width // HD),
             bytes_accessed=2 * rows * width * 2 + 4 * slots * width * 2,
         ),
-    )(starts, ends, query_rot, key_rot, value_new, key_pool, value_pool)
+    )(starts, ends, cos2, sin2, query_new, key_new, value_new, key_pool, value_pool)
 
 
 def gate_up_kernel(x_ref, w_ref, o_ref, acc, acc_sq):
@@ -177,30 +187,26 @@
     down_proj,
 ):
     owned = query_new.shape[0]
-    groups = query_new.shape[1] // HD
     req_count = lax.axis_size(REQ)
     head_count = lax.axis_size(HEAD)
     first_slot = lax.axis_index(REQ) * owned
     my_requests = lax.dynamic_slice_in_dim(slot_request, first_slot, owned, 0)
     my_lengths = jnp.take(lengths, my_requests, axis=0)
     cosine, sine_table = rope_tables(my_lengths)
-    shaped = (owned, groups, HD)
-    query_rot = rotate_half(
-        query_new.astype(jnp.float32).reshape(shaped), cosine, sine_table
-    ).astype(jnp.bfloat16)
-    key_rot = rotate_half(key_new.astype(jnp.float32).reshape(shaped), cosine, sine_table).astype(
-        jnp.bfloat16
-    )
+    cos2 = jnp.concatenate([cosine, cosine], axis=1)
+    sin2 = jnp.concatenate([-sine_table, sine_table], axis=1)
     seg_ends = jnp.cumsum(my_lengths)
     starts = (seg_ends - my_lengths).astype(jnp.int32)
     attention = attend_local(
-        query_rot.reshape(owned, groups * HD),
-        key_rot.reshape(owned, groups * HD),
+        query_new,
+        key_new,
         value_new,
         key_pool,
         value_pool,
         starts[:, None],
         seg_ends.astype(jnp.int32)[:, None],
+        cos2,
+        sin2,
     )
     partial_sums = jnp.dot(
         lax.all_gather(attention, REQ, axis=0, tiled=True),

time: 314 us -> 311 us (level)
  local copies, waits for them, and re-layouts: 22.4 us -> 18.9 us
    unnamed x20 -> x18, local copies, waits for them, and re-layouts: 9.16 us -> 7.71 us
  transfers between devices with their start and end apart: 5 -> 5, of which waited for: 5 -> 5; matrix products, arithmetic and copies ran while one was open for 6% -> 7% of each run, Pallas kernels for 0% -> 0%
where the time goes in v10:
time: 311 us; the launch traced here: 310 us
  waiting for transfers between devices  178 us (57%)
  blocking collectives  41.2 us (13%)
  Pallas kernels  30.6 us (10%)
  other arithmetic  19.1 us (6%)
  local copies, waits for them, and re-layouts  18.9 us (6%)
  between operations  13.9 us (4%)
  matrix products  8.63 us (3%)
    all_gather x1, waiting for transfers between devices, body(): lax.all_gather(block_t[None], REQ + (HEAD,), axis=0, tiled=True)  74.1 us
    all_gather x1, waiting for transfers between devices, body(): lax.all_gather(attention, REQ, axis=0, tiled=True)  49.9 us
    all_to_all x1, blocking collectives, body(): received = lax.all_to_all(chip_sums, CHIPS, 0, 0, tiled=True)  41.2 us
    all_gather x1, waiting for transfers between devices, body(): active_all = lax.all_gather(active_t, HEAD, axis=0, tiled=True)  28.2 us
    reduce_scatter x1, waiting for transfers between devices, body(): lax.psum_scatter(partial_sums, HEAD, scatter_dimension=0, tiled=True)  20.4 us
    pallas_call x1, Pallas kernels, gate_up(): pl.pallas_call(gate_up_kernel, grid=(chunks // R_PER_STEP,), in_specs=[pl...  17 us
    pallas_call x1, Pallas kernels, attend_local(): pl.pallas_call(attention_kernel, grid=(steps,), in_specs=[bound_spec, bou...  13.6 us
    unnamed x18, local copies, waits for them, and re-layouts  7.71 us
  transfers between devices with their start and end apart: 5, of which 5 were waited for; matrix products, arithmetic and copies ran while one was open for 7% of the time, Pallas kernels for 0%

profile of v10, /device:TPU:0, one launch (start us, length us, event | category | flops | bytes accessed | tf_op | source)
XLA Modules:
  0.0 310.5 jit_solution(11959422515150128808)
XLA Ops:
  7.2 0.0 copy-start
  7.2 0.0 all-gather.6.cloned.1.call-start
  7.2 0.8 compare_select_fusion.1
  8.1 1.5 gather_fusion.1
  9.6 0.8 fusion.5
  10.3 0.1 copy.29
  10.4 0.1 broadcast_in_dim.44.end_ref
  10.5 0.0 copy-start.5
  10.5 0.1 reduce.1
  10.7 0.7 copy.30.start_ref
  11.4 0.2 fusion.4
  11.6 0.7 pad_maximum_fusion
  12.3 0.0 copy-done.5
  12.3 0.0 copy-start.4
  12.3 13.6 %shard_map.140 = bf16[64,1280]{1,0:T(8,128)(2,1)} custom-call(s32[64,1]{1,0:T(8,128)} %copy.30.start_ref, s32[64,1]{1,0:T(8,128)} %copy-done.5, f32[64,128]{1,0:T(8,128)} %get-tuple-element.13.cos_ref, f32[64,128]{1,0:T(8,128)} %get-tuple-element.14.sin_ref, bf16[64,1280]{1,0:T(8,128)(2,1)} %q_ref.1, bf16[64,1280]{1,0:T(8,128)(2,1)} %k_ref.1, ...), custom_call_target="tpu_custom_call" | custom-call | flops 1158676480 | bytes 18759680 | tf_op jit(solution)/shard_map/pallas_call | solution.py:90
  25.9 0.0 all-gather.6.cloned.1.call-update
  25.9 0.0 copy-start.2
  26.0 0.0 reduce-scatter.2.cloned.1.call-start
  26.0 49.9 %all-gather.6.cloned.1.call-done = bf16[2048,1280]{1,0:T(8,128)(2,1)} async-done(((bf16[64,1280]{1,0:T(8,128)(2,1)}), bf16[2048,1280]{1,0:T(8,128)(2,1)}) %all-gather.6.cloned.1.call-update) | async-done | bytes 5242896 | tf_op jit(solution)/shard_map/all_gather | solution.py:212
  75.9 0.0 copy-done.4
  75.9 5.4 %fusion.6 = f32[2048,160]{0,1:T(8,128)} fusion(bf16[2048,1280]{1,0:T(8,128)(2,1)} %all-gather.6.cloned.1.call-done, bf16[1280,160]{0,1:T(8,128)(2,1)S(1)} %copy-done.4), kind=kOutput, calls=%fused_computation.31 | convolution fusion | flops 838860800 | bytes 6963200 | tf_op jit(solution)/shard_map/dot_general | solution.py:211
  81.4 0.0 reduce-scatter.2.cloned.1.call-update
  81.4 0.0 all-gather.8.cloned.1.call-start
  81.4 0.0 copy-done.2
  81.5 0.5 copy.27
  82.0 0.8 compare_and_fusion
  82.7 2.0 gather_fusion
  84.7 0.1 copy.28
  84.8 0.1 pad.14.clone
  84.9 20.4 %reduce-scatter.2.cloned.1.call-done = f32[512,160]{0,1:T(8,128)} async-done(((f32[2048,160]{0,1:T(8,128)}), f32[512,160]{0,1:T(8,128)}) %reduce-scatter.2.cloned.1.call-update) | async-done | bytes 327696 | tf_op jit(solution)/shard_map/reduce_scatter | solution.py:216
  105.3 1.1 multiply_reduce_fusion
  106.3 0.0 copy-start.3
  106.4 0.8 maximum_maximum_fusion
  107.1 0.0 copy-start.6
  107.1 0.0 all-gather.8.cloned.1.call-update
  107.2 0.0 all-gather.10.cloned.1.call-start
  107.2 1.7 copy.31
  109.0 2.5 copy.33
  111.5 0.0 copy-done.3
  111.5 0.0 copy-done.6
  111.5 4.3 %multiply_convert_fusion.1 = (bf16[5120,108]{1,0:T(8,128)(2,1)}, bf16[5120,108]{1,0:T(8,128)(2,1)}) fusion(bf16[5120,108]{1,0:T(8,128)(2,1)S(1)} %copy.31, f32[5120]{0:T(1024)S(1)} %convert_element_type.91, bf16[5120,108]{1,0:T(8,128)(2,1)} %copy.33), kind=kLoop, calls=%fused_computation.12 | loop fusion | flops 3317760 | bytes 4444160 | tf_op jit(solution)/shard_map/convert_element_type | solution.py:241
  115.8 1.9 copy.32
  117.8 2.9 copy.34
  120.7 3.4 %fusion.3.w_ref = bf16[32,224,160]{2,1,0:T(8,128)(2,1)} fusion(bf16[32,108,160]{2,1,0:T(8,128)(2,1)} %bitcast.23, bf16[32,108,160]{2,1,0:T(8,128)(2,1)S(1)} %bitcast.22), kind=kLoop, calls=%fused_computation.9 | loop fusion | flops 9175040 | bytes 4505600 | tf_op jit(solution)/shard_map/concatenate | solution.py:245
  124.0 74.1 %all-gather.8.cloned.1.call-done = bf16[22528,512]{1,0:T(8,128)(2,1)} async-done(((bf16[176,512]{1,0:T(8,128)(2,1)}), bf16[22528,512]{1,0:T(8,128)(2,1)}) %all-gather.8.cloned.1.call-update) | async-done | bytes 23068688 | tf_op jit(solution)/shard_map/all_gather | solution.py:233
  198.1 17.0 %shard_map.141 = bf16[108,2048]{1,0:T(8,128)(2,1)} custom-call(bf16[32,4,176,512]{3,2,1,0:T(8,128)(2,1)} %bitcast.21, bf16[32,224,160]{2,1,0:T(8,128)(2,1)} %fusion.3.w_ref), custom_call_target="tpu_custom_call" | custom-call | flops 4697620480 | bytes 25804800 | tf_op jit(solution)/shard_map/pallas_call | solution.py:152
  215.1 0.0 all-gather.10.cloned.1.call-update
  215.1 28.2 %all-gather.10.cloned.1.call-done = bf16[4,108,2048]{2,1,0:T(8,128)(2,1)} async-done(((bf16[1,108,2048]{2,1,0:T(8,128)(2,1)}), bf16[4,108,2048]{2,1,0:T(8,128)(2,1)}) %all-gather.10.cloned.1.call-update) | async-done | bytes 1769488 | tf_op jit(solution)/shard_map/all_gather | solution.py:247
  243.4 1.6 reshape.90
  245.0 0.0 copy-done
  245.0 3.2 %convolution_convert_fusion = bf16[2048,1280]{1,0:T(8,128)(2,1)S(1)} fusion(bf16[432,2048]{1,0:T(8,128)(2,1)S(1)} %reshape.90, bf16[432,1280]{1,0:T(8,128)(2,1)S(1)} %copy-done), kind=kOutput, calls=%fused_computation.2 | convolution fusion | flops 2267545600 | bytes 8118272 | tf_op jit(solution)/shard_map/dot_general | solution.py:248
  248.2 0.0 copy-start.1
  248.2 2.0 dynamic-slice_bitcast_fusion
  250.2 1.3 copy-done.1
  251.5 0.0 collective-permute-start
  251.5 5.2 %collective-permute-done = bf16[16,64,1280]{2,1,0:T(8,128)(2,1)} collective-permute-done((bf16[16,64,1280]{2,1,0:T(8,128)(2,1)}, bf16[16,64,1280]{2,1,0:T(8,128)(2,1)}, u32[]{:S(2)}, u32[]{:S(2)}) %collective-permute-start) | collective-permute-done | bytes 2621472 | tf_op jit(solution)/shard_map/ppermute | solution.py:257
  256.7 3.3 %fusion.2 = bf16[16,64,1280]{2,1,0:T(8,128)(2,1)S(1)} fusion(bf16[16,64,1280]{2,1,0:T(8,128)(2,1)} %collective-permute-done, bf16[16,2,64,1280]{3,2,1,0:T(8,128)(2,1)} %bitcast.25, s32[]{:T(128)S(6)} %select_n.44), kind=kLoop, calls=%fused_computation.8 | loop fusion | flops 5242880 | bytes 7864324 | tf_op jit(solution)/shard_map/convert_element_type | solution.py:258
  260.0 41.2 %all_to_all.5 = bf16[16,64,1280]{2,1,0:T(8,128)(2,1)} all-to-all(bf16[16,64,1280]{2,1,0:T(8,128)(2,1)S(1)} %fusion.2), channel_id=1, replica_groups=mesh['chip'=16,'core'=2,'y'=4] {'chip'}, dimensions={0} | all-to-all | bytes 5242880 | tf_op jit(solution)/shard_map/all_to_all | solution.py:259
  301.2 2.8 reduce_sum.25
  (8 shorter events, 0.0 us)
Async XLA Ops:
  7.2 237.8 %copy-start = (bf16[432,1280]{1,0:T(8,128)(2,1)S(1)}, bf16[432,1280]{1,0:T(8,128)(2,1)}, u32[]{:S(2)}) copy-start(bf16[432,1280]{1,0:T(8,128)(2,1)} %param.25) | copy-start | bytes 3317764
  7.2 68.8 %all-gather.6.cloned.1.call-start = ((), (), s32[]{:S(2)}) async-start(), calls=%async_computation.2 | async-start | bytes 5406720 | tf_op jit(solution)/shard_map/all_gather | solution.py:212
  10.5 1.8 copy-start.5
  12.3 63.6 %copy-start.4 = (bf16[1280,160]{0,1:T(8,128)(2,1)S(1)}, bf16[1280,160]{0,1:T(8,128)(2,1)}, u32[]{:S(2)}) copy-start(bf16[1280,160]{0,1:T(8,128)(2,1)} %param.21) | copy-start | bytes 1228804
  25.9 55.5 %copy-start.2 = (bf16[2048,160]{0,1:T(8,128)(2,1)S(1)}, bf16[2048,160]{0,1:T(8,128)(2,1)}, u32[]{:S(2)}) copy-start(bf16[2048,160]{0,1:T(8,128)(2,1)} %param.20) | copy-start | bytes 1966084
  26.0 79.3 %reduce-scatter.2.cloned.1.call-start = ((), (), s32[]{:S(2)}) async-start(), calls=%async_computation.3 | async-start | bytes 1638400 | tf_op jit(solution)/shard_map/reduce_scatter | solution.py:216
  81.4 116.7 %all-gather.8.cloned.1.call-start = ((), (), s32[]{:S(2)}) async-start(), calls=%async_computation.4 | async-start | bytes 23248896 | tf_op jit(solution)/shard_map/all_gather | solution.py:233
  106.3 5.2 %copy-start.3 = (bf16[512,160]{0,1:T(8,128)(2,1)}, bf16[512,160]{0,1:T(8,128)(2,1)S(1)}, u32[]{:S(2)}) copy-start(bf16[512,160]{0,1:T(8,128)(2,1)S(1)} %get-tuple-element.3) | copy-start | bytes 491524
  107.1 4.4 %copy-start.6 = (bf16[5120]{0:T(1024)(128)(2,1)S(1)}, bf16[5120]{0:T(1024)(128)(2,1)}, u32[]{:S(2)}) copy-start(bf16[5120]{0:T(1024)(128)(2,1)} %param.22) | copy-start | bytes 30724
  107.2 136.2 %all-gather.10.cloned.1.call-start = ((), (), s32[]{:S(2)}) async-start(), calls=%async_computation.5 | async-start | bytes 2293760 | tf_op jit(solution)/shard_map/all_gather | solution.py:247
  248.2 3.2 %copy-start.1 = (bf16[2048,1280]{1,0:T(8,128)(2,1)}, bf16[2048,1280]{1,0:T(8,128)(2,1)S(1)}, u32[]{:S(2)}) copy-start(bf16[2048,1280]{1,0:T(8,128)(2,1)S(1)} %convolution_convert_fusion) | copy-start | bytes 15728644
  251.5 5.3 %collective-permute-start = (bf16[16,64,1280]{2,1,0:T(8,128)(2,1)}, bf16[16,64,1280]{2,1,0:T(8,128)(2,1)}, u32[]{:S(2)}, u32[]{:S(2)}) collective-permute-start(bf16[16,64,1280]{2,1,0:T(8,128)(2,1)} %dynamic-slice_bitcast_fusion), channel_id=1, source_target_pairs={{0,4},{4,0},{1,5},{5,1},{2,6},{6,2},{3,7},{7,3},{8,12},{12,8},{9,1... | collective-permute-start | bytes 7864328 | tf_op jit(solution)/shard_map/ppermute | solution.py:257
Sparse Core Ops, SparseCore 0:
  26.1 49.8 all-gather.5
  81.5 23.7 reduce-scatter.1
  108.4 89.6 all-gather.7
  215.3 28.0 all-gather.9

commit v11 on v10

--- a/solution.py
+++ b/solution.py
@@ -213,8 +213,11 @@
         out_proj,
         preferred_element_type=jnp.float32,
     )
-    summed = lax.psum_scatter(partial_sums, HEAD, scatter_dimension=0, tiled=True)
-    quarter = summed.shape[0]
+    quarter = partial_sums.shape[0] // head_count
+    exchanged = lax.all_to_all(
+        partial_sums.reshape(head_count, quarter, partial_sums.shape[1]), HEAD, 0, 0, tiled=True
+    )
+    summed = jnp.sum(exchanged, axis=0)
     quarter_slots = lax.dynamic_slice_in_dim(
         slot_request, lax.axis_index(HEAD) * quarter, quarter, 0
     )

time: 311 us -> 315 us (1.013)
  blocking collectives: 41.2 us -> 0 us
  waiting for transfers between devices: 178 us -> 207 us
  starting transfers between devices: 0.17 us -> 11.3 us
  local copies, waits for them, and re-layouts: 18.9 us -> 23.7 us
    all_to_all x0 -> x2, waiting for transfers between devices: none -> 53.3 us  [the longest x1 39.9 us: body(): received = lax.all_to_all(chip_sums, CHIPS, 0, 0, tiled=True)]
    all_to_all x1 -> x0, blocking collectives: 41.2 us -> none  [body(): received = lax.all_to_all(chip_sums, CHIPS, 0, 0, tiled=True)]
    reduce_scatter x1 -> x0, waiting for transfers between devices: 20.4 us -> none  [body(): lax.psum_scatter(partial_sums, HEAD, scatter_dimension=0, tiled=True)]
    all_to_all x0 -> x2, starting transfers between devices: none -> 11.3 us  [the longest x1 6.99 us: body(): received = lax.all_to_all(chip_sums, CHIPS, 0, 0, tiled=True)]
    all_gather x1, waiting for transfers between devices: 74.1 us -> 70.3 us  [body(): lax.all_gather(block_t[None], REQ + (HEAD,), axis=0, tiled=True)]
    unnamed x18 -> x15, local copies, waits for them, and re-layouts: 7.71 us -> 9.43 us
  transfers between devices with their start and end apart: 5 -> 6, of which waited for: 5 -> 6; matrix products, arithmetic and copies ran while one was open for 7% -> 7% of each run, Pallas kernels for 0% -> 0%
where the time goes in v11:
time: 315 us
  waiting for transfers between devices  207 us (66%)
  Pallas kernels  30.6 us (10%)
  local copies, waits for them, and re-layouts  23.7 us (8%)
  other arithmetic  20.5 us (7%)
  between operations  13.9 us (4%)
  starting transfers between devices  11.3 us (4%)
  matrix products  7.53 us (2%)
    all_gather x1, waiting for transfers between devices, body(): lax.all_gather(block_t[None], REQ + (HEAD,), axis=0, tiled=True)  70.3 us
    all_gather x1, waiting for transfers between devices, body(): lax.all_gather(attention, REQ, axis=0, tiled=True)  50 us
    all_to_all x1, waiting for transfers between devices, body(): received = lax.all_to_all(chip_sums, CHIPS, 0, 0, tiled=True)  39.9 us
    all_gather x1, waiting for transfers between devices, body(): active_all = lax.all_gather(active_t, HEAD, axis=0, tiled=True)  28.2 us
    pallas_call x1, Pallas kernels, gate_up(): pl.pallas_call(gate_up_kernel, grid=(chunks // R_PER_STEP,), in_specs=[pl...  17 us
    pallas_call x1, Pallas kernels, attend_local(): pl.pallas_call(attention_kernel, grid=(steps,), in_specs=[bound_spec, bou...  13.6 us
    all_to_all x1, waiting for transfers between devices, body(): lax.all_to_all(partial_sums.reshape(head_count, quarter, partial_sums.sha...  13.4 us
    unnamed x15, local copies, waits for them, and re-layouts  9.43 us
  transfers between devices with their start and end apart: 6, of which 6 were waited for; matrix products, arithmetic and copies ran while one was open for 7% of the time, Pallas kernels for 0%

profile of v11, /device:TPU:0, one launch (start us, length us, event | category | flops | bytes accessed | tf_op | source)
XLA Modules:
  0.0 314.8 jit_solution(13076926647027057849)
XLA Ops:
  7.2 0.0 copy-start
  7.2 0.0 all-gather.6.cloned.1.call-start
  7.2 0.8 compare_select_fusion.1
  8.1 1.5 gather_fusion.1
  9.6 0.8 fusion.5
  10.3 0.1 copy.46
  10.4 0.1 broadcast_in_dim.44.end_ref
  10.5 0.0 copy-start.3
  10.5 0.1 reduce.1
  10.7 0.7 copy.47.start_ref
  11.4 0.2 fusion.4
  11.6 0.7 pad_maximum_fusion
  12.3 0.0 copy-done.3
  12.3 0.0 copy-start.2
  12.3 13.6 %shard_map.140 = bf16[64,1280]{1,0:T(8,128)(2,1)} custom-call(s32[64,1]{1,0:T(8,128)} %copy.47.start_ref, s32[64,1]{1,0:T(8,128)} %copy-done.3, f32[64,128]{1,0:T(8,128)} %get-tuple-element.21.cos_ref, f32[64,128]{1,0:T(8,128)} %get-tuple-element.22.sin_ref, bf16[64,1280]{1,0:T(8,128)(2,1)} %q_ref.1, bf16[64,1280]{1,0:T(8,128)(2,1)} %k_ref.1, ...), custom_call_target="tpu_custom_call" | custom-call | flops 1158676480 | bytes 18759680 | tf_op jit(solution)/shard_map/pallas_call | solution.py:90
  25.9 0.0 all-gather.6.cloned.1.call-update
  25.9 50.0 %all-gather.6.cloned.1.call-done = bf16[2048,1280]{1,0:T(8,128)(2,1)} async-done(((bf16[64,1280]{1,0:T(8,128)(2,1)}), bf16[2048,1280]{1,0:T(8,128)(2,1)}) %all-gather.6.cloned.1.call-update) | async-done | bytes 5242896 | tf_op jit(solution)/shard_map/all_gather | solution.py:212
  75.9 0.0 copy-done.2
  75.9 4.3 %fusion.6 = f32[2048,160]{0,1:T(8,128)S(1)} fusion(bf16[2048,1280]{1,0:T(8,128)(2,1)} %all-gather.6.cloned.1.call-done, bf16[1280,160]{0,1:T(8,128)(2,1)S(1)} %copy-done.2), kind=kOutput, calls=%fused_computation.32 | convolution fusion | flops 838860800 | bytes 6963200 | tf_op jit(solution)/shard_map/dot_general | solution.py:211
  80.3 1.2 copy.62
  81.5 4.3 %all-to-all-start = ((f32[4,512,160]{1,2,0:T(8,128)}), f32[4,512,160]{1,2,0:T(8,128)S(1)}, u32[]{:S(2)}, u32[]{:S(2)}) async-start(f32[4,512,160]{1,2,0:T(8,128)} %bitcast.30), calls=%async_computation | async-start | bytes 2621440 | tf_op jit(solution)/shard_map/all_to_all | solution.py:217
  85.8 0.0 all-gather.8.cloned.1.call-start
  85.8 1.4 copy.45
  87.2 0.8 compare_and_fusion
  87.9 2.6 gather_fusion
  90.5 0.1 pad.14.clone
  90.6 13.4 %all-to-all-done = f32[4,512,160]{1,2,0:T(8,128)S(1)} async-done(((f32[4,512,160]{1,2,0:T(8,128)}), f32[4,512,160]{1,2,0:T(8,128)S(1)}, u32[]{:S(2)}, u32[]{:S(2)}) %all-to-all-start) | async-done | bytes 1310752 | tf_op jit(solution)/shard_map/all_to_all | solution.py:217
  104.1 0.1 reduce_sum.32
  104.2 0.2 copy.50
  104.4 0.0 copy-start.4
  104.4 1.2 multiply_reduce_fusion
  105.6 0.2 copy.52
  105.8 0.2 copy.51
  106.0 0.2 maximum_maximum_fusion
  106.2 0.8 copy.53
  107.0 0.0 all-gather.8.cloned.1.call-update
  107.0 0.0 all-gather.10.cloned.1.call-start
  107.0 1.7 copy.54
  108.8 0.0 copy-done.4
  108.8 2.5 copy.56
  111.4 4.4 %multiply_convert_fusion.1 = (bf16[5120,108]{1,0:T(8,128)(2,1)}, bf16[5120,108]{1,0:T(8,128)(2,1)}) fusion(bf16[5120,108]{1,0:T(8,128)(2,1)S(1)} %copy.54, f32[5120]{0:T(1024)S(1)} %convert_element_type.98, bf16[5120,108]{1,0:T(8,128)(2,1)} %copy.56), kind=kLoop, calls=%fused_computation.12 | loop fusion | flops 3317760 | bytes 4444160 | tf_op jit(solution)/shard_map/convert_element_type | solution.py:244
  115.8 1.9 copy.57
  117.7 2.9 copy.55
  120.6 3.4 %fusion.3.w_ref = bf16[32,224,160]{2,1,0:T(8,128)(2,1)} fusion(bf16[32,108,160]{2,1,0:T(8,128)(2,1)S(1)} %bitcast.26, bf16[32,108,160]{2,1,0:T(8,128)(2,1)} %bitcast.27), kind=kLoop, calls=%fused_computation.9 | loop fusion | flops 9175040 | bytes 4505600 | tf_op jit(solution)/shard_map/concatenate | solution.py:248
  123.9 70.3 %all-gather.8.cloned.1.call-done = bf16[22528,512]{1,0:T(8,128)(2,1)} async-done(((bf16[176,512]{1,0:T(8,128)(2,1)}), bf16[22528,512]{1,0:T(8,128)(2,1)}) %all-gather.8.cloned.1.call-update) | async-done | bytes 23068688 | tf_op jit(solution)/shard_map/all_gather | solution.py:236
  194.3 17.0 %shard_map.141 = bf16[108,2048]{1,0:T(8,128)(2,1)} custom-call(bf16[32,4,176,512]{3,2,1,0:T(8,128)(2,1)} %bitcast.25, bf16[32,224,160]{2,1,0:T(8,128)(2,1)} %fusion.3.w_ref), custom_call_target="tpu_custom_call" | custom-call | flops 4697620480 | bytes 25804800 | tf_op jit(solution)/shard_map/pallas_call | solution.py:152
  211.3 0.0 all-gather.10.cloned.1.call-update
  211.3 28.2 %all-gather.10.cloned.1.call-done = bf16[4,108,2048]{2,1,0:T(8,128)(2,1)} async-done(((bf16[1,108,2048]{2,1,0:T(8,128)(2,1)}), bf16[4,108,2048]{2,1,0:T(8,128)(2,1)}) %all-gather.10.cloned.1.call-update) | async-done | bytes 1769488 | tf_op jit(solution)/shard_map/all_gather | solution.py:250
  239.6 1.6 reshape.94
  241.2 0.0 copy-done
  241.2 3.2 %convolution_convert_fusion = bf16[2048,1280]{1,0:T(8,128)(2,1)S(1)} fusion(bf16[432,2048]{1,0:T(8,128)(2,1)S(1)} %reshape.94, bf16[432,1280]{1,0:T(8,128)(2,1)S(1)} %copy-done), kind=kOutput, calls=%fused_computation.2 | convolution fusion | flops 2267545600 | bytes 8118272 | tf_op jit(solution)/shard_map/dot_general | solution.py:251
  244.4 0.0 copy-start.1
  244.4 1.9 dynamic-slice_bitcast_fusion
  246.4 1.3 copy-done.1
  247.7 0.0 collective-permute-start
  247.7 5.2 %collective-permute-done = bf16[16,64,1280]{2,1,0:T(8,128)(2,1)} collective-permute-done((bf16[16,64,1280]{2,1,0:T(8,128)(2,1)}, bf16[16,64,1280]{2,1,0:T(8,128)(2,1)}, u32[]{:S(2)}, u32[]{:S(2)}) %collective-permute-start) | collective-permute-done | bytes 2621472 | tf_op jit(solution)/shard_map/ppermute | solution.py:260
  252.9 4.8 %fusion.2 = bf16[16,64,1280]{2,1,0:T(8,128)(2,1)} fusion(bf16[16,64,1280]{2,1,0:T(8,128)(2,1)} %collective-permute-done, bf16[16,2,64,1280]{3,2,1,0:T(8,128)(2,1)} %bitcast.29, s32[]{:T(128)S(6)} %select_n.46), kind=kLoop, calls=%fused_computation.8 | loop fusion | flops 5242880 | bytes 7864324 | tf_op jit(solution)/shard_map/convert_element_type | solution.py:261
  257.8 7.0 %all-to-all-start.1 = ((bf16[16,64,1280]{2,1,0:T(8,128)(2,1)}), bf16[16,64,1280]{2,1,0:T(8,128)(2,1)}, u32[]{:S(2)}, u32[]{:S(2)}) async-start(bf16[16,64,1280]{2,1,0:T(8,128)(2,1)} %fusion.2), calls=%async_computation.1 | async-start | bytes 5242880 | tf_op jit(solution)/shard_map/all_to_all | solution.py:262
  264.8 0.8 copy.58
  265.5 39.9 %all-to-all-done.1 = bf16[16,64,1280]{2,1,0:T(8,128)(2,1)} async-done(((bf16[16,64,1280]{2,1,0:T(8,128)(2,1)}), bf16[16,64,1280]{2,1,0:T(8,128)(2,1)}, u32[]{:S(2)}, u32[]{:S(2)}) %all-to-all-start.1) | async-done | bytes 2621472 | tf_op jit(solution)/shard_map/all_to_all | solution.py:262
  305.4 2.8 reduce_sum.35
  (8 shorter events, 0.0 us)
Async XLA Ops:
  7.2 234.0 %copy-start = (bf16[432,1280]{1,0:T(8,128)(2,1)S(1)}, bf16[432,1280]{1,0:T(8,128)(2,1)}, u32[]{:S(2)}) copy-start(bf16[432,1280]{1,0:T(8,128)(2,1)} %param.25) | copy-start | bytes 3317764
  7.2 68.7 %all-gather.6.cloned.1.call-start = ((), (), s32[]{:S(2)}) async-start(), calls=%async_computation.2 | async-start | bytes 5406720 | tf_op jit(solution)/shard_map/all_gather | solution.py:212
  10.5 1.8 copy-start.3
  12.3 63.6 %copy-start.2 = (bf16[1280,160]{0,1:T(8,128)(2,1)S(1)}, bf16[1280,160]{0,1:T(8,128)(2,1)}, u32[]{:S(2)}) copy-start(bf16[1280,160]{0,1:T(8,128)(2,1)} %param.21) | copy-start | bytes 1228804
  81.5 22.6 %all-to-all-start = ((f32[4,512,160]{1,2,0:T(8,128)}), f32[4,512,160]{1,2,0:T(8,128)S(1)}, u32[]{:S(2)}, u32[]{:S(2)}) async-start(f32[4,512,160]{1,2,0:T(8,128)} %bitcast.30), calls=%async_computation | async-start | bytes 2621440 | tf_op jit(solution)/shard_map/all_to_all | solution.py:217
  85.8 108.5 %all-gather.8.cloned.1.call-start = ((), (), s32[]{:S(2)}) async-start(), calls=%async_computation.3 | async-start | bytes 23248896 | tf_op jit(solution)/shard_map/all_gather | solution.py:236
  104.4 4.4 %copy-start.4 = (bf16[5120]{0:T(1024)(128)(2,1)S(1)}, bf16[5120]{0:T(1024)(128)(2,1)}, u32[]{:S(2)}) copy-start(bf16[5120]{0:T(1024)(128)(2,1)} %param.22) | copy-start | bytes 30724
  107.0 132.6 %all-gather.10.cloned.1.call-start = ((), (), s32[]{:S(2)}) async-start(), calls=%async_computation.4 | async-start | bytes 2293760 | tf_op jit(solution)/shard_map/all_gather | solution.py:250
  244.4 3.2 %copy-start.1 = (bf16[2048,1280]{1,0:T(8,128)(2,1)}, bf16[2048,1280]{1,0:T(8,128)(2,1)S(1)}, u32[]{:S(2)}) copy-start(bf16[2048,1280]{1,0:T(8,128)(2,1)S(1)} %convolution_convert_fusion) | copy-start | bytes 15728644
  247.7 5.3 %collective-permute-start = (bf16[16,64,1280]{2,1,0:T(8,128)(2,1)}, bf16[16,64,1280]{2,1,0:T(8,128)(2,1)}, u32[]{:S(2)}, u32[]{:S(2)}) collective-permute-start(bf16[16,64,1280]{2,1,0:T(8,128)(2,1)} %dynamic-slice_bitcast_fusion), channel_id=1, source_target_pairs={{0,4},{4,0},{1,5},{5,1},{2,6},{6,2},{3,7},{7,3},{8,12},{12,8},{9,1... | collective-permute-start | bytes 7864328 | tf_op jit(solution)/shard_map/ppermute | solution.py:260
  257.8 47.7 %all-to-all-start.1 = ((bf16[16,64,1280]{2,1,0:T(8,128)(2,1)}), bf16[16,64,1280]{2,1,0:T(8,128)(2,1)}, u32[]{:S(2)}, u32[]{:S(2)}) async-start(bf16[16,64,1280]{2,1,0:T(8,128)(2,1)} %fusion.2), calls=%async_computation.1 | async-start | bytes 5242880 | tf_op jit(solution)/shard_map/all_to_all | solution.py:262
Sparse Core Ops, SparseCore 0:
  26.1 49.8 all-gather.5
  107.1 87.1 all-gather.7
  211.4 28.0 all-gather.9

commit v12 on v10

--- a/solution.py
+++ b/solution.py
@@ -245,16 +245,25 @@
     weights_t = jnp.concatenate([prepared(gate_proj), prepared(up_proj)], axis=1)
     active_t = gate_up(hidden_t, weights_t, col_block)
     active_all = lax.all_gather(active_t, HEAD, axis=0, tiled=True)
-    down_sums = lax.dot_general(
-        active_all, down_proj, (((0,), (0,)), ((), ())), preferred_element_type=jnp.float32
-    )
     cores = lax.axis_size(CORE)
     chips = req_count // cores
-    pieces = down_sums.astype(jnp.bfloat16).reshape(chips, cores, owned, down_sums.shape[1])
+    units_all = active_all.shape[0]
+    by_core = active_all.reshape(units_all, chips, cores, owned)
     my_core = lax.axis_index(CORE)
-    kept = lax.dynamic_index_in_dim(pieces, my_core, axis=1, keepdims=False)
-    sent = lax.dynamic_index_in_dim(pieces, cores - 1 - my_core, axis=1, keepdims=False)
+
+    def down_for(core):
+        columns = lax.dynamic_index_in_dim(by_core, core, axis=2, keepdims=False)
+        sums = lax.dot_general(
+            columns.reshape(units_all, chips * owned),
+            down_proj,
+            (((0,), (0,)), ((), ())),
+            preferred_element_type=jnp.float32,
+        )
+        return sums.astype(jnp.bfloat16).reshape(chips, owned, sums.shape[1])
+
+    sent = down_for(cores - 1 - my_core)
     arrived = lax.ppermute(sent, CORE, [(core, cores - 1 - core) for core in range(cores)])
+    kept = down_for(my_core)
     chip_sums = (kept.astype(jnp.float32) + arrived.astype(jnp.float32)).astype(jnp.bfloat16)
     received = lax.all_to_all(chip_sums, CHIPS, 0, 0, tiled=True)
     ffn_out = jnp.sum(received.astype(jnp.float32), axis=0).astype(jnp.bfloat16)

time: 311 us -> 310 us (level)
    all_gather x0 -> x1, local copies, waits for them, and re-layouts: none -> 4.23 us  [body(): active_all = lax.all_gather(active_t, HEAD, axis=0, tiled=True)]
    reshape x0 -> x1, local copies, waits for them, and re-layouts: none -> 3.3 us  [body(): by_core = active_all.reshape(units_all, chips, cores, owned)]
    unnamed x18 -> x15, local copies, waits for them, and re-layouts: 7.71 us -> 4.8 us
where the time goes in v12:
time: 310 us; the launch traced here: 309 us
  waiting for transfers between devices  176 us (57%)
  blocking collectives  41.2 us (13%)
  Pallas kernels  30.6 us (10%)
  local copies, waits for them, and re-layouts  21.8 us (7%)
  other arithmetic  16.6 us (5%)
  between operations  14 us (5%)
  matrix products  8.47 us (3%)
    all_gather x1, waiting for transfers between devices, body(): lax.all_gather(block_t[None], REQ + (HEAD,), axis=0, tiled=True)  74.1 us
    all_gather x1, waiting for transfers between devices, body(): lax.all_gather(attention, REQ, axis=0, tiled=True)  49.9 us
    all_to_all x1, blocking collectives, body(): received = lax.all_to_all(chip_sums, CHIPS, 0, 0, tiled=True)  41.2 us
    all_gather x1, waiting for transfers between devices, body(): active_all = lax.all_gather(active_t, HEAD, axis=0, tiled=True)  28.2 us
    reduce_scatter x1, waiting for transfers between devices, body(): lax.psum_scatter(partial_sums, HEAD, scatter_dimension=0, tiled=True)  20.4 us
    pallas_call x1, Pallas kernels, gate_up(): pl.pallas_call(gate_up_kernel, grid=(chunks // R_PER_STEP,), in_specs=[pl...  17 us
    pallas_call x1, Pallas kernels, attend_local(): pl.pallas_call(attention_kernel, grid=(steps,), in_specs=[bound_spec, bou...  13.6 us
  transfers between devices with their start and end apart: 5, of which 5 were waited for; matrix products, arithmetic and copies ran while one was open for 7% of the time, Pallas kernels for 0%

profile of v12, /device:TPU:0, one launch (start us, length us, event | category | flops | bytes accessed | tf_op | source)
XLA Modules:
  0.0 309.1 jit_solution(11391332107265503209)
XLA Ops:
  7.2 0.0 copy-start
  7.2 0.0 all-gather.6.cloned.1.call-start
  7.2 0.8 compare_select_fusion.1
  8.1 1.5 gather_fusion.1
  9.6 0.8 fusion.5
  10.3 0.1 copy.30
  10.4 0.1 broadcast_in_dim.44.end_ref
  10.5 0.0 copy-start.4
  10.5 0.1 reduce.1
  10.7 0.7 copy.31.start_ref
  11.4 0.2 fusion.4
  11.6 0.7 pad_maximum_fusion
  12.3 0.0 copy-done.4
  12.3 0.0 copy-start.3
  12.3 13.6 %shard_map.140 = bf16[64,1280]{1,0:T(8,128)(2,1)} custom-call(s32[64,1]{1,0:T(8,128)} %copy.31.start_ref, s32[64,1]{1,0:T(8,128)} %copy-done.4, f32[64,128]{1,0:T(8,128)} %get-tuple-element.15.cos_ref, f32[64,128]{1,0:T(8,128)} %get-tuple-element.16.sin_ref, bf16[64,1280]{1,0:T(8,128)(2,1)} %q_ref.1, bf16[64,1280]{1,0:T(8,128)(2,1)} %k_ref.1, ...), custom_call_target="tpu_custom_call" | custom-call | flops 1158676480 | bytes 18759680 | tf_op jit(solution)/shard_map/pallas_call | solution.py:90
  25.9 0.0 all-gather.6.cloned.1.call-update
  25.9 0.0 copy-start.1
  26.0 0.0 reduce-scatter.2.cloned.1.call-start
  26.0 49.9 %all-gather.6.cloned.1.call-done = bf16[2048,1280]{1,0:T(8,128)(2,1)} async-done(((bf16[64,1280]{1,0:T(8,128)(2,1)}), bf16[2048,1280]{1,0:T(8,128)(2,1)}) %all-gather.6.cloned.1.call-update) | async-done | bytes 5242896 | tf_op jit(solution)/shard_map/all_gather | solution.py:212
  75.9 0.0 copy-done.3
  75.9 5.4 %fusion.6 = f32[2048,160]{0,1:T(8,128)} fusion(bf16[2048,1280]{1,0:T(8,128)(2,1)} %all-gather.6.cloned.1.call-done, bf16[1280,160]{0,1:T(8,128)(2,1)S(1)} %copy-done.3), kind=kOutput, calls=%fused_computation.33 | convolution fusion | flops 838860800 | bytes 6963200 | tf_op jit(solution)/shard_map/dot_general | solution.py:211
  81.4 0.0 reduce-scatter.2.cloned.1.call-update
  81.4 0.0 all-gather.8.cloned.1.call-start
  81.4 0.0 copy-done.1
  81.5 0.5 copy.28
  82.0 0.8 compare_and_fusion
  82.7 2.0 gather_fusion
  84.7 0.1 copy.29
  84.8 0.1 pad.14.clone
  84.9 20.4 %reduce-scatter.2.cloned.1.call-done = f32[512,160]{0,1:T(8,128)} async-done(((f32[2048,160]{0,1:T(8,128)}), f32[512,160]{0,1:T(8,128)}) %reduce-scatter.2.cloned.1.call-update) | async-done | bytes 327696 | tf_op jit(solution)/shard_map/reduce_scatter | solution.py:216
  105.3 1.1 multiply_reduce_fusion
  106.3 0.0 copy-start.2
  106.4 0.8 maximum_maximum_fusion
  107.1 0.0 copy-start.5
  107.1 0.0 all-gather.8.cloned.1.call-update
  107.2 0.0 all-gather.10.cloned.1.call-start
  107.2 1.7 copy.32
  109.0 2.5 copy.34
  111.5 0.0 copy-done.2
  111.5 0.0 copy-done.5
  111.5 4.3 %multiply_convert_fusion.1 = (bf16[5120,108]{1,0:T(8,128)(2,1)}, bf16[5120,108]{1,0:T(8,128)(2,1)}) fusion(bf16[5120,108]{1,0:T(8,128)(2,1)S(1)} %copy.32, f32[5120]{0:T(1024)S(1)} %convert_element_type.94, bf16[5120,108]{1,0:T(8,128)(2,1)} %copy.34), kind=kLoop, calls=%fused_computation.12 | loop fusion | flops 3317760 | bytes 4444160 | tf_op jit(solution)/shard_map/convert_element_type | solution.py:241
  115.8 1.9 copy.33
  117.8 2.9 copy.35
  120.6 3.4 %fusion.3.w_ref = bf16[32,224,160]{2,1,0:T(8,128)(2,1)} fusion(bf16[32,108,160]{2,1,0:T(8,128)(2,1)} %bitcast.26, bf16[32,108,160]{2,1,0:T(8,128)(2,1)S(1)} %bitcast.25), kind=kLoop, calls=%fused_computation.10 | loop fusion | flops 9175040 | bytes 4505600 | tf_op jit(solution)/shard_map/concatenate | solution.py:245
  124.0 74.1 %all-gather.8.cloned.1.call-done = bf16[22528,512]{1,0:T(8,128)(2,1)} async-done(((bf16[176,512]{1,0:T(8,128)(2,1)}), bf16[22528,512]{1,0:T(8,128)(2,1)}) %all-gather.8.cloned.1.call-update) | async-done | bytes 23068688 | tf_op jit(solution)/shard_map/all_gather | solution.py:233
  198.1 17.0 %shard_map.141 = bf16[108,2048]{1,0:T(8,128)(2,1)} custom-call(bf16[32,4,176,512]{3,2,1,0:T(8,128)(2,1)} %bitcast.24, bf16[32,224,160]{2,1,0:T(8,128)(2,1)} %fusion.3.w_ref), custom_call_target="tpu_custom_call" | custom-call | flops 4697620480 | bytes 25804800 | tf_op jit(solution)/shard_map/pallas_call | solution.py:152
  215.1 0.0 all-gather.10.cloned.1.call-update
  215.1 28.2 %all-gather.10.cloned.1.call-done = bf16[4,108,2048]{2,1,0:T(8,128)(2,1)} async-done(((bf16[1,108,2048]{2,1,0:T(8,128)(2,1)}), bf16[4,108,2048]{2,1,0:T(8,128)(2,1)}) %all-gather.10.cloned.1.call-update) | async-done | bytes 1769488 | tf_op jit(solution)/shard_map/all_gather | solution.py:247
  243.4 4.2 %copy.36 = bf16[4,108,2048]{1,0,2:T(4,128)(2,1)} copy(bf16[4,108,2048]{2,1,0:T(8,128)(2,1)} %all-gather.10.cloned.1.call-done) | data formatting | bytes 3538944 | tf_op jit(solution)/shard_map/all_gather | solution.py:247
  247.6 3.3 %reshape.79 = bf16[432,16,2,64]{0,3,2,1:T(8,128)(2,1)S(1)} reshape(bf16[4,108,2048]{1,0,2:T(4,128)(2,1)} %copy.36) | data formatting | bytes 3538944 | tf_op jit(solution)/shard_map/reshape | solution.py:251
  250.9 0.2 constant_dynamic-slice_fusion
  251.1 0.0 copy-done
  251.1 1.5 convolution_convert_fusion
  252.7 0.3 collective-permute-start
  252.9 1.5 convolution_convert_fusion.1
  254.5 3.4 %collective-permute-done = bf16[16,64,1280]{2,1,0:T(8,128)(2,1)S(1)} collective-permute-done((bf16[16,64,1280]{2,1,0:T(8,128)(2,1)S(1)}, bf16[16,64,1280]{2,1,0:T(8,128)(2,1)S(1)}, u32[]{:S(2)}, u32[]{:S(2)}) %collective-permute-start) | collective-permute-done | bytes 2621472 | tf_op jit(solution)/shard_map/ppermute | solution.py:265
  257.8 0.8 fusion.2
  258.7 41.2 %all_to_all.5 = bf16[16,64,1280]{2,1,0:T(8,128)(2,1)} all-to-all(bf16[16,64,1280]{2,1,0:T(8,128)(2,1)S(1)} %fusion.2), channel_id=1, replica_groups=mesh['chip'=16,'core'=2,'y'=4] {'chip'}, dimensions={0} | all-to-all | bytes 5242880 | tf_op jit(solution)/shard_map/all_to_all | solution.py:268
  299.8 2.8 reduce_sum.25
  (8 shorter events, 0.0 us)
Async XLA Ops:
  7.2 244.0 %copy-start = (bf16[432,1280]{1,0:T(8,128)(2,1)S(1)}, bf16[432,1280]{1,0:T(8,128)(2,1)}, u32[]{:S(2)}) copy-start(bf16[432,1280]{1,0:T(8,128)(2,1)} %param.25) | copy-start | bytes 3317764
  7.2 68.8 %all-gather.6.cloned.1.call-start = ((), (), s32[]{:S(2)}) async-start(), calls=%async_computation.2 | async-start | bytes 5406720 | tf_op jit(solution)/shard_map/all_gather | solution.py:212
  10.5 1.8 copy-start.4
  12.3 63.6 %copy-start.3 = (bf16[1280,160]{0,1:T(8,128)(2,1)S(1)}, bf16[1280,160]{0,1:T(8,128)(2,1)}, u32[]{:S(2)}) copy-start(bf16[1280,160]{0,1:T(8,128)(2,1)} %param.21) | copy-start | bytes 1228804
  25.9 55.5 %copy-start.1 = (bf16[2048,160]{0,1:T(8,128)(2,1)S(1)}, bf16[2048,160]{0,1:T(8,128)(2,1)}, u32[]{:S(2)}) copy-start(bf16[2048,160]{0,1:T(8,128)(2,1)} %param.20) | copy-start | bytes 1966084
  26.0 79.3 %reduce-scatter.2.cloned.1.call-start = ((), (), s32[]{:S(2)}) async-start(), calls=%async_computation.3 | async-start | bytes 1638400 | tf_op jit(solution)/shard_map/reduce_scatter | solution.py:216
  81.4 116.7 %all-gather.8.cloned.1.call-start = ((), (), s32[]{:S(2)}) async-start(), calls=%async_computation.4 | async-start | bytes 23248896 | tf_op jit(solution)/shard_map/all_gather | solution.py:233
  106.3 5.2 %copy-start.2 = (bf16[512,160]{0,1:T(8,128)(2,1)}, bf16[512,160]{0,1:T(8,128)(2,1)S(1)}, u32[]{:S(2)}) copy-start(bf16[512,160]{0,1:T(8,128)(2,1)S(1)} %get-tuple-element.3) | copy-start | bytes 491524
  107.1 4.4 %copy-start.5 = (bf16[5120]{0:T(1024)(128)(2,1)S(1)}, bf16[5120]{0:T(1024)(128)(2,1)}, u32[]{:S(2)}) copy-start(bf16[5120]{0:T(1024)(128)(2,1)} %param.22) | copy-start | bytes 30724
  107.2 136.2 %all-gather.10.cloned.1.call-start = ((), (), s32[]{:S(2)}) async-start(), calls=%async_computation.5 | async-start | bytes 2293760 | tf_op jit(solution)/shard_map/all_gather | solution.py:247
  252.7 5.2 %collective-permute-start = (bf16[16,64,1280]{2,1,0:T(8,128)(2,1)S(1)}, bf16[16,64,1280]{2,1,0:T(8,128)(2,1)S(1)}, u32[]{:S(2)}, u32[]{:S(2)}) collective-permute-start(bf16[16,64,1280]{2,1,0:T(8,128)(2,1)S(1)} %bitcast.37), channel_id=1, source_target_pairs={{0,4},{4,0},{1,5},{5,1},{2,6},{6,2},{3,7},{7,3},{8,12},{12,8},{9,1... | collective-permute-start | bytes 7864328 | tf_op jit(solution)/shard_map/ppermute | solution.py:265
Sparse Core Ops, SparseCore 0:
  26.1 49.8 all-gather.5
  81.5 23.7 reduce-scatter.1
  108.4 89.6 all-gather.7
  215.3 28.0 all-gather.9

commit v13 on v12

--- a/solution.py
+++ b/solution.py
@@ -230,6 +230,13 @@
     block_t = jnp.concatenate(
         [attended.T, high[None], low[None], jnp.zeros((pad_rows, quarter), jnp.bfloat16)], axis=0
     )
+    cores = lax.axis_size(CORE)
+    owner_pairs = quarter // (owned * cores)
+    block_t = (
+        block_t.reshape(block_t.shape[0], owner_pairs, cores, owned)
+        .transpose(0, 2, 1, 3)
+        .reshape(block_t.shape[0], quarter)
+    )
     hidden_t = lax.all_gather(block_t[None], REQ + (HEAD,), axis=0, tiled=True).reshape(
         req_count, head_count, column_width + SQ_ROWS, quarter
     )
@@ -245,10 +252,9 @@
     weights_t = jnp.concatenate([prepared(gate_proj), prepared(up_proj)], axis=1)
     active_t = gate_up(hidden_t, weights_t, col_block)
     active_all = lax.all_gather(active_t, HEAD, axis=0, tiled=True)
-    cores = lax.axis_size(CORE)
     chips = req_count // cores
     units_all = active_all.shape[0]
-    by_core = active_all.reshape(units_all, chips, cores, owned)
+    by_core = active_all.reshape(units_all, head_count, cores, owner_pairs * owned)
     my_core = lax.axis_index(CORE)
 
     def down_for(core):

time: 310 us -> 318 us (1.026)
  local copies, waits for them, and re-layouts: 21.8 us -> 31.2 us
    dynamic_slice x1, local copies, waits for them, and re-layouts: 0.23 us -> 12 us  [down_for(): columns = lax.dynamic_index_in_dim(by_core, core, axis=2, keepdims=False)]
    all_gather x1 -> x0, local copies, waits for them, and re-layouts: 4.23 us -> none  [body(): active_all = lax.all_gather(active_t, HEAD, axis=0, tiled=True)]
where the time goes in v13:
time: 318 us; the launch traced here: 317 us
  waiting for transfers between devices  175 us (55%)
  blocking collectives  41.2 us (13%)
  local copies, waits for them, and re-layouts  31.2 us (10%)
  Pallas kernels  30.6 us (10%)
  other arithmetic  16.1 us (5%)
  between operations  14 us (4%)
  matrix products  8.82 us (3%)
    all_gather x1, waiting for transfers between devices, body(): lax.all_gather(block_t[None], REQ + (HEAD,), axis=0, tiled=True)  73.3 us
    all_gather x1, waiting for transfers between devices, body(): lax.all_gather(attention, REQ, axis=0, tiled=True)  49.9 us
    all_to_all x1, blocking collectives, body(): received = lax.all_to_all(chip_sums, CHIPS, 0, 0, tiled=True)  41.2 us
    all_gather x1, waiting for transfers between devices, body(): active_all = lax.all_gather(active_t, HEAD, axis=0, tiled=True)  28.2 us
    reduce_scatter x1, waiting for transfers between devices, body(): lax.psum_scatter(partial_sums, HEAD, scatter_dimension=0, tiled=True)  20.3 us
    pallas_call x1, Pallas kernels, gate_up(): pl.pallas_call(gate_up_kernel, grid=(chunks // R_PER_STEP,), in_specs=[pl...  17 us
    pallas_call x1, Pallas kernels, attend_local(): pl.pallas_call(attention_kernel, grid=(steps,), in_specs=[bound_spec, bou...  13.6 us
    dynamic_slice x1, local copies, waits for them, and re-layouts, down_for(): columns = lax.dynamic_index_in_dim(by_core, core, axis=2, keepdims=False)  12 us
  transfers between devices with their start and end apart: 5, of which 5 were waited for; matrix products, arithmetic and copies ran while one was open for 7% of the time, Pallas kernels for 0%

profile of v13, /device:TPU:0, one launch (start us, length us, event | category | flops | bytes accessed | tf_op | source)
XLA Modules:
  0.0 317.1 jit_solution(55418806528860096)
XLA Ops:
  7.2 0.0 copy-start
  7.2 0.0 all-gather.5.cloned.1.call-start
  7.2 0.8 compare_select_fusion.1
  8.1 1.5 gather_fusion.1
  9.6 0.8 fusion.5
  10.3 0.1 copy.59
  10.4 0.1 broadcast_in_dim.41.end_ref
  10.5 0.0 copy-start.5
  10.5 0.1 reduce.1
  10.7 0.7 copy.60.start_ref
  11.4 0.2 fusion.4
  11.6 0.7 pad_maximum_fusion
  12.3 0.0 copy-done.5
  12.3 13.6 %shard_map.140 = bf16[64,1280]{1,0:T(8,128)(2,1)} custom-call(s32[64,1]{1,0:T(8,128)} %copy.60.start_ref, s32[64,1]{1,0:T(8,128)} %copy-done.5, f32[64,128]{1,0:T(8,128)} %get-tuple-element.15.cos_ref, f32[64,128]{1,0:T(8,128)} %get-tuple-element.16.sin_ref, bf16[64,1280]{1,0:T(8,128)(2,1)} %q_ref.1, bf16[64,1280]{1,0:T(8,128)(2,1)} %k_ref.1, ...), custom_call_target="tpu_custom_call" | custom-call | flops 1158676480 | bytes 18759680 | tf_op jit(solution)/shard_map/pallas_call | solution.py:90
  25.9 0.0 all-gather.5.cloned.1.call-update
  26.0 0.0 copy-start.2
  26.0 0.0 reduce-scatter.2.cloned.1.call-start
  26.0 49.9 %all-gather.5.cloned.1.call-done = bf16[2048,1280]{1,0:T(8,128)(2,1)} async-done(((bf16[64,1280]{1,0:T(8,128)(2,1)}), bf16[2048,1280]{1,0:T(8,128)(2,1)}) %all-gather.5.cloned.1.call-update) | async-done | bytes 5242896 | tf_op jit(solution)/shard_map/all_gather | solution.py:212
  75.9 0.0 copy-done.4
  75.9 5.4 %fusion.6 = f32[2048,160]{0,1:T(8,128)} fusion(bf16[2048,1280]{1,0:T(8,128)(2,1)} %all-gather.5.cloned.1.call-done, bf16[1280,160]{0,1:T(8,128)(2,1)S(1)} %copy-done.4), kind=kOutput, calls=%fused_computation.34 | convolution fusion | flops 838860800 | bytes 6963200 | tf_op jit(solution)/shard_map/dot_general | solution.py:211
  81.4 0.0 reduce-scatter.2.cloned.1.call-update
  81.4 0.0 all-gather.7.cloned.1.call-start
  81.5 0.0 copy-done.2
  81.5 0.5 copy.57
  82.0 0.8 compare_and_fusion
  82.8 2.0 gather_fusion
  84.7 0.1 copy.58
  84.9 0.1 pad.14.clone
  84.9 20.3 %reduce-scatter.2.cloned.1.call-done = f32[512,160]{0,1:T(8,128)} async-done(((f32[2048,160]{0,1:T(8,128)}), f32[512,160]{0,1:T(8,128)}) %reduce-scatter.2.cloned.1.call-update) | async-done | bytes 327696 | tf_op jit(solution)/shard_map/reduce_scatter | solution.py:216
  105.3 1.1 multiply_reduce_fusion
  106.3 0.1 reduce_sum.24
  106.4 0.1 copy.61
  106.6 0.2 copy.64
  106.7 0.2 copy.65
  106.9 0.2 maximum_bitcast_fusion
  107.1 0.8 copy.67
  107.9 0.0 all-gather.7.cloned.1.call-update
  107.9 0.0 all-gather.9.cloned.1.call-start
  108.0 1.7 copy.68
  109.7 2.5 copy.70
  112.2 0.0 copy-done.3
  112.2 0.0 copy-done.6
  112.2 4.4 %multiply_convert_fusion.1 = (bf16[5120,108]{1,0:T(8,128)(2,1)}, bf16[5120,108]{1,0:T(8,128)(2,1)}) fusion(bf16[5120,108]{1,0:T(8,128)(2,1)S(1)} %copy.68, f32[5120]{0:T(1024)S(1)} %convert_element_type.98, bf16[5120,108]{1,0:T(8,128)(2,1)} %copy.70), kind=kLoop, calls=%fused_computation.12 | loop fusion | flops 3317760 | bytes 4444160 | tf_op jit(solution)/shard_map/convert_element_type | solution.py:248
  116.6 1.9 copy.71
  118.5 2.9 copy.69
  121.4 3.4 %fusion.3.w_ref = bf16[32,224,160]{2,1,0:T(8,128)(2,1)} fusion(bf16[32,108,160]{2,1,0:T(8,128)(2,1)S(1)} %bitcast.28, bf16[32,108,160]{2,1,0:T(8,128)(2,1)} %bitcast.29), kind=kLoop, calls=%fused_computation.10 | loop fusion | flops 9175040 | bytes 4505600 | tf_op jit(solution)/shard_map/concatenate | solution.py:252
  124.8 73.3 %all-gather.7.cloned.1.call-done = bf16[128,176,512]{2,1,0:T(8,128)(2,1)} async-done(((bf16[1,176,512]{2,1,0:T(8,128)(2,1)}), bf16[128,176,512]{2,1,0:T(8,128)(2,1)}) %all-gather.7.cloned.1.call-update) | async-done | bytes 23068688 | tf_op jit(solution)/shard_map/all_gather | solution.py:240
  198.1 17.0 %shard_map.141 = bf16[108,2048]{1,0:T(8,128)(2,1)} custom-call(bf16[32,4,176,512]{3,2,1,0:T(8,128)(2,1)} %bitcast.27, bf16[32,224,160]{2,1,0:T(8,128)(2,1)} %fusion.3.w_ref), custom_call_target="tpu_custom_call" | custom-call | flops 4697620480 | bytes 25804800 | tf_op jit(solution)/shard_map/pallas_call | solution.py:152
  215.1 0.0 all-gather.9.cloned.1.call-update
  215.1 28.2 %all-gather.9.cloned.1.call-done = bf16[4,108,2048]{2,1,0:T(8,128)(2,1)} async-done(((bf16[1,108,2048]{2,1,0:T(8,128)(2,1)}), bf16[4,108,2048]{2,1,0:T(8,128)(2,1)}) %all-gather.9.cloned.1.call-update) | async-done | bytes 1769488 | tf_op jit(solution)/shard_map/all_gather | solution.py:254
  243.4 2.3 reshape.95
  245.7 12.0 %dynamic-slice_reduce_fusion = (bf16[432,4,256]{2,1,0:T(4,128)(2,1)}, bf16[432,4,256]{2,1,0:T(4,128)(2,1)}) fusion(bf16[432,4,2,256]{3,2,1,0:T(2,128)(2,1)S(1)} %reshape.95, s32[]{:T(128)S(6)} %select_n.45, s32[]{:T(128)S(6)} %select_n.44), kind=kLoop, calls=%fused_computation.13 | loop fusion | bytes 3538952 | tf_op jit(solution)/shard_map/jit(dynamic_index_in_dim)/dynamic_slice | solution.py:261
  257.7 1.3 copy.73
  259.0 0.0 copy-done
  259.0 0.0 copy-start.1
  259.0 1.8 convolution_convert_fusion
  260.8 0.1 collective-permute-start
  260.9 0.0 copy-done.1
  260.9 0.2 copy.72
  261.1 1.6 convolution_convert_fusion.1
  262.7 3.1 collective-permute-done
  265.8 0.8 fusion.2
  266.6 41.2 %all_to_all.5 = bf16[16,64,1280]{2,1,0:T(8,128)(2,1)} all-to-all(bf16[16,64,1280]{2,1,0:T(8,128)(2,1)S(1)} %fusion.2), channel_id=1, replica_groups=mesh['chip'=16,'core'=2,'y'=4] {'chip'}, dimensions={0} | all-to-all | bytes 5242880 | tf_op jit(solution)/shard_map/all_to_all | solution.py:274
  307.8 2.8 reduce_sum.25
  (12 shorter events, 0.1 us)
Async XLA Ops:
  7.2 251.8 %copy-start = (bf16[432,1280]{1,0:T(8,128)(2,1)S(1)}, bf16[432,1280]{1,0:T(8,128)(2,1)}, u32[]{:S(2)}) copy-start(bf16[432,1280]{1,0:T(8,128)(2,1)} %param.25) | copy-start | bytes 3317764
  7.2 68.8 %all-gather.5.cloned.1.call-start = ((), (), s32[]{:S(2)}) async-start(), calls=%async_computation.2 | async-start | bytes 5406720 | tf_op jit(solution)/shard_map/all_gather | solution.py:212
  10.5 1.8 copy-start.5
  12.3 63.6 %copy-start.4 = (bf16[1280,160]{0,1:T(8,128)(2,1)S(1)}, bf16[1280,160]{0,1:T(8,128)(2,1)}, u32[]{:S(2)}) copy-start(bf16[1280,160]{0,1:T(8,128)(2,1)} %param.21) | copy-start | bytes 1228804
  26.0 55.5 %copy-start.2 = (bf16[2048,160]{0,1:T(8,128)(2,1)S(1)}, bf16[2048,160]{0,1:T(8,128)(2,1)}, u32[]{:S(2)}) copy-start(bf16[2048,160]{0,1:T(8,128)(2,1)} %param.20) | copy-start | bytes 1966084
  26.0 79.3 %reduce-scatter.2.cloned.1.call-start = ((), (), s32[]{:S(2)}) async-start(), calls=%async_computation.3 | async-start | bytes 1638400 | tf_op jit(solution)/shard_map/reduce_scatter | solution.py:216
  81.4 116.7 %all-gather.7.cloned.1.call-start = ((), (), s32[]{:S(2)}) async-start(), calls=%async_computation.4 | async-start | bytes 23248896 | tf_op jit(solution)/shard_map/all_gather | solution.py:240
  106.3 5.9 %copy-start.3 = (bf16[512,160]{0,1:T(8,128)(2,1)}, bf16[512,160]{0,1:T(8,128)(2,1)S(1)}, u32[]{:S(2)}) copy-start(bf16[512,160]{0,1:T(8,128)(2,1)S(1)} %get-tuple-element.5) | copy-start | bytes 491524
  107.9 4.4 %copy-start.6 = (bf16[5120]{0:T(1024)(128)(2,1)S(1)}, bf16[5120]{0:T(1024)(128)(2,1)}, u32[]{:S(2)}) copy-start(bf16[5120]{0:T(1024)(128)(2,1)} %param.22) | copy-start | bytes 30724
  107.9 135.5 %all-gather.9.cloned.1.call-start = ((), (), s32[]{:S(2)}) async-start(), calls=%async_computation.5 | async-start | bytes 2293760 | tf_op jit(solution)/shard_map/all_gather | solution.py:254
  259.0 1.9 copy-start.1
  260.8 5.0 %collective-permute-start = (bf16[16,64,1280]{2,1,0:T(8,128)(2,1)S(1)}, bf16[16,64,1280]{2,1,0:T(8,128)(2,1)S(1)}, u32[]{:S(2)}, u32[]{:S(2)}) collective-permute-start(bf16[16,64,1280]{2,1,0:T(8,128)(2,1)S(1)} %bitcast.42), channel_id=1, source_target_pairs={{0,4},{4,0},{1,5},{5,1},{2,6},{6,2},{3,7},{7,3},{8,12},{12,8},{9,1... | collective-permute-start | bytes 7864328 | tf_op jit(solution)/shard_map/ppermute | solution.py:271
Sparse Core Ops, SparseCore 0:
  26.1 49.8 all-gather.4
  81.5 23.7 reduce-scatter.1
  108.4 89.6 all-gather.6
  215.3 28.0 all-gather.8

commit v14 on v12

--- a/solution.py
+++ b/solution.py
@@ -252,7 +252,7 @@
     my_core = lax.axis_index(CORE)
 
     def down_for(core):
-        columns = lax.dynamic_index_in_dim(by_core, core, axis=2, keepdims=False)
+        columns = by_core[:, :, core, :]
         sums = lax.dot_general(
             columns.reshape(units_all, chips * owned),
             down_proj,
@@ -261,9 +261,11 @@
         )
         return sums.astype(jnp.bfloat16).reshape(chips, owned, sums.shape[1])
 
-    sent = down_for(cores - 1 - my_core)
+    halves = [down_for(core) for core in range(cores)]
+    first_core = my_core == 0
+    sent = jnp.where(first_core, halves[1], halves[0])
     arrived = lax.ppermute(sent, CORE, [(core, cores - 1 - core) for core in range(cores)])
-    kept = down_for(my_core)
+    kept = jnp.where(first_core, halves[0], halves[1])
     chip_sums = (kept.astype(jnp.float32) + arrived.astype(jnp.float32)).astype(jnp.bfloat16)
     received = lax.all_to_all(chip_sums, CHIPS, 0, 0, tiled=True)
     ffn_out = jnp.sum(received.astype(jnp.float32), axis=0).astype(jnp.bfloat16)

time: 310 us -> 311 us (level)
  no operation moved by 1% of the time
where the time goes in v14:
time: 311 us; the launch traced here: 310 us
  waiting for transfers between devices  177 us (57%)
  blocking collectives  41.2 us (13%)
  Pallas kernels  30.7 us (10%)
  local copies, waits for them, and re-layouts  21.8 us (7%)
  other arithmetic  16.7 us (5%)
  between operations  14 us (5%)
  matrix products  8.47 us (3%)
    all_gather x1, waiting for transfers between devices, body(): lax.all_gather(block_t[None], REQ + (HEAD,), axis=0, tiled=True)  74 us
    all_gather x1, waiting for transfers between devices, body(): lax.all_gather(attention, REQ, axis=0, tiled=True)  49.9 us
    all_to_all x1, blocking collectives, body(): received = lax.all_to_all(chip_sums, CHIPS, 0, 0, tiled=True)  41.2 us
    all_gather x1, waiting for transfers between devices, body(): active_all = lax.all_gather(active_t, HEAD, axis=0, tiled=True)  28.2 us
    reduce_scatter x1, waiting for transfers between devices, body(): lax.psum_scatter(partial_sums, HEAD, scatter_dimension=0, tiled=True)  20.4 us
    pallas_call x1, Pallas kernels, gate_up(): pl.pallas_call(gate_up_kernel, grid=(chunks // R_PER_STEP,), in_specs=[pl...  17 us
    pallas_call x1, Pallas kernels, attend_local(): pl.pallas_call(attention_kernel, grid=(steps,), in_specs=[bound_spec, bou...  13.6 us
  transfers between devices with their start and end apart: 5, of which 5 were waited for; matrix products, arithmetic and copies ran while one was open for 7% of the time, Pallas kernels for 0%

profile of v14, /device:TPU:0, one launch (start us, length us, event | category | flops | bytes accessed | tf_op | source)
XLA Modules:
  0.0 310.5 jit_solution(1863648337293272815)
XLA Ops:
  7.2 0.0 copy-start
  7.2 0.0 all-gather.6.cloned.1.call-start
  7.2 0.8 compare_select_fusion.1
  8.1 1.5 gather_fusion.1
  9.6 0.8 fusion.5
  10.3 0.1 copy.30
  10.4 0.1 broadcast_in_dim.44.end_ref
  10.5 0.0 copy-start.4
  10.5 0.1 reduce.1
  10.7 0.7 copy.31.start_ref
  11.4 0.2 fusion.4
  11.6 0.7 pad_maximum_fusion
  12.3 0.0 copy-done.4
  12.3 0.0 copy-start.3
  12.3 13.6 %shard_map.140 = bf16[64,1280]{1,0:T(8,128)(2,1)} custom-call(s32[64,1]{1,0:T(8,128)} %copy.31.start_ref, s32[64,1]{1,0:T(8,128)} %copy-done.4, f32[64,128]{1,0:T(8,128)} %get-tuple-element.17.cos_ref, f32[64,128]{1,0:T(8,128)} %get-tuple-element.18.sin_ref, bf16[64,1280]{1,0:T(8,128)(2,1)} %q_ref.1, bf16[64,1280]{1,0:T(8,128)(2,1)} %k_ref.1, ...), custom_call_target="tpu_custom_call" | custom-call | flops 1158676480 | bytes 18759680 | tf_op jit(solution)/shard_map/pallas_call | solution.py:90
  25.9 0.0 all-gather.6.cloned.1.call-update
  25.9 0.0 copy-start.1
  26.0 0.0 reduce-scatter.2.cloned.1.call-start
  26.0 49.9 %all-gather.6.cloned.1.call-done = bf16[2048,1280]{1,0:T(8,128)(2,1)} async-done(((bf16[64,1280]{1,0:T(8,128)(2,1)}), bf16[2048,1280]{1,0:T(8,128)(2,1)}) %all-gather.6.cloned.1.call-update) | async-done | bytes 5242896 | tf_op jit(solution)/shard_map/all_gather | solution.py:212
  75.9 0.0 copy-done.3
  75.9 5.4 %fusion.7 = f32[2048,160]{0,1:T(8,128)} fusion(bf16[2048,1280]{1,0:T(8,128)(2,1)} %all-gather.6.cloned.1.call-done, bf16[1280,160]{0,1:T(8,128)(2,1)S(1)} %copy-done.3), kind=kOutput, calls=%fused_computation.34 | convolution fusion | flops 838860800 | bytes 6963200 | tf_op jit(solution)/shard_map/dot_general | solution.py:211
  81.4 0.0 reduce-scatter.2.cloned.1.call-update
  81.4 0.0 all-gather.8.cloned.1.call-start
  81.4 0.0 copy-done.1
  81.4 0.0 copy-start.5
  81.5 0.5 copy.28
  82.0 0.8 compare_and_fusion
  82.7 2.0 gather_fusion
  84.7 0.1 copy.29
  84.8 0.1 pad.14.clone
  84.9 20.4 %reduce-scatter.2.cloned.1.call-done = f32[512,160]{0,1:T(8,128)} async-done(((f32[2048,160]{0,1:T(8,128)}), f32[512,160]{0,1:T(8,128)}) %reduce-scatter.2.cloned.1.call-update) | async-done | bytes 327696 | tf_op jit(solution)/shard_map/reduce_scatter | solution.py:216
  105.3 1.1 multiply_reduce_fusion
  106.3 0.0 copy-start.2
  106.4 0.8 maximum_maximum_fusion
  107.1 0.0 all-gather.8.cloned.1.call-update
  107.1 0.0 all-gather.10.cloned.1.call-start
  107.2 0.0 copy-done.5
  107.2 1.7 copy.32
  109.0 2.5 copy.34
  111.5 0.0 copy-done.2
  111.5 4.4 %multiply_convert_fusion.1 = (bf16[5120,108]{1,0:T(8,128)(2,1)}, bf16[5120,108]{1,0:T(8,128)(2,1)}) fusion(bf16[5120,108]{1,0:T(8,128)(2,1)S(1)} %copy.32, f32[5120]{0:T(1024)S(1)} %convert_element_type.94, bf16[5120,108]{1,0:T(8,128)(2,1)} %copy.34), kind=kLoop, calls=%fused_computation.12 | loop fusion | flops 3317760 | bytes 4444160 | tf_op jit(solution)/shard_map/convert_element_type | solution.py:241
  115.9 1.9 copy.35
  117.8 2.9 copy.33
  120.7 3.4 %fusion.3.w_ref = bf16[32,224,160]{2,1,0:T(8,128)(2,1)} fusion(bf16[32,108,160]{2,1,0:T(8,128)(2,1)S(1)} %bitcast.25, bf16[32,108,160]{2,1,0:T(8,128)(2,1)} %bitcast.26), kind=kLoop, calls=%fused_computation.10 | loop fusion | flops 9175040 | bytes 4505600 | tf_op jit(solution)/shard_map/concatenate | solution.py:245
  124.1 74.0 %all-gather.8.cloned.1.call-done = bf16[22528,512]{1,0:T(8,128)(2,1)} async-done(((bf16[176,512]{1,0:T(8,128)(2,1)}), bf16[22528,512]{1,0:T(8,128)(2,1)}) %all-gather.8.cloned.1.call-update) | async-done | bytes 23068688 | tf_op jit(solution)/shard_map/all_gather | solution.py:233
  198.1 17.0 %shard_map.141 = bf16[108,2048]{1,0:T(8,128)(2,1)} custom-call(bf16[32,4,176,512]{3,2,1,0:T(8,128)(2,1)} %bitcast.24, bf16[32,224,160]{2,1,0:T(8,128)(2,1)} %fusion.3.w_ref), custom_call_target="tpu_custom_call" | custom-call | flops 4697620480 | bytes 25804800 | tf_op jit(solution)/shard_map/pallas_call | solution.py:152
  215.1 0.0 all-gather.10.cloned.1.call-update
  215.1 28.2 %all-gather.10.cloned.1.call-done = bf16[4,108,2048]{2,1,0:T(8,128)(2,1)} async-done(((bf16[1,108,2048]{2,1,0:T(8,128)(2,1)}), bf16[4,108,2048]{2,1,0:T(8,128)(2,1)}) %all-gather.10.cloned.1.call-update) | async-done | bytes 1769488 | tf_op jit(solution)/shard_map/all_gather | solution.py:247
  243.4 4.3 %copy.36 = bf16[4,108,2048]{1,0,2:T(4,128)(2,1)} copy(bf16[4,108,2048]{2,1,0:T(8,128)(2,1)} %all-gather.10.cloned.1.call-done) | data formatting | bytes 3538944 | tf_op jit(solution)/shard_map/all_gather | solution.py:247
  247.6 3.3 %reshape.73 = bf16[432,16,2,64]{0,3,2,1:T(8,128)(2,1)S(1)} reshape(bf16[4,108,2048]{1,0,2:T(4,128)(2,1)} %copy.36) | data formatting | bytes 3538944 | tf_op jit(solution)/shard_map/reshape | solution.py:251
  250.9 0.2 fusion.6
  251.1 0.0 copy-done
  251.1 1.5 convolution_convert_fusion.1
  252.6 1.5 broadcast_select_fusion
  254.2 0.1 collective-permute-start
  254.3 4.9 %collective-permute-done = bf16[16,64,1280]{2,1,0:T(8,128)(2,1)S(1)} collective-permute-done((bf16[16,64,1280]{2,1,0:T(8,128)(2,1)S(1)}, bf16[16,64,1280]{2,1,0:T(8,128)(2,1)S(1)}, u32[]{:S(2)}, u32[]{:S(2)}) %collective-permute-start) | collective-permute-done | bytes 2621472 | tf_op jit(solution)/shard_map/ppermute | solution.py:267
  259.2 0.8 fusion.2
  260.0 41.2 %all_to_all.5 = bf16[16,64,1280]{2,1,0:T(8,128)(2,1)} all-to-all(bf16[16,64,1280]{2,1,0:T(8,128)(2,1)S(1)} %fusion.2), channel_id=1, replica_groups=mesh['chip'=16,'core'=2,'y'=4] {'chip'}, dimensions={0} | all-to-all | bytes 5242880 | tf_op jit(solution)/shard_map/all_to_all | solution.py:270
  301.1 2.8 reduce_sum.25
  (8 shorter events, 0.0 us)
Async XLA Ops:
  7.2 243.9 %copy-start = (bf16[432,1280]{1,0:T(8,128)(2,1)S(1)}, bf16[432,1280]{1,0:T(8,128)(2,1)}, u32[]{:S(2)}) copy-start(bf16[432,1280]{1,0:T(8,128)(2,1)} %param.25) | copy-start | bytes 3317764
  7.2 68.7 %all-gather.6.cloned.1.call-start = ((), (), s32[]{:S(2)}) async-start(), calls=%async_computation.2 | async-start | bytes 5406720 | tf_op jit(solution)/shard_map/all_gather | solution.py:212
  10.5 1.8 copy-start.4
  12.3 63.6 %copy-start.3 = (bf16[1280,160]{0,1:T(8,128)(2,1)S(1)}, bf16[1280,160]{0,1:T(8,128)(2,1)}, u32[]{:S(2)}) copy-start(bf16[1280,160]{0,1:T(8,128)(2,1)} %param.21) | copy-start | bytes 1228804
  25.9 55.5 %copy-start.1 = (bf16[2048,160]{0,1:T(8,128)(2,1)S(1)}, bf16[2048,160]{0,1:T(8,128)(2,1)}, u32[]{:S(2)}) copy-start(bf16[2048,160]{0,1:T(8,128)(2,1)} %param.20) | copy-start | bytes 1966084
  26.0 79.3 %reduce-scatter.2.cloned.1.call-start = ((), (), s32[]{:S(2)}) async-start(), calls=%async_computation.3 | async-start | bytes 1638400 | tf_op jit(solution)/shard_map/reduce_scatter | solution.py:216
  81.4 116.7 %all-gather.8.cloned.1.call-start = ((), (), s32[]{:S(2)}) async-start(), calls=%async_computation.4 | async-start | bytes 23248896 | tf_op jit(solution)/shard_map/all_gather | solution.py:233
  81.4 25.8 %copy-start.5 = (bf16[5120]{0:T(1024)(128)(2,1)S(1)}, bf16[5120]{0:T(1024)(128)(2,1)}, u32[]{:S(2)}) copy-start(bf16[5120]{0:T(1024)(128)(2,1)} %param.22) | copy-start | bytes 30724
  106.3 5.2 %copy-start.2 = (bf16[512,160]{0,1:T(8,128)(2,1)}, bf16[512,160]{0,1:T(8,128)(2,1)S(1)}, u32[]{:S(2)}) copy-start(bf16[512,160]{0,1:T(8,128)(2,1)S(1)} %get-tuple-element.3) | copy-start | bytes 491524
  107.1 136.2 %all-gather.10.cloned.1.call-start = ((), (), s32[]{:S(2)}) async-start(), calls=%async_computation.5 | async-start | bytes 2293760 | tf_op jit(solution)/shard_map/all_gather | solution.py:247
  254.2 5.0 %collective-permute-start = (bf16[16,64,1280]{2,1,0:T(8,128)(2,1)S(1)}, bf16[16,64,1280]{2,1,0:T(8,128)(2,1)S(1)}, u32[]{:S(2)}, u32[]{:S(2)}) collective-permute-start(bf16[16,64,1280]{2,1,0:T(8,128)(2,1)S(1)} %bitcast.37), channel_id=1, source_target_pairs={{0,4},{4,0},{1,5},{5,1},{2,6},{6,2},{3,7},{7,3},{8,12},{12,8},{9,1... | collective-permute-start | bytes 7864328 | tf_op jit(solution)/shard_map/ppermute | solution.py:267
Sparse Core Ops, SparseCore 0:
  26.1 49.8 all-gather.5
  81.5 23.7 reduce-scatter.1
  108.4 89.6 all-gather.7
  215.3 28.0 all-gather.9

commit v15 on v12

--- a/solution.py
+++ b/solution.py
@@ -248,16 +248,13 @@
     cores = lax.axis_size(CORE)
     chips = req_count // cores
     units_all = active_all.shape[0]
-    by_core = active_all.reshape(units_all, chips, cores, owned)
+    by_core = active_all.T.reshape(chips, cores, owned, units_all)
     my_core = lax.axis_index(CORE)
 
     def down_for(core):
-        columns = lax.dynamic_index_in_dim(by_core, core, axis=2, keepdims=False)
-        sums = lax.dot_general(
-            columns.reshape(units_all, chips * owned),
-            down_proj,
-            (((0,), (0,)), ((), ())),
-            preferred_element_type=jnp.float32,
+        rows = lax.dynamic_index_in_dim(by_core, core, axis=1, keepdims=False)
+        sums = jnp.dot(
+            rows.reshape(chips * owned, units_all), down_proj, preferred_element_type=jnp.float32
         )
         return sums.astype(jnp.bfloat16).reshape(chips, owned, sums.shape[1])
 

time: 310 us -> 308 us (level)
    all_gather x1 -> x0, local copies, waits for them, and re-layouts: 4.23 us -> none  [body(): active_all = lax.all_gather(active_t, HEAD, axis=0, tiled=True)]
    reshape x1 -> x0, local copies, waits for them, and re-layouts: 3.3 us -> none  [body(): by_core = active_all.reshape(units_all, chips, cores, owned)]
    unnamed x15 -> x16, local copies, waits for them, and re-layouts: 4.8 us -> 7.37 us
where the time goes in v15:
time: 308 us; the launch traced here: 307 us
  waiting for transfers between devices  176 us (57%)
  blocking collectives  41.2 us (13%)
  Pallas kernels  30.6 us (10%)
  local copies, waits for them, and re-layouts  19.6 us (6%)
  other arithmetic  16.6 us (5%)
  between operations  14 us (5%)
  matrix products  8.47 us (3%)
    all_gather x1, waiting for transfers between devices, body(): lax.all_gather(block_t[None], REQ + (HEAD,), axis=0, tiled=True)  74.1 us
    all_gather x1, waiting for transfers between devices, body(): lax.all_gather(attention, REQ, axis=0, tiled=True)  49.9 us
    all_to_all x1, blocking collectives, body(): received = lax.all_to_all(chip_sums, CHIPS, 0, 0, tiled=True)  41.2 us
    all_gather x1, waiting for transfers between devices, body(): active_all = lax.all_gather(active_t, HEAD, axis=0, tiled=True)  28.2 us
    reduce_scatter x1, waiting for transfers between devices, body(): lax.psum_scatter(partial_sums, HEAD, scatter_dimension=0, tiled=True)  20.4 us
    pallas_call x1, Pallas kernels, gate_up(): pl.pallas_call(gate_up_kernel, grid=(chunks // R_PER_STEP,), in_specs=[pl...  17 us
    pallas_call x1, Pallas kernels, attend_local(): pl.pallas_call(attention_kernel, grid=(steps,), in_specs=[bound_spec, bou...  13.6 us
    unnamed x16, local copies, waits for them, and re-layouts  7.37 us
  transfers between devices with their start and end apart: 5, of which 5 were waited for; matrix products, arithmetic and copies ran while one was open for 7% of the time, Pallas kernels for 0%

profile of v15, /device:TPU:0, one launch (start us, length us, event | category | flops | bytes accessed | tf_op | source)
XLA Modules:
  0.0 307.0 jit_solution(2842487862998880439)
XLA Ops:
  7.2 0.0 copy-start
  7.2 0.0 all-gather.6.cloned.1.call-start
  7.2 0.8 compare_select_fusion.1
  8.1 1.5 gather_fusion.1
  9.6 0.8 fusion.5
  10.3 0.1 copy.30
  10.4 0.1 broadcast_in_dim.44.end_ref
  10.5 0.0 copy-start.4
  10.5 0.1 reduce.1
  10.7 0.7 copy.31.start_ref
  11.4 0.2 fusion.4
  11.6 0.7 pad_maximum_fusion
  12.3 0.0 copy-done.4
  12.3 0.0 copy-start.3
  12.3 13.6 %shard_map.140 = bf16[64,1280]{1,0:T(8,128)(2,1)} custom-call(s32[64,1]{1,0:T(8,128)} %copy.31.start_ref, s32[64,1]{1,0:T(8,128)} %copy-done.4, f32[64,128]{1,0:T(8,128)} %get-tuple-element.15.cos_ref, f32[64,128]{1,0:T(8,128)} %get-tuple-element.16.sin_ref, bf16[64,1280]{1,0:T(8,128)(2,1)} %q_ref.1, bf16[64,1280]{1,0:T(8,128)(2,1)} %k_ref.1, ...), custom_call_target="tpu_custom_call" | custom-call | flops 1158676480 | bytes 18759680 | tf_op jit(solution)/shard_map/pallas_call | solution.py:90
  25.9 0.0 all-gather.6.cloned.1.call-update
  25.9 0.0 copy-start.1
  26.0 0.0 reduce-scatter.2.cloned.1.call-start
  26.0 49.9 %all-gather.6.cloned.1.call-done = bf16[2048,1280]{1,0:T(8,128)(2,1)} async-done(((bf16[64,1280]{1,0:T(8,128)(2,1)}), bf16[2048,1280]{1,0:T(8,128)(2,1)}) %all-gather.6.cloned.1.call-update) | async-done | bytes 5242896 | tf_op jit(solution)/shard_map/all_gather | solution.py:212
  75.9 0.0 copy-done.3
  75.9 5.4 %fusion.6 = f32[2048,160]{0,1:T(8,128)} fusion(bf16[2048,1280]{1,0:T(8,128)(2,1)} %all-gather.6.cloned.1.call-done, bf16[1280,160]{0,1:T(8,128)(2,1)S(1)} %copy-done.3), kind=kOutput, calls=%fused_computation.33 | convolution fusion | flops 838860800 | bytes 6963200 | tf_op jit(solution)/shard_map/dot_general | solution.py:211
  81.4 0.0 reduce-scatter.2.cloned.1.call-update
  81.4 0.0 all-gather.8.cloned.1.call-start
  81.4 0.0 copy-done.1
  81.5 0.5 copy.28
  82.0 0.8 compare_and_fusion
  82.7 2.0 gather_fusion
  84.7 0.1 copy.29
  84.8 0.1 pad.14.clone
  84.9 20.4 %reduce-scatter.2.cloned.1.call-done = f32[512,160]{0,1:T(8,128)} async-done(((f32[2048,160]{0,1:T(8,128)}), f32[512,160]{0,1:T(8,128)}) %reduce-scatter.2.cloned.1.call-update) | async-done | bytes 327696 | tf_op jit(solution)/shard_map/reduce_scatter | solution.py:216
  105.3 1.1 multiply_reduce_fusion
  106.3 0.0 copy-start.2
  106.4 0.8 maximum_maximum_fusion
  107.1 0.0 copy-start.5
  107.1 0.0 all-gather.8.cloned.1.call-update
  107.2 0.0 all-gather.10.cloned.1.call-start
  107.2 1.7 copy.32
  109.0 2.5 copy.34
  111.5 0.0 copy-done.2
  111.5 0.0 copy-done.5
  111.5 4.3 %multiply_convert_fusion.1 = (bf16[5120,108]{1,0:T(8,128)(2,1)}, bf16[5120,108]{1,0:T(8,128)(2,1)}) fusion(bf16[5120,108]{1,0:T(8,128)(2,1)S(1)} %copy.32, f32[5120]{0:T(1024)S(1)} %convert_element_type.94, bf16[5120,108]{1,0:T(8,128)(2,1)} %copy.34), kind=kLoop, calls=%fused_computation.12 | loop fusion | flops 3317760 | bytes 4444160 | tf_op jit(solution)/shard_map/convert_element_type | solution.py:241
  115.8 1.9 copy.33
  117.8 2.9 copy.35
  120.6 3.4 %fusion.3.w_ref = bf16[32,224,160]{2,1,0:T(8,128)(2,1)} fusion(bf16[32,108,160]{2,1,0:T(8,128)(2,1)} %bitcast.27, bf16[32,108,160]{2,1,0:T(8,128)(2,1)S(1)} %bitcast.26), kind=kLoop, calls=%fused_computation.10 | loop fusion | flops 9175040 | bytes 4505600 | tf_op jit(solution)/shard_map/concatenate | solution.py:245
  124.0 74.1 %all-gather.8.cloned.1.call-done = bf16[22528,512]{1,0:T(8,128)(2,1)} async-done(((bf16[176,512]{1,0:T(8,128)(2,1)}), bf16[22528,512]{1,0:T(8,128)(2,1)}) %all-gather.8.cloned.1.call-update) | async-done | bytes 23068688 | tf_op jit(solution)/shard_map/all_gather | solution.py:233
  198.1 17.0 %shard_map.141 = bf16[108,2048]{1,0:T(8,128)(2,1)} custom-call(bf16[32,4,176,512]{3,2,1,0:T(8,128)(2,1)} %bitcast.24, bf16[32,224,160]{2,1,0:T(8,128)(2,1)} %fusion.3.w_ref), custom_call_target="tpu_custom_call" | custom-call | flops 4697620480 | bytes 25804800 | tf_op jit(solution)/shard_map/pallas_call | solution.py:152
  215.1 0.0 all-gather.10.cloned.1.call-update
  215.1 28.2 %all-gather.10.cloned.1.call-done = bf16[4,108,2048]{2,1,0:T(8,128)(2,1)} async-done(((bf16[1,108,2048]{2,1,0:T(8,128)(2,1)}), bf16[4,108,2048]{2,1,0:T(8,128)(2,1)}) %all-gather.10.cloned.1.call-update) | async-done | bytes 1769488 | tf_op jit(solution)/shard_map/all_gather | solution.py:247
  243.4 2.6 reshape.105
  245.9 2.8 copy.36
  248.7 0.2 constant_dynamic-slice_fusion
  248.9 0.0 copy-done
  249.0 1.5 convolution_convert_fusion
  250.5 0.3 collective-permute-start
  250.8 1.5 convolution_convert_fusion.1
  252.3 3.4 %collective-permute-done = bf16[16,64,1280]{2,1,0:T(8,128)(2,1)S(1)} collective-permute-done((bf16[16,64,1280]{2,1,0:T(8,128)(2,1)S(1)}, bf16[16,64,1280]{2,1,0:T(8,128)(2,1)S(1)}, u32[]{:S(2)}, u32[]{:S(2)}) %collective-permute-start) | collective-permute-done | bytes 2621472 | tf_op jit(solution)/shard_map/ppermute | solution.py:262
  255.6 0.8 fusion.2
  256.5 41.2 %all_to_all.5 = bf16[16,64,1280]{2,1,0:T(8,128)(2,1)} all-to-all(bf16[16,64,1280]{2,1,0:T(8,128)(2,1)S(1)} %fusion.2), channel_id=1, replica_groups=mesh['chip'=16,'core'=2,'y'=4] {'chip'}, dimensions={0} | all-to-all | bytes 5242880 | tf_op jit(solution)/shard_map/all_to_all | solution.py:265
  297.6 2.8 reduce_sum.25
  (8 shorter events, 0.0 us)
Async XLA Ops:
  7.2 241.8 %copy-start = (bf16[432,1280]{1,0:T(8,128)(2,1)S(1)}, bf16[432,1280]{1,0:T(8,128)(2,1)}, u32[]{:S(2)}) copy-start(bf16[432,1280]{1,0:T(8,128)(2,1)} %param.25) | copy-start | bytes 3317764
  7.2 68.8 %all-gather.6.cloned.1.call-start = ((), (), s32[]{:S(2)}) async-start(), calls=%async_computation.2 | async-start | bytes 5406720 | tf_op jit(solution)/shard_map/all_gather | solution.py:212
  10.5 1.8 copy-start.4
  12.3 63.6 %copy-start.3 = (bf16[1280,160]{0,1:T(8,128)(2,1)S(1)}, bf16[1280,160]{0,1:T(8,128)(2,1)}, u32[]{:S(2)}) copy-start(bf16[1280,160]{0,1:T(8,128)(2,1)} %param.21) | copy-start | bytes 1228804
  25.9 55.5 %copy-start.1 = (bf16[2048,160]{0,1:T(8,128)(2,1)S(1)}, bf16[2048,160]{0,1:T(8,128)(2,1)}, u32[]{:S(2)}) copy-start(bf16[2048,160]{0,1:T(8,128)(2,1)} %param.20) | copy-start | bytes 1966084
  26.0 79.3 %reduce-scatter.2.cloned.1.call-start = ((), (), s32[]{:S(2)}) async-start(), calls=%async_computation.3 | async-start | bytes 1638400 | tf_op jit(solution)/shard_map/reduce_scatter | solution.py:216
  81.4 116.7 %all-gather.8.cloned.1.call-start = ((), (), s32[]{:S(2)}) async-start(), calls=%async_computation.4 | async-start | bytes 23248896 | tf_op jit(solution)/shard_map/all_gather | solution.py:233
  106.3 5.2 %copy-start.2 = (bf16[512,160]{0,1:T(8,128)(2,1)}, bf16[512,160]{0,1:T(8,128)(2,1)S(1)}, u32[]{:S(2)}) copy-start(bf16[512,160]{0,1:T(8,128)(2,1)S(1)} %get-tuple-element.3) | copy-start | bytes 491524
  107.1 4.4 %copy-start.5 = (bf16[5120]{0:T(1024)(128)(2,1)S(1)}, bf16[5120]{0:T(1024)(128)(2,1)}, u32[]{:S(2)}) copy-start(bf16[5120]{0:T(1024)(128)(2,1)} %param.22) | copy-start | bytes 30724
  107.2 136.2 %all-gather.10.cloned.1.call-start = ((), (), s32[]{:S(2)}) async-start(), calls=%async_computation.5 | async-start | bytes 2293760 | tf_op jit(solution)/shard_map/all_gather | solution.py:247
  250.5 5.2 %collective-permute-start = (bf16[16,64,1280]{2,1,0:T(8,128)(2,1)S(1)}, bf16[16,64,1280]{2,1,0:T(8,128)(2,1)S(1)}, u32[]{:S(2)}, u32[]{:S(2)}) collective-permute-start(bf16[16,64,1280]{2,1,0:T(8,128)(2,1)S(1)} %bitcast.39), channel_id=1, source_target_pairs={{0,4},{4,0},{1,5},{5,1},{2,6},{6,2},{3,7},{7,3},{8,12},{12,8},{9,1... | collective-permute-start | bytes 7864328 | tf_op jit(solution)/shard_map/ppermute | solution.py:262
Sparse Core Ops, SparseCore 0:
  26.1 49.8 all-gather.5
  81.5 23.7 reduce-scatter.1
  108.4 89.6 all-gather.7
  215.3 28.0 all-gather.9
